TPU v7x, 512 devices: a whole 4x8x8 slice. The times are simulated.
512 devices in a mesh: gx: 16 (over y, core), gy: 32 (over x, z).
Axes of the slice: x: 4, y: 8, z: 8, core: 2. Of those that a mesh axis runs over, the one named last changes fastest.
Arguments:
- right_side: float32 [128, 262144], P('gx', 'gy'), may hold values from -6 to 6
- initial_guess: float32 [128, 262144], P('gx', 'gy'), may hold values from -1.2 to 1.2
- coefficients: float32 [5, 128, 16384], P(None, 'gx', 'gy'), may hold values from -1 to 2, as said below
Outputs:
- solution: float32 [128, 262144], P('gx', 'gy')
- residual: float32 [128, 262144], P('gx', 'gy')
Inputs may be any that keep to these rules, and one draw needn't show every extreme that they name: `coefficients`: component 0 is the diffusivity, within 0.5 to 2; components 1 to 3 the drift velocities along the three dimensions, within -1 to 1; component 4 the reaction rate, within 0.5 to 2.
All inputs are finite; a program needn't handle non-finite values.
Results may differ from a plain program's by a relative error of at most 0.0003.
Values sent between devices are 32-bit elements; how exact they have to be, the bound alone decides.
No kernel may reach another device: no remote copies, remote signals or barrier semaphores. Data moves between devices by JAX's collectives and lax.ppermute only.
A program may use at most 64 MiB of HBM per device.

v0:
```python
import jax
import jax.numpy as jnp
from jax import lax
from jax.sharding import PartitionSpec as P

NZ = 32
RHS = 16
STEPS = 3


SHIFT = 7.5
SCALE = 4.0


def extended(block, sides, width):
    for axis, dim in sides:
        count = lax.axis_size(axis)
        forward = [(i, i + 1) for i in range(count - 1)]
        backward = [(target, source) for source, target in forward]
        low = lax.ppermute(
            lax.slice_in_dim(block, block.shape[dim] - width, None, axis=dim), axis, forward
        )
        high = lax.ppermute(lax.slice_in_dim(block, 0, width, axis=dim), axis, backward)
        block = jnp.concatenate([low, block, high], axis=dim)
    return block


def operate(padded, coefs):
    diffusivity, drift_x, drift_y, drift_z, reaction = coefs
    center = padded[1:-1, 1:-1]
    x_plus = padded[2:, 1:-1]
    x_minus = padded[:-2, 1:-1]
    y_plus = padded[1:-1, 2:]
    y_minus = padded[1:-1, :-2]
    zero_rim = jnp.zeros(center.shape[:2] + (RHS,), center.dtype)
    z_plus = jnp.concatenate([center[:, :, RHS:], zero_rim], axis=2)
    z_minus = jnp.concatenate([zero_rim, center[:, :, :-RHS]], axis=2)
    beside = x_plus + x_minus + y_plus + y_minus + z_plus + z_minus
    drift = (
        drift_x * (x_plus - x_minus) + drift_y * (y_plus - y_minus) + drift_z * (z_plus - z_minus)
    )
    return (reaction + 6.0 * diffusivity) * center - diffusivity * beside + 0.5 * drift


def widen(table):
    return [jnp.repeat(table[:, :, i * NZ : (i + 1) * NZ], RHS, axis=2) for i in range(5)]


def combine_rhs(field, weights):
    lanes = jnp.kron(jnp.eye(128 // RHS, dtype=jnp.float32), weights)
    flat = field.reshape(-1, 128)
    return jnp.dot(flat, lanes, precision=lax.Precision.HIGHEST).reshape(field.shape)


def per_device(right_side, initial_guess, coefficients):
    rows_x = right_side.shape[0]
    rows_y = right_side.shape[1] // (NZ * RHS)
    width = NZ * RHS
    rhs_field = right_side.reshape(rows_x, rows_y, width)
    guess = initial_guess.reshape(rows_x, rows_y, width)
    coef_local = jnp.transpose(coefficients.reshape(5, rows_x, rows_y, NZ), (1, 2, 0, 3)).reshape(
        rows_x, rows_y, 5 * NZ
    )
    inner_coefs = widen(coef_local)
    guess_pad = extended(guess, (("gx", 0), ("gy", 1)), 1)
    initial_res = rhs_field - operate(guess_pad, inner_coefs)
    krylov = [initial_res]
    current = initial_res
    for step in range(STEPS):
        padded = extended(current, (("gx", 0), ("gy", 1)), 1)
        current = (operate(padded, inner_coefs) - SHIFT * current) / SCALE
        krylov.append(current)
    blocks = len(krylov)
    groups = 128 // RHS
    stacked = jnp.concatenate([v.reshape(-1, 128) for v in krylov], axis=1)
    products = jnp.dot(stacked.T, stacked, precision=lax.Precision.HIGHEST)
    products = products.reshape(blocks, groups, RHS, blocks, groups, RHS)
    diagonal = jnp.eye(groups, dtype=jnp.float32)[None, :, None, None, :, None]
    local_gram = jnp.sum(products * diagonal, axis=(1, 4)).reshape(blocks * RHS, blocks * RHS)
    gram = lax.psum(local_gram, ("gx", "gy"))
    shift_map = SHIFT * jnp.eye(blocks * RHS, STEPS * RHS, dtype=jnp.float32) + SCALE * jnp.eye(
        blocks * RHS, STEPS * RHS, k=-RHS, dtype=jnp.float32
    )
    normal = jnp.dot(
        shift_map.T,
        jnp.dot(gram, shift_map, precision=lax.Precision.HIGHEST),
        precision=lax.Precision.HIGHEST,
    )
    target = jnp.dot(shift_map.T, gram[:, :RHS], precision=lax.Precision.HIGHEST)
    factor = jnp.linalg.cholesky(normal)
    weights = jax.scipy.linalg.cho_solve((factor, True), target)
    solution = guess
    for step in range(STEPS):
        solution = solution + combine_rhs(krylov[step], weights[step * RHS : (step + 1) * RHS])
    update_pad = extended(solution, (("gx", 0), ("gy", 1)), 1)
    residual = rhs_field - operate(update_pad, inner_coefs)
    return (
        solution.reshape(rows_x, rows_y * NZ * RHS),
        residual.reshape(rows_x, rows_y * NZ * RHS),
    )


def solution(mesh):
    placed = (P("gx", "gy"), P("gx", "gy"), P(None, "gx", "gy"))
    return jax.shard_map(
        per_device,
        mesh=mesh,
        in_specs=placed,
        out_specs=(P("gx", "gy"), P("gx", "gy")),
        check_vma=False,
    )
```

profile of v0, /device:TPU:6, one launch (start us, length us, event | category | flops | bytes accessed | tf_op | source)
XLA Modules:
  0.0 237.0 jit_solution(5623281883208357478)
XLA Ops:
  0.6 1.3 slice_reduce_fusion.1
  1.9 1.7 collective-permute-start.1
  3.7 1.3 collective-permute-start
  5.0 1.1 copy.35
  6.1 0.9 fusion.51
  7.0 1.0 reshape.149
  8.6 11.2 %collective-permute-start.2 = (f32[10,1,512]{2,1,0:T(1,128)S(1)}, f32[10,1,512]{2,1,0:T(1,128)S(1)}, u32[]{:S(2)}, u32[]{:S(2)}) collective-permute-start(f32[10,1,512]{2,1,0:T(1,128)S(1)} %get-tuple-element.16), channel_id=1, source_target_pairs={{1,0},{2,1},{3,2},{4,3},{5,4},{6,5},{7,6},{8,7},{9,8},{10,9},{11,1... | collective-permute-start | bytes 61448 | tf_op jit(solution)/shard_map/ppermute | solution.py:23
  19.8 1.9 collective-permute-start.3
  22.5 1.6 reshape.151
  24.6 1.6 reshape.152
  26.8 1.6 reshape.154
  29.0 1.6 reshape.155
  31.1 1.6 reshape.156
  32.7 2.1 bitcast_subtract_fusion.1
  34.8 1.3 collective-permute-start.4
  36.1 4.7 %collective-permute-start.5 = (f32[1,16,512]{2,1,0:T(8,128)S(1)}, f32[1,16,512]{2,1,0:T(8,128)S(1)}, u32[]{:S(2)}, u32[]{:S(2)}) collective-permute-start(f32[1,16,512]{2,1,0:T(8,128)S(1)} %get-tuple-element.30), channel_id=1, source_target_pairs={{0,32},{32,64},{64,96},{96,128},{128,160},{160,192},{192,224},{224... | collective-permute-start | bytes 98312 | tf_op jit(solution)/shard_map/ppermute | solution.py:20
  40.8 0.8 collective-permute-done.5
  41.7 5.8 %collective-permute-start.6 = (f32[10,1,512]{2,1,0:T(1,128)S(1)}, f32[10,1,512]{2,1,0:T(1,128)S(1)}, u32[]{:S(2)}, u32[]{:S(2)}) collective-permute-start(f32[10,1,512]{2,1,0:T(1,128)S(1)} %get-tuple-element.14), channel_id=1, source_target_pairs={{1,0},{2,1},{3,2},{4,3},{5,4},{6,5},{7,6},{8,7},{9,8},{10,9},{11,1... | collective-permute-start | bytes 61448 | tf_op jit(solution)/shard_map/ppermute | solution.py:23
  47.5 2.1 collective-permute-start.7
  49.7 5.5 %collective-permute-done.7 = f32[10,1,512]{2,1,0:T(1,128)S(1)} collective-permute-done((f32[10,1,512]{2,1,0:T(1,128)S(1)}, f32[10,1,512]{2,1,0:T(1,128)S(1)}, u32[]{:S(2)}, u32[]{:S(2)}) %collective-permute-start.7) | collective-permute-done | bytes 20512 | tf_op jit(solution)/shard_map/ppermute | solution.py:20
  55.6 1.3 collective-permute-start.8
  56.9 3.6 %collective-permute-start.9 = (f32[1,16,512]{2,1,0:T(8,128)S(1)}, f32[1,16,512]{2,1,0:T(8,128)S(1)}, u32[]{:S(2)}, u32[]{:S(2)}) collective-permute-start(f32[1,16,512]{2,1,0:T(8,128)S(1)} %get-tuple-element.26), channel_id=1, source_target_pairs={{0,32},{32,64},{64,96},{96,128},{128,160},{160,192},{192,224},{224... | collective-permute-start | bytes 98312 | tf_op jit(solution)/shard_map/ppermute | solution.py:20
  60.5 0.8 collective-permute-done.9
  61.3 1.9 collective-permute-start.10
  63.3 3.9 %collective-permute-start.11 = (f32[10,1,512]{2,1,0:T(1,128)S(1)}, f32[10,1,512]{2,1,0:T(1,128)S(1)}, u32[]{:S(2)}, u32[]{:S(2)}) collective-permute-start(f32[10,1,512]{2,1,0:T(1,128)S(1)} %get-tuple-element.13), channel_id=1, source_target_pairs={{0,1},{1,2},{2,3},{3,4},{4,5},{5,6},{6,7},{7,8},{8,9},{9,10},{10,1... | collective-permute-start | bytes 61448 | tf_op jit(solution)/shard_map/ppermute | solution.py:20
  67.3 3.7 %collective-permute-done.11 = f32[10,1,512]{2,1,0:T(1,128)S(1)} collective-permute-done((f32[10,1,512]{2,1,0:T(1,128)S(1)}, f32[10,1,512]{2,1,0:T(1,128)S(1)}, u32[]{:S(2)}, u32[]{:S(2)}) %collective-permute-start.11) | collective-permute-done | bytes 20512 | tf_op jit(solution)/shard_map/ppermute | solution.py:20
  71.4 1.3 collective-permute-start.12
  72.7 5.3 %collective-permute-start.13 = (f32[1,16,512]{2,1,0:T(8,128)S(1)}, f32[1,16,512]{2,1,0:T(8,128)S(1)}, u32[]{:S(2)}, u32[]{:S(2)}) collective-permute-start(f32[1,16,512]{2,1,0:T(8,128)S(1)} %get-tuple-element.22), channel_id=1, source_target_pairs={{0,32},{32,64},{64,96},{96,128},{128,160},{160,192},{192,224},{224... | collective-permute-start | bytes 98312 | tf_op jit(solution)/shard_map/ppermute | solution.py:20
  78.1 0.8 collective-permute-done.13
  78.9 1.9 collective-permute-start.14
  80.8 3.9 %collective-permute-start.15 = (f32[10,1,512]{2,1,0:T(1,128)S(1)}, f32[10,1,512]{2,1,0:T(1,128)S(1)}, u32[]{:S(2)}, u32[]{:S(2)}) collective-permute-start(f32[10,1,512]{2,1,0:T(1,128)S(1)} %get-tuple-element.11), channel_id=1, source_target_pairs={{0,1},{1,2},{2,3},{3,4},{4,5},{5,6},{6,7},{7,8},{8,9},{9,10},{10,1... | collective-permute-start | bytes 61448 | tf_op jit(solution)/shard_map/ppermute | solution.py:20
  84.9 3.7 %collective-permute-done.15 = f32[10,1,512]{2,1,0:T(1,128)S(1)} collective-permute-done((f32[10,1,512]{2,1,0:T(1,128)S(1)}, f32[10,1,512]{2,1,0:T(1,128)S(1)}, u32[]{:S(2)}, u32[]{:S(2)}) %collective-permute-start.15) | collective-permute-done | bytes 20512 | tf_op jit(solution)/shard_map/ppermute | solution.py:20
  89.0 1.9 fusion
  90.8 4.9 %reshape.161 = f32[4,8,16,4,8,16]{5,4,3,2,1,0:T(8,128)} reshape(f32[512,512]{1,0:T(8,128)S(1)} %fusion) | data formatting | bytes 2097152 | tf_op jit(solution)/shard_map/reshape | solution.py:77
  95.8 4.8 %multiply_reduce_fusion = f32[4,16,4,16]{3,2,1,0:T(4,128)S(1)} fusion(f32[4,8,16,4,8,16]{5,4,3,2,1,0:T(8,128)} %reshape.161, f32[8,8]{1,0:T(8,128)S(1)} %fusion.31), kind=kLoop, calls=%fused_computation | loop fusion | flops 520192 | bytes 1065216 | tf_op jit(solution)/shard_map/reduce_sum | solution.py:79
  100.7 102.2 %psum.7 = f32[64,64]{1,0:T(8,128)S(1)} all-reduce(f32[64,64]{1,0:T(8,128)S(1)} %reshape.162), channel_id=1, replica_groups=mesh['gx'=16,'gy'=32] {'gx','gy'}, use_global_device_ids=true, to_apply=%region_1.0 | all-reduce | flops 4096 | bytes 32768 | tf_op jit(solution)/shard_map/psum | solution.py:80
  203.8 4.4 %cholesky.16 = f32[48,48]{1,0:T(8,128)S(1)} custom-call(f32[48,48]{1,0:T(8,128)S(1)} %fusion.18), custom_call_target="Cholesky" | custom-call | tf_op jit(solution)/shard_map/jit(cholesky)/cholesky | solution.py:90
  208.3 0.6 compare_reduce_fusion
  208.9 0.7 fusion.13
  209.6 3.7 %custom-call.10 = f32[1,48,48]{1,2,0:T(8,128)S(1)} custom-call(f32[1,48,48]{2,1,0:T(8,128)S(1)} %fusion.13), custom_call_target="InvertDiagBlocksLowerTriangular" | custom-call | tf_op jit(solution)/shard_map/jit(_cho_solve)/triangular_solve | solution.py:91
  215.8 1.3 fusion.56
  217.5 1.3 collective-permute-start.16
  218.8 3.0 %collective-permute-start.17 = (f32[1,16,512]{2,1,0:T(8,128)S(1)}, f32[1,16,512]{2,1,0:T(8,128)S(1)}, u32[]{:S(2)}, u32[]{:S(2)}) collective-permute-start(f32[1,16,512]{2,1,0:T(8,128)S(1)} %get-tuple-element.18), channel_id=1, source_target_pairs={{0,32},{32,64},{64,96},{96,128},{128,160},{160,192},{192,224},{224... | collective-permute-start | bytes 98312 | tf_op jit(solution)/shard_map/ppermute | solution.py:20
  221.8 0.8 add_add_fusion.1
  222.7 5.0 %collective-permute-start.18 = (f32[10,1,512]{2,1,0:T(1,128)S(1)}, f32[10,1,512]{2,1,0:T(1,128)S(1)}, u32[]{:S(2)}, u32[]{:S(2)}) collective-permute-start(f32[10,1,512]{2,1,0:T(1,128)S(1)} %get-tuple-element.8), channel_id=1, source_target_pairs={{1,0},{2,1},{3,2},{4,3},{5,4},{6,5},{7,6},{8,7},{9,8},{10,9},{11,1... | collective-permute-start | bytes 61448 | tf_op jit(solution)/shard_map/ppermute | solution.py:23
  227.7 1.9 collective-permute-start.19
  229.8 5.9 %collective-permute-done.19 = f32[10,1,512]{2,1,0:T(1,128)S(1)} collective-permute-done((f32[10,1,512]{2,1,0:T(1,128)S(1)}, f32[10,1,512]{2,1,0:T(1,128)S(1)}, u32[]{:S(2)}, u32[]{:S(2)}) %collective-permute-start.19) | collective-permute-done | bytes 20512 | tf_op jit(solution)/shard_map/ppermute | solution.py:20
  236.1 0.9 copy.25
  (87 shorter events, 9.8 us)
Async XLA Ops:
  0.6 7.7 %copy-start = (f32[8,8192]{1,0:T(8,128)S(1)}, f32[8,8192]{1,0:T(8,128)}, u32[]{:S(2)}) copy-start(f32[8,8192]{1,0:T(8,128)} %param.4) | copy-start | bytes 786436
  1.9 6.4 %collective-permute-start.1 = (f32[1,16,512]{2,1,0:T(8,128)S(1)}, f32[1,16,512]{2,1,0:T(8,128)S(1)}, u32[]{:S(2)}, u32[]{:S(2)}) collective-permute-start(f32[1,16,512]{2,1,0:T(8,128)S(1)} %slice.227), channel_id=1, source_target_pairs={{0,32},{32,64},{64,96},{96,128},{128,160},{160,192},{192,224},{224... | collective-permute-start | bytes 98312 | tf_op jit(solution)/shard_map/ppermute | solution.py:20
  3.7 4.8 %collective-permute-start = (f32[1,16,512]{2,1,0:T(8,128)S(1)}, f32[1,16,512]{2,1,0:T(8,128)S(1)}, u32[]{:S(2)}, u32[]{:S(2)}) collective-permute-start(f32[1,16,512]{2,1,0:T(8,128)S(1)} %slice.224), channel_id=1, source_target_pairs={{32,0},{64,32},{96,64},{128,96},{160,128},{192,160},{224,192},{256... | collective-permute-start | bytes 98312 | tf_op jit(solution)/shard_map/ppermute | solution.py:23
  6.1 15.8 %copy-start.2 = (f32[1,8,16,512]{3,2,1,0:T(8,128)}, f32[1,8,16,512]{3,2,1,0:T(8,128)S(1)}, u32[]{:S(2)}) copy-start(f32[1,8,16,512]{3,2,1,0:T(8,128)S(1)} %copy.35) | copy-start | bytes 786436
  8.5 15.5 %copy-start.5 = (f32[10,16,512]{2,1,0:T(8,128)}, f32[10,16,512]{2,1,0:T(8,128)S(1)}, u32[]{:S(2)}) copy-start(f32[10,16,512]{2,1,0:T(8,128)S(1)} %constant_dynamic-update-slice_fusion) | copy-start | bytes 983044
  8.6 24.1 %collective-permute-start.2 = (f32[10,1,512]{2,1,0:T(1,128)S(1)}, f32[10,1,512]{2,1,0:T(1,128)S(1)}, u32[]{:S(2)}, u32[]{:S(2)}) collective-permute-start(f32[10,1,512]{2,1,0:T(1,128)S(1)} %get-tuple-element.16), channel_id=1, source_target_pairs={{1,0},{2,1},{3,2},{4,3},{5,4},{6,5},{7,6},{8,7},{9,8},{10,9},{11,1... | collective-permute-start | bytes 61448 | tf_op jit(solution)/shard_map/ppermute | solution.py:23
  19.8 12.9 %collective-permute-start.3 = (f32[10,1,512]{2,1,0:T(1,128)S(1)}, f32[10,1,512]{2,1,0:T(1,128)S(1)}, u32[]{:S(2)}, u32[]{:S(2)}) collective-permute-start(f32[10,1,512]{2,1,0:T(1,128)S(1)} %get-tuple-element.17), channel_id=1, source_target_pairs={{0,1},{1,2},{2,3},{3,4},{4,5},{5,6},{6,7},{7,8},{8,9},{9,10},{10,1... | collective-permute-start | bytes 61448 | tf_op jit(solution)/shard_map/ppermute | solution.py:20
  34.8 6.1 %collective-permute-start.4 = (f32[1,16,512]{2,1,0:T(8,128)S(1)}, f32[1,16,512]{2,1,0:T(8,128)S(1)}, u32[]{:S(2)}, u32[]{:S(2)}) collective-permute-start(f32[1,16,512]{2,1,0:T(8,128)S(1)} %get-tuple-element.31), channel_id=1, source_target_pairs={{32,0},{64,32},{96,64},{128,96},{160,128},{192,160},{224,192},{256... | collective-permute-start | bytes 98312 | tf_op jit(solution)/shard_map/ppermute | solution.py:23
  36.1 5.6 %collective-permute-start.5 = (f32[1,16,512]{2,1,0:T(8,128)S(1)}, f32[1,16,512]{2,1,0:T(8,128)S(1)}, u32[]{:S(2)}, u32[]{:S(2)}) collective-permute-start(f32[1,16,512]{2,1,0:T(8,128)S(1)} %get-tuple-element.30), channel_id=1, source_target_pairs={{0,32},{32,64},{64,96},{96,128},{128,160},{160,192},{192,224},{224... | collective-permute-start | bytes 98312 | tf_op jit(solution)/shard_map/ppermute | solution.py:20
  41.7 8.0 %collective-permute-start.6 = (f32[10,1,512]{2,1,0:T(1,128)S(1)}, f32[10,1,512]{2,1,0:T(1,128)S(1)}, u32[]{:S(2)}, u32[]{:S(2)}) collective-permute-start(f32[10,1,512]{2,1,0:T(1,128)S(1)} %get-tuple-element.14), channel_id=1, source_target_pairs={{1,0},{2,1},{3,2},{4,3},{5,4},{6,5},{7,6},{8,7},{9,8},{10,9},{11,1... | collective-permute-start | bytes 61448 | tf_op jit(solution)/shard_map/ppermute | solution.py:23
  47.5 7.8 %collective-permute-start.7 = (f32[10,1,512]{2,1,0:T(1,128)S(1)}, f32[10,1,512]{2,1,0:T(1,128)S(1)}, u32[]{:S(2)}, u32[]{:S(2)}) collective-permute-start(f32[10,1,512]{2,1,0:T(1,128)S(1)} %get-tuple-element.15), channel_id=1, source_target_pairs={{0,1},{1,2},{2,3},{3,4},{4,5},{5,6},{6,7},{7,8},{8,9},{9,10},{10,1... | collective-permute-start | bytes 61448 | tf_op jit(solution)/shard_map/ppermute | solution.py:20
  55.6 4.9 %collective-permute-start.8 = (f32[1,16,512]{2,1,0:T(8,128)S(1)}, f32[1,16,512]{2,1,0:T(8,128)S(1)}, u32[]{:S(2)}, u32[]{:S(2)}) collective-permute-start(f32[1,16,512]{2,1,0:T(8,128)S(1)} %get-tuple-element.27), channel_id=1, source_target_pairs={{32,0},{64,32},{96,64},{128,96},{160,128},{192,160},{224,192},{256... | collective-permute-start | bytes 98312 | tf_op jit(solution)/shard_map/ppermute | solution.py:23
  56.9 4.4 %collective-permute-start.9 = (f32[1,16,512]{2,1,0:T(8,128)S(1)}, f32[1,16,512]{2,1,0:T(8,128)S(1)}, u32[]{:S(2)}, u32[]{:S(2)}) collective-permute-start(f32[1,16,512]{2,1,0:T(8,128)S(1)} %get-tuple-element.26), channel_id=1, source_target_pairs={{0,32},{32,64},{64,96},{96,128},{128,160},{160,192},{192,224},{224... | collective-permute-start | bytes 98312 | tf_op jit(solution)/shard_map/ppermute | solution.py:20
  61.3 6.0 %collective-permute-start.10 = (f32[10,1,512]{2,1,0:T(1,128)S(1)}, f32[10,1,512]{2,1,0:T(1,128)S(1)}, u32[]{:S(2)}, u32[]{:S(2)}) collective-permute-start(f32[10,1,512]{2,1,0:T(1,128)S(1)} %get-tuple-element.12), channel_id=1, source_target_pairs={{1,0},{2,1},{3,2},{4,3},{5,4},{6,5},{7,6},{8,7},{9,8},{10,9},{11,1... | collective-permute-start | bytes 61448 | tf_op jit(solution)/shard_map/ppermute | solution.py:23
  63.3 7.8 %collective-permute-start.11 = (f32[10,1,512]{2,1,0:T(1,128)S(1)}, f32[10,1,512]{2,1,0:T(1,128)S(1)}, u32[]{:S(2)}, u32[]{:S(2)}) collective-permute-start(f32[10,1,512]{2,1,0:T(1,128)S(1)} %get-tuple-element.13), channel_id=1, source_target_pairs={{0,1},{1,2},{2,3},{3,4},{4,5},{5,6},{6,7},{7,8},{8,9},{9,10},{10,1... | collective-permute-start | bytes 61448 | tf_op jit(solution)/shard_map/ppermute | solution.py:20
  71.4 6.7 %collective-permute-start.12 = (f32[1,16,512]{2,1,0:T(8,128)S(1)}, f32[1,16,512]{2,1,0:T(8,128)S(1)}, u32[]{:S(2)}, u32[]{:S(2)}) collective-permute-start(f32[1,16,512]{2,1,0:T(8,128)S(1)} %get-tuple-element.23), channel_id=1, source_target_pairs={{32,0},{64,32},{96,64},{128,96},{160,128},{192,160},{224,192},{256... | collective-permute-start | bytes 98312 | tf_op jit(solution)/shard_map/ppermute | solution.py:23
  72.7 6.1 %collective-permute-start.13 = (f32[1,16,512]{2,1,0:T(8,128)S(1)}, f32[1,16,512]{2,1,0:T(8,128)S(1)}, u32[]{:S(2)}, u32[]{:S(2)}) collective-permute-start(f32[1,16,512]{2,1,0:T(8,128)S(1)} %get-tuple-element.22), channel_id=1, source_target_pairs={{0,32},{32,64},{64,96},{96,128},{128,160},{160,192},{192,224},{224... | collective-permute-start | bytes 98312 | tf_op jit(solution)/shard_map/ppermute | solution.py:20
  78.9 6.0 %collective-permute-start.14 = (f32[10,1,512]{2,1,0:T(1,128)S(1)}, f32[10,1,512]{2,1,0:T(1,128)S(1)}, u32[]{:S(2)}, u32[]{:S(2)}) collective-permute-start(f32[10,1,512]{2,1,0:T(1,128)S(1)} %get-tuple-element.10), channel_id=1, source_target_pairs={{1,0},{2,1},{3,2},{4,3},{5,4},{6,5},{7,6},{8,7},{9,8},{10,9},{11,1... | collective-permute-start | bytes 61448 | tf_op jit(solution)/shard_map/ppermute | solution.py:23
  80.8 7.8 %collective-permute-start.15 = (f32[10,1,512]{2,1,0:T(1,128)S(1)}, f32[10,1,512]{2,1,0:T(1,128)S(1)}, u32[]{:S(2)}, u32[]{:S(2)}) collective-permute-start(f32[10,1,512]{2,1,0:T(1,128)S(1)} %get-tuple-element.11), channel_id=1, source_target_pairs={{0,1},{1,2},{2,3},{3,4},{4,5},{5,6},{6,7},{7,8},{8,9},{9,10},{10,1... | collective-permute-start | bytes 61448 | tf_op jit(solution)/shard_map/ppermute | solution.py:20
  84.9 5.9 %copy-start.3 = (f32[512,128]{1,0:T(8,128)}, f32[512,128]{1,0:T(8,128)S(1)}, u32[]{:S(2)}) copy-start(f32[512,128]{1,0:T(8,128)S(1)} %reshape.159) | copy-start | bytes 786436
  214.9 2.3 copy-start.1
  217.2 18.5 %copy-start.4 = (f32[8,8192]{1,0:T(8,128)S(1)}, f32[8,8192]{1,0:T(8,128)}, u32[]{:S(2)}) copy-start(f32[8,8192]{1,0:T(8,128)} %param.3) | copy-start | bytes 786436
  217.5 5.1 %collective-permute-start.16 = (f32[1,16,512]{2,1,0:T(8,128)S(1)}, f32[1,16,512]{2,1,0:T(8,128)S(1)}, u32[]{:S(2)}, u32[]{:S(2)}) collective-permute-start(f32[1,16,512]{2,1,0:T(8,128)S(1)} %get-tuple-element.19), channel_id=1, source_target_pairs={{32,0},{64,32},{96,64},{128,96},{160,128},{192,160},{224,192},{256... | collective-permute-start | bytes 98312 | tf_op jit(solution)/shard_map/ppermute | solution.py:23
  218.8 3.9 %collective-permute-start.17 = (f32[1,16,512]{2,1,0:T(8,128)S(1)}, f32[1,16,512]{2,1,0:T(8,128)S(1)}, u32[]{:S(2)}, u32[]{:S(2)}) collective-permute-start(f32[1,16,512]{2,1,0:T(8,128)S(1)} %get-tuple-element.18), channel_id=1, source_target_pairs={{0,32},{32,64},{64,96},{96,128},{128,160},{160,192},{192,224},{224... | collective-permute-start | bytes 98312 | tf_op jit(solution)/shard_map/ppermute | solution.py:20
  222.7 7.1 %collective-permute-start.18 = (f32[10,1,512]{2,1,0:T(1,128)S(1)}, f32[10,1,512]{2,1,0:T(1,128)S(1)}, u32[]{:S(2)}, u32[]{:S(2)}) collective-permute-start(f32[10,1,512]{2,1,0:T(1,128)S(1)} %get-tuple-element.8), channel_id=1, source_target_pairs={{1,0},{2,1},{3,2},{4,3},{5,4},{6,5},{7,6},{8,7},{9,8},{10,9},{11,1... | collective-permute-start | bytes 61448 | tf_op jit(solution)/shard_map/ppermute | solution.py:23
  227.7 8.0 %collective-permute-start.19 = (f32[10,1,512]{2,1,0:T(1,128)S(1)}, f32[10,1,512]{2,1,0:T(1,128)S(1)}, u32[]{:S(2)}, u32[]{:S(2)}) collective-permute-start(f32[10,1,512]{2,1,0:T(1,128)S(1)} %get-tuple-element.9), channel_id=1, source_target_pairs={{0,1},{1,2},{2,3},{3,4},{4,5},{5,6},{6,7},{7,8},{8,9},{9,10},{10,1... | collective-permute-start | bytes 61448 | tf_op jit(solution)/shard_map/ppermute | solution.py:20
where the time goes:
time: 242 us; the launch traced here: 237 us
  blocking collectives  102 us (42%)
  starting transfers between devices  64.4 us (27%)
  local copies, waits for them, and re-layouts  23.5 us (10%)
  waiting for transfers between devices  21.3 us (9%)
  other arithmetic  19 us (8%)
  matrix products  5.15 us (2%)
    psum x1, blocking collectives, per_device(): gram = lax.psum(local_gram, ('gx', 'gy'))  102 us
    ppermute x10, starting transfers between devices, extended(): lax.ppermute(lax.slice_in_dim(block, 0, width, axis=dim), axis, backward)  32.3 us
    ppermute x10, starting transfers between devices, extended(): lax.ppermute(lax.slice_in_dim(block, block.shape[dim] - width, None, axis...  32.1 us
    ppermute x10, waiting for transfers between devices, extended(): lax.ppermute(lax.slice_in_dim(block, block.shape[dim] - width, None, axis...  21.3 us
    reshape x5, local copies, waits for them, and re-layouts, widen(): jnp.repeat(table[:, :, i * NZ:(i + 1) * NZ], RHS, axis=2)  7.77 us
    another operation x3, other arithmetic, per_device(): factor = jnp.linalg.cholesky(normal)  5.05 us
    reshape x1, local copies, waits for them, and re-layouts, per_device(): products = products.reshape(blocks, groups, RHS, blocks, groups, RHS)  4.93 us
  transfers between devices with their start and end apart: 20, of which 8 were waited for; matrix products, arithmetic and copies ran while one was open for 7% of the time, Pallas kernels for 0%

commit v1 on v0

v1 whole, which is shorter than its diff:
```python
import jax
import jax.numpy as jnp
from jax import lax
from jax.sharding import PartitionSpec as P

NZ = 32
RHS = 16
STEPS = 3


SHIFT = 7.5
SCALE = 4.0

HIGH = lax.Precision.HIGHEST


def exchange(arrays, axis, dim_of):
    count = lax.axis_size(axis)
    forward = [(i, i + 1) for i in range(count - 1)]
    backward = [(i + 1, i) for i in range(count - 1)]
    ups, downs, shapes = [], [], []
    for block, width in arrays:
        dim = dim_of(block)
        top = lax.slice_in_dim(block, block.shape[dim] - width, None, axis=dim)
        bottom = lax.slice_in_dim(block, 0, width, axis=dim)
        ups.append(top.reshape(-1))
        downs.append(bottom.reshape(-1))
        shapes.append(top.shape)
    low = lax.ppermute(jnp.concatenate(ups), axis, forward)
    high = lax.ppermute(jnp.concatenate(downs), axis, backward)
    out = []
    offset = 0
    for (block, width), shape in zip(arrays, shapes):
        size = 1
        for s in shape:
            size *= s
        dim = dim_of(block)
        lo = low[offset : offset + size].reshape(shape)
        hi = high[offset : offset + size].reshape(shape)
        offset += size
        out.append(jnp.concatenate([lo, block, hi], axis=dim))
    return out


def operate(padded, coefs):
    diffusivity, drift_x, drift_y, drift_z, reaction = coefs
    center = padded[1:-1, 1:-1]
    x_plus = padded[2:, 1:-1]
    x_minus = padded[:-2, 1:-1]
    y_plus = padded[1:-1, 2:]
    y_minus = padded[1:-1, :-2]
    zero_rim = jnp.zeros(center.shape[:2] + (RHS,), center.dtype)
    z_plus = jnp.concatenate([center[:, :, RHS:], zero_rim], axis=2)
    z_minus = jnp.concatenate([zero_rim, center[:, :, :-RHS]], axis=2)
    beside = x_plus + x_minus + y_plus + y_minus + z_plus + z_minus
    drift = (
        drift_x * (x_plus - x_minus) + drift_y * (y_plus - y_minus) + drift_z * (z_plus - z_minus)
    )
    return (reaction + 6.0 * diffusivity) * center - diffusivity * beside + 0.5 * drift


def crop(coefs, margin):
    if margin == 0:
        return coefs
    return [c[margin:-margin, margin:-margin] for c in coefs]


def allreduce(x, axes):
    for axis in axes:
        count = lax.axis_size(axis)
        bit = 1
        while bit < count:
            x = x + lax.ppermute(x, axis, [(i, i ^ bit) for i in range(count)])
            bit *= 2
    return x


def per_device(right_side, initial_guess, coefficients):
    rows_x = right_side.shape[0]
    rows_y = right_side.shape[1] // (NZ * RHS)
    width = NZ * RHS
    depth = STEPS + 1
    rhs_field = right_side.reshape(rows_x, rows_y, width)
    guess = initial_guess.reshape(rows_x, rows_y, width)
    coef = coefficients.reshape(5, rows_x, rows_y, NZ)

    guess_e, rhs_e, coef_e = exchange(
        [(guess, depth), (rhs_field, depth - 1), (coef, depth - 1)],
        "gx",
        lambda a: 0 if a.ndim == 3 else 1,
    )
    guess_e, rhs_e, coef_e = exchange(
        [(guess_e, depth), (rhs_e, depth - 1), (coef_e, depth - 1)],
        "gy",
        lambda a: 1 if a.ndim == 3 else 2,
    )
    ex, ey = coef_e.shape[1], coef_e.shape[2]
    spread = jnp.repeat(jnp.eye(NZ, dtype=jnp.float32), RHS, axis=1)
    wide = jnp.dot(coef_e.reshape(5 * ex * ey, NZ), spread, precision=HIGH).reshape(5, ex, ey, width)
    coefs = [wide[i] for i in range(5)]

    current = rhs_e - operate(guess_e, coefs)
    krylov = [current]
    for step in range(STEPS):
        inner = crop(coefs, step + 1)
        center = current[1:-1, 1:-1]
        current = (operate(current, inner) - SHIFT * center) / SCALE
        krylov.append(current)
    local = []
    for j, block in enumerate(krylov):
        margin = STEPS - j
        if margin:
            block = block[margin:-margin, margin:-margin]
        local.append(block)

    blocks = len(local)
    groups = 128 // RHS
    stacked = jnp.concatenate([v.reshape(-1, 128) for v in local], axis=1)
    products = jnp.dot(stacked.T, stacked, precision=HIGH)
    products = products.reshape(blocks, groups, RHS, blocks, groups, RHS)
    diagonal = jnp.eye(groups, dtype=jnp.float32)[None, :, None, None, :, None]
    local_gram = jnp.sum(products * diagonal, axis=(1, 4)).reshape(blocks * RHS, blocks * RHS)
    gram = allreduce(local_gram, ("gx", "gy"))
    shift_map = SHIFT * jnp.eye(blocks * RHS, STEPS * RHS, dtype=jnp.float32) + SCALE * jnp.eye(
        blocks * RHS, STEPS * RHS, k=-RHS, dtype=jnp.float32
    )
    normal = jnp.dot(
        shift_map.T,
        jnp.dot(gram, shift_map, precision=HIGH),
        precision=HIGH,
    )
    target = jnp.dot(shift_map.T, gram[:, :RHS], precision=HIGH)
    factor = jnp.linalg.cholesky(normal)
    weights = jax.scipy.linalg.cho_solve((factor, True), target)
    padded = jnp.concatenate([weights, jnp.zeros((RHS, RHS), jnp.float32)], axis=0)
    applied = jnp.dot(shift_map, weights, precision=HIGH)
    eye_g = jnp.eye(groups, dtype=jnp.float32)
    mix = jnp.concatenate(
        [
            jnp.concatenate(
                [jnp.kron(eye_g, padded[j * RHS : (j + 1) * RHS]), jnp.kron(eye_g, applied[j * RHS : (j + 1) * RHS])],
                axis=1,
            )
            for j in range(blocks)
        ],
        axis=0,
    )
    updates = jnp.dot(stacked, mix, precision=HIGH)
    solution = guess.reshape(-1, 128) + updates[:, :128]
    residual = local[0].reshape(-1, 128) - updates[:, 128:]
    return (
        solution.reshape(rows_x, rows_y * NZ * RHS),
        residual.reshape(rows_x, rows_y * NZ * RHS),
    )


def solution(mesh):
    placed = (P("gx", "gy"), P("gx", "gy"), P(None, "gx", "gy"))
    return jax.shard_map(
        per_device,
        mesh=mesh,
        in_specs=placed,
        out_specs=(P("gx", "gy"), P("gx", "gy")),
        check_vma=False,
    )
```

time: 242 us -> 157 us (0.65); the launches traced: 237 us -> 156 us
  blocking collectives: 102 us -> 0 us
  local copies, waits for them, and re-layouts: 23.5 us -> 35.8 us
  waiting for transfers between devices: 21.3 us -> 32.5 us
  starting transfers between devices: 64.4 us -> 56.9 us
  other arithmetic: 19 us -> 22.3 us
    psum x1 -> x0, blocking collectives: 102 us -> none  [per_device(): gram = lax.psum(local_gram, ('gx', 'gy'))]
    ppermute x20 -> x13, waiting for transfers between devices: 21.3 us -> 32.5 us  [the longest x9 25.7 us: allreduce(): x = x + lax.ppermute(x, axis, [(i, i ^ bit) for i in range(count)])]
    ppermute x20 -> x13, starting transfers between devices: 64.4 us -> 56.9 us  [the longest x9 40.7 us: allreduce(): x = x + lax.ppermute(x, axis, [(i, i ^ bit) for i in range(count)])]
    slice x13 -> x29, local copies, waits for them, and re-layouts: 1.72 us -> 7.95 us  [the longest x6 2.47 us: exchange(): hi = high[offset:offset + size].reshape(shape)]
    mul x3 -> x7, local copies, waits for them, and re-layouts: 0.56 us -> 5.48 us  [the longest x4 2.83 us: per_device(): jnp.kron(eye_g, applied[j * RHS:(j + 1) * RHS])]
    broadcast_in_dim x5 -> x1, local copies, waits for them, and re-layouts: 3.01 us -> 0.02 us  [per_device(): spread = jnp.repeat(jnp.eye(NZ, dtype=jnp.float32), RHS, axis=1)]
    reshape x18 -> x28, local copies, waits for them, and re-layouts: 9.48 us -> 9.3 us  [the longest x6 2.5 us: exchange(): hi = high[offset:offset + size].reshape(shape)]
  transfers between devices with their start and end apart: 20 -> 13, of which waited for: 8 -> 12; matrix products, arithmetic and copies ran while one was open for 7% -> 0% of each run, Pallas kernels for 0% -> 0%
where the time goes in v1:
time: 157 us; the launch traced here: 156 us
  starting transfers between devices  56.9 us (36%)
  local copies, waits for them, and re-layouts  35.8 us (23%)
  waiting for transfers between devices  32.5 us (21%)
  other arithmetic  22.3 us (14%)
  matrix products  6.94 us (4%)
    ppermute x9, starting transfers between devices, allreduce(): x = x + lax.ppermute(x, axis, [(i, i ^ bit) for i in range(count)])  40.7 us
    ppermute x9, waiting for transfers between devices, allreduce(): x = x + lax.ppermute(x, axis, [(i, i ^ bit) for i in range(count)])  25.7 us
    ppermute x2, starting transfers between devices, exchange(): high = lax.ppermute(jnp.concatenate(downs), axis, backward)  10.1 us
    ppermute x2, starting transfers between devices, exchange(): low = lax.ppermute(jnp.concatenate(ups), axis, forward)  6.04 us
    reshape x1, local copies, waits for them, and re-layouts, per_device(): products = products.reshape(blocks, groups, RHS, blocks, groups, RHS)  5.1 us
    another operation x3, other arithmetic, per_device(): factor = jnp.linalg.cholesky(normal)  5.05 us
    ppermute x2, waiting for transfers between devices, exchange(): high = lax.ppermute(jnp.concatenate(downs), axis, backward)  4.89 us
    reduce_sum x1, other arithmetic, per_device(): jnp.sum(products * diagonal, axis=(1, 4))  4.78 us
  transfers between devices with their start and end apart: 13, of which 12 were waited for; matrix products, arithmetic and copies ran while one was open for 0% of the time, Pallas kernels for 0%

profile of v1, /device:TPU:6, one launch (start us, length us, event | category | flops | bytes accessed | tf_op | source)
XLA Modules:
  0.0 156.0 jit_solution(8181201047331516054)
XLA Ops:
  0.6 1.1 reshape.207
  1.8 1.1 slice_bitcast_fusion.2
  2.9 1.1 fusion.94
  4.1 1.8 %collective-permute-start = (f32[65024]{0:T(1024)S(1)}, f32[65024]{0:T(1024)S(1)}, u32[]{:S(2)}, u32[]{:S(2)}) collective-permute-start(f32[65024]{0:T(1024)S(1)} %pad_maximum_fusion.2), channel_id=1, source_target_pairs={{0,32},{32,64},{64,96},{96,128},{128,160},{160,192},{192,224},{224... | collective-permute-start | bytes 780296 | tf_op jit(solution)/shard_map/ppermute | solution.py:29
  6.1 1.3 collective-permute-start.1
  7.6 3.3 %collective-permute-done.1 = f32[65024]{0:T(1024)S(1)} collective-permute-done((f32[65024]{0:T(1024)S(1)}, f32[65024]{0:T(1024)S(1)}, u32[]{:S(2)}, u32[]{:S(2)}) %collective-permute-start.1) | collective-permute-done | bytes 260128 | tf_op jit(solution)/shard_map/ppermute | solution.py:30
  11.3 1.1 copy_dynamic-update-slice_fusion.1
  13.0 4.3 %collective-permute-start.2 = (f32[60992]{0:T(1024)S(1)}, f32[60992]{0:T(1024)S(1)}, u32[]{:S(2)}, u32[]{:S(2)}) collective-permute-start(f32[60992]{0:T(1024)S(1)} %pad_maximum_fusion.4), channel_id=1, source_target_pairs={{0,1},{1,2},{2,3},{3,4},{4,5},{5,6},{6,7},{7,8},{8,9},{9,10},{10,1... | collective-permute-start | bytes 731912 | tf_op jit(solution)/shard_map/ppermute | solution.py:29
  17.5 8.9 %collective-permute-start.3 = (f32[60992]{0:T(1024)S(1)}, f32[60992]{0:T(1024)S(1)}, u32[]{:S(2)}, u32[]{:S(2)}) collective-permute-start(f32[60992]{0:T(1024)S(1)} %pad_maximum_fusion.5), channel_id=1, source_target_pairs={{1,0},{2,1},{3,2},{4,3},{5,4},{6,5},{7,6},{8,7},{9,8},{10,9},{11,1... | collective-permute-start | bytes 731912 | tf_op jit(solution)/shard_map/ppermute | solution.py:30
  26.4 2.0 %collective-permute-done.2 = f32[60992]{0:T(1024)S(1)} collective-permute-done((f32[60992]{0:T(1024)S(1)}, f32[60992]{0:T(1024)S(1)}, u32[]{:S(2)}, u32[]{:S(2)}) %collective-permute-start.2) | collective-permute-done | bytes 244000 | tf_op jit(solution)/shard_map/ppermute | solution.py:29
  28.5 1.6 %collective-permute-done.3 = f32[60992]{0:T(1024)S(1)} collective-permute-done((f32[60992]{0:T(1024)S(1)}, f32[60992]{0:T(1024)S(1)}, u32[]{:S(2)}, u32[]{:S(2)}) %collective-permute-start.3) | collective-permute-done | bytes 244000 | tf_op jit(solution)/shard_map/ppermute | solution.py:30
  31.2 2.7 %fusion.97 = f32[1540,512]{1,0:T(8,128)S(1)} fusion(f32[1540,32]{1,0:T(8,128)S(1)} %reshape.242, f32[32,512]{0,1:T(8,128)S(1)} %bitcast.55), kind=kOutput, calls=%fused_computation.157 | convolution fusion | flops 302776320 | bytes 3416576 | tf_op jit(solution)/shard_map/dot_general | solution.py:99
  33.9 1.3 fusion.86
  35.4 1.2 squeeze.18
  39.8 1.3 pad_maximum_fusion.1
  41.1 1.4 fusion.87
  42.4 1.5 slice.386
  44.0 1.6 %reshape.223 = f32[14,3,512]{2,1,0:T(4,128)} reshape(f32[21504]{0:T(1024)} %slice.386) | data formatting | bytes 172032 | tf_op jit(solution)/shard_map/reshape | solution.py:38
  45.5 1.5 slice.390
  47.1 1.6 %reshape.227 = f32[14,3,512]{2,1,0:T(4,128)} reshape(f32[21504]{0:T(1024)} %slice.390) | data formatting | bytes 172032 | tf_op jit(solution)/shard_map/reshape | solution.py:39
  48.6 2.7 %fusion.2 = f32[14,22,512]{2,1,0:T(8,128)S(1)} fusion(f32[16,24,512]{2,1,0:T(8,128)S(1)} %pad_maximum_fusion.1, f32[14,3,512]{2,1,0:T(4,128)} %reshape.227, f32[14,16,512]{2,1,0:T(8,128)} %copy-done.3, f32[14,3,512]{2,1,0:T(4,128)} %reshape.223, f32[14,22,512]{2,1,0:T(8,128)} %squeeze.19, f32[14,22,512]{2,1,0:T(8,128)S(1)} %squeeze.18, ...), kind=kLoop, calls=%fused_computation.6 | loop fusion | flops 3627008 | bytes 8791552 | tf_op jit(solution)/shard_map/sub | solution.py:102
  56.2 1.9 %fusion.98 = f32[512,512]{1,0:T(8,128)S(1)} fusion(f32[512,512]{1,0:T(8,128)S(1)} %constant_dynamic-update-slice_fusion.7), kind=kOutput, calls=%fused_computation.158 | convolution fusion | flops 1610612736 | bytes 2097152 | tf_op jit(solution)/shard_map/dot_general | solution.py:119
  58.1 5.1 %reshape.238 = f32[4,8,16,4,8,16]{5,4,3,2,1,0:T(8,128)} reshape(f32[512,512]{1,0:T(8,128)S(1)} %fusion.98) | data formatting | bytes 2097152 | tf_op jit(solution)/shard_map/reshape | solution.py:120
  63.2 4.8 %multiply_reduce_fusion = f32[4,16,4,16]{3,2,1,0:T(4,128)S(1)} fusion(f32[4,8,16,4,8,16]{5,4,3,2,1,0:T(8,128)} %reshape.238, f32[8,8]{1,0:T(8,128)S(1)} %fusion.70), kind=kLoop, calls=%fused_computation | loop fusion | flops 520192 | bytes 1065216 | tf_op jit(solution)/shard_map/reduce_sum | solution.py:122
  68.1 5.8 %collective-permute-start.4 = (f32[64,64]{1,0:T(8,128)S(1)}, f32[64,64]{1,0:T(8,128)S(1)}, u32[]{:S(2)}, u32[]{:S(2)}) collective-permute-start(f32[64,64]{1,0:T(8,128)S(1)} %reshape.239), channel_id=1, source_target_pairs={{0,32},{32,0},{64,96},{96,64},{128,160},{160,128},{192,224},{224,1... | collective-permute-start | bytes 49160 | tf_op jit(solution)/shard_map/ppermute | solution.py:73
  74.8 5.2 %collective-permute-start.5 = (f32[64,64]{1,0:T(8,128)S(1)}, f32[64,64]{1,0:T(8,128)S(1)}, u32[]{:S(2)}, u32[]{:S(2)}) collective-permute-start(f32[64,64]{1,0:T(8,128)S(1)} %add.230), channel_id=1, source_target_pairs={{0,64},{32,96},{64,0},{96,32},{128,192},{160,224},{192,128},{224,1... | collective-permute-start | bytes 49160 | tf_op jit(solution)/shard_map/ppermute | solution.py:73
  80.0 1.9 %collective-permute-done.5 = f32[64,64]{1,0:T(8,128)S(1)} collective-permute-done((f32[64,64]{1,0:T(8,128)S(1)}, f32[64,64]{1,0:T(8,128)S(1)}, u32[]{:S(2)}, u32[]{:S(2)}) %collective-permute-start.5) | collective-permute-done | bytes 16416 | tf_op jit(solution)/shard_map/ppermute | solution.py:73
  81.9 5.1 %collective-permute-start.6 = (f32[64,64]{1,0:T(8,128)S(1)}, f32[64,64]{1,0:T(8,128)S(1)}, u32[]{:S(2)}, u32[]{:S(2)}) collective-permute-start(f32[64,64]{1,0:T(8,128)S(1)} %add.231), channel_id=1, source_target_pairs={{0,128},{32,160},{64,192},{96,224},{128,0},{160,32},{192,64},{224,... | collective-permute-start | bytes 49160 | tf_op jit(solution)/shard_map/ppermute | solution.py:73
  87.1 2.2 %collective-permute-done.6 = f32[64,64]{1,0:T(8,128)S(1)} collective-permute-done((f32[64,64]{1,0:T(8,128)S(1)}, f32[64,64]{1,0:T(8,128)S(1)}, u32[]{:S(2)}, u32[]{:S(2)}) %collective-permute-start.6) | collective-permute-done | bytes 16416 | tf_op jit(solution)/shard_map/ppermute | solution.py:73
  89.2 8.1 %collective-permute-start.7 = (f32[64,64]{1,0:T(8,128)S(1)}, f32[64,64]{1,0:T(8,128)S(1)}, u32[]{:S(2)}, u32[]{:S(2)}) collective-permute-start(f32[64,64]{1,0:T(8,128)S(1)} %add.232), channel_id=1, source_target_pairs={{0,256},{32,288},{64,320},{96,352},{128,384},{160,416},{192,448},{... | collective-permute-start | bytes 49160 | tf_op jit(solution)/shard_map/ppermute | solution.py:73
  97.3 2.0 %collective-permute-done.7 = f32[64,64]{1,0:T(8,128)S(1)} collective-permute-done((f32[64,64]{1,0:T(8,128)S(1)}, f32[64,64]{1,0:T(8,128)S(1)}, u32[]{:S(2)}, u32[]{:S(2)}) %collective-permute-start.7) | collective-permute-done | bytes 16416 | tf_op jit(solution)/shard_map/ppermute | solution.py:73
  99.3 1.9 %collective-permute-start.8 = (f32[64,64]{1,0:T(8,128)S(1)}, f32[64,64]{1,0:T(8,128)S(1)}, u32[]{:S(2)}, u32[]{:S(2)}) collective-permute-start(f32[64,64]{1,0:T(8,128)S(1)} %add.233), channel_id=1, source_target_pairs={{0,1},{1,0},{2,3},{3,2},{4,5},{5,4},{6,7},{7,6},{8,9},{9,8},{10,11... | collective-permute-start | bytes 49160 | tf_op jit(solution)/shard_map/ppermute | solution.py:73
  101.2 3.9 %collective-permute-done.8 = f32[64,64]{1,0:T(8,128)S(1)} collective-permute-done((f32[64,64]{1,0:T(8,128)S(1)}, f32[64,64]{1,0:T(8,128)S(1)}, u32[]{:S(2)}, u32[]{:S(2)}) %collective-permute-start.8) | collective-permute-done | bytes 16416 | tf_op jit(solution)/shard_map/ppermute | solution.py:73
  105.1 4.1 %collective-permute-start.9 = (f32[64,64]{1,0:T(8,128)S(1)}, f32[64,64]{1,0:T(8,128)S(1)}, u32[]{:S(2)}, u32[]{:S(2)}) collective-permute-start(f32[64,64]{1,0:T(8,128)S(1)} %add.234), channel_id=1, source_target_pairs={{0,2},{1,3},{2,0},{3,1},{4,6},{5,7},{6,4},{7,5},{8,10},{9,11},{10,... | collective-permute-start | bytes 49160 | tf_op jit(solution)/shard_map/ppermute | solution.py:73
  109.2 2.6 %collective-permute-done.9 = f32[64,64]{1,0:T(8,128)S(1)} collective-permute-done((f32[64,64]{1,0:T(8,128)S(1)}, f32[64,64]{1,0:T(8,128)S(1)}, u32[]{:S(2)}, u32[]{:S(2)}) %collective-permute-start.9) | collective-permute-done | bytes 16416 | tf_op jit(solution)/shard_map/ppermute | solution.py:73
  111.8 5.3 %collective-permute-start.10 = (f32[64,64]{1,0:T(8,128)S(1)}, f32[64,64]{1,0:T(8,128)S(1)}, u32[]{:S(2)}, u32[]{:S(2)}) collective-permute-start(f32[64,64]{1,0:T(8,128)S(1)} %add.235), channel_id=1, source_target_pairs={{0,4},{1,5},{2,6},{3,7},{4,0},{5,1},{6,2},{7,3},{8,12},{9,13},{10,... | collective-permute-start | bytes 49160 | tf_op jit(solution)/shard_map/ppermute | solution.py:73
  117.1 4.5 %collective-permute-done.10 = f32[64,64]{1,0:T(8,128)S(1)} collective-permute-done((f32[64,64]{1,0:T(8,128)S(1)}, f32[64,64]{1,0:T(8,128)S(1)}, u32[]{:S(2)}, u32[]{:S(2)}) %collective-permute-start.10) | collective-permute-done | bytes 16416 | tf_op jit(solution)/shard_map/ppermute | solution.py:73
  121.6 2.4 %collective-permute-start.11 = (f32[64,64]{1,0:T(8,128)S(1)}, f32[64,64]{1,0:T(8,128)S(1)}, u32[]{:S(2)}, u32[]{:S(2)}) collective-permute-start(f32[64,64]{1,0:T(8,128)S(1)} %add.236), channel_id=1, source_target_pairs={{0,8},{1,9},{2,10},{3,11},{4,12},{5,13},{6,14},{7,15},{8,0},{9,1},... | collective-permute-start | bytes 49160 | tf_op jit(solution)/shard_map/ppermute | solution.py:73
  124.0 3.4 %collective-permute-done.11 = f32[64,64]{1,0:T(8,128)S(1)} collective-permute-done((f32[64,64]{1,0:T(8,128)S(1)}, f32[64,64]{1,0:T(8,128)S(1)}, u32[]{:S(2)}, u32[]{:S(2)}) %collective-permute-start.11) | collective-permute-done | bytes 16416 | tf_op jit(solution)/shard_map/ppermute | solution.py:73
  127.4 2.9 %collective-permute-start.12 = (f32[64,64]{1,0:T(8,128)S(1)}, f32[64,64]{1,0:T(8,128)S(1)}, u32[]{:S(2)}, u32[]{:S(2)}) collective-permute-start(f32[64,64]{1,0:T(8,128)S(1)} %add.237), channel_id=1, source_target_pairs={{0,16},{1,17},{2,18},{3,19},{4,20},{5,21},{6,22},{7,23},{8,24},{9,... | collective-permute-start | bytes 49160 | tf_op jit(solution)/shard_map/ppermute | solution.py:73
  130.4 4.4 %collective-permute-done.12 = f32[64,64]{1,0:T(8,128)S(1)} collective-permute-done((f32[64,64]{1,0:T(8,128)S(1)}, f32[64,64]{1,0:T(8,128)S(1)}, u32[]{:S(2)}, u32[]{:S(2)}) %collective-permute-start.12) | collective-permute-done | bytes 16416 | tf_op jit(solution)/shard_map/ppermute | solution.py:73
  135.7 4.4 %cholesky.16 = f32[48,48]{1,0:T(8,128)S(1)} custom-call(f32[48,48]{1,0:T(8,128)S(1)} %fusion.52), custom_call_target="Cholesky" | custom-call | tf_op jit(solution)/shard_map/jit(cholesky)/cholesky | solution.py:133
  141.4 3.7 %custom-call.10 = f32[1,48,48]{1,2,0:T(8,128)S(1)} custom-call(f32[1,48,48]{2,1,0:T(8,128)S(1)} %fusion.47), custom_call_target="InvertDiagBlocksLowerTriangular" | custom-call | tf_op jit(solution)/shard_map/jit(_cho_solve)/triangular_solve | solution.py:134
  146.3 1.6 %broadcast_multiply_fusion.6 = (f32[8,16,8,16]{3,2,1,0:T(8,128)}, f32[8,16,8,16]{3,2,1,0:T(8,128)}, f32[8,16,8,16]{3,2,1,0:T(8,128)}, f32[8,16,8,16]{3,2,1,0:T(8...) fusion(f32[16,16]{1,0:T(8,128)S(1)} %copy.51, ...), kind=kLoop, calls=%fused_computation.72 | loop fusion | flops 114688 | bytes 466176 | tf_op jit(solution)/shard_map/jit(kron)/mul | solution.py:141
  147.9 1.2 mul.353
  149.1 1.2 mul.356
  150.4 1.2 mul.359
  151.6 1.2 mul.362
  (129 shorter events, 18.6 us)
Async XLA Ops:
  0.6 12.0 %copy-start.4 = (f32[8,8192]{1,0:T(8,128)S(1)}, f32[8,8192]{1,0:T(8,128)}, u32[]{:S(2)}) copy-start(f32[8,8192]{1,0:T(8,128)} %param.3) | copy-start | bytes 786436
  4.1 3.3 %collective-permute-start = (f32[65024]{0:T(1024)S(1)}, f32[65024]{0:T(1024)S(1)}, u32[]{:S(2)}, u32[]{:S(2)}) collective-permute-start(f32[65024]{0:T(1024)S(1)} %pad_maximum_fusion.2), channel_id=1, source_target_pairs={{0,32},{32,64},{64,96},{96,128},{128,160},{160,192},{192,224},{224... | collective-permute-start | bytes 780296 | tf_op jit(solution)/shard_map/ppermute | solution.py:29
  6.1 4.8 %collective-permute-start.1 = (f32[65024]{0:T(1024)S(1)}, f32[65024]{0:T(1024)S(1)}, u32[]{:S(2)}, u32[]{:S(2)}) collective-permute-start(f32[65024]{0:T(1024)S(1)} %pad_maximum_fusion.3), channel_id=1, source_target_pairs={{32,0},{64,32},{96,64},{128,96},{160,128},{192,160},{224,192},{256... | collective-permute-start | bytes 780296 | tf_op jit(solution)/shard_map/ppermute | solution.py:30
  12.5 18.5 %copy-start.2 = (f32[16,16,512]{2,1,0:T(8,128)}, f32[16,16,512]{2,1,0:T(8,128)S(1)}, u32[]{:S(2)}) copy-start(f32[16,16,512]{2,1,0:T(8,128)S(1)} %constant_dynamic-update-slice_fusion) | copy-start | bytes 1572868
  12.9 17.2 %copy-start.3 = (f32[14,16,512]{2,1,0:T(8,128)}, f32[14,16,512]{2,1,0:T(8,128)S(1)}, u32[]{:S(2)}) copy-start(f32[14,16,512]{2,1,0:T(8,128)S(1)} %constant_dynamic-update-slice_fusion.2) | copy-start | bytes 1376260
  13.0 15.4 %collective-permute-start.2 = (f32[60992]{0:T(1024)S(1)}, f32[60992]{0:T(1024)S(1)}, u32[]{:S(2)}, u32[]{:S(2)}) collective-permute-start(f32[60992]{0:T(1024)S(1)} %pad_maximum_fusion.4), channel_id=1, source_target_pairs={{0,1},{1,2},{2,3},{3,4},{4,5},{5,6},{6,7},{7,8},{8,9},{9,10},{10,1... | collective-permute-start | bytes 731912 | tf_op jit(solution)/shard_map/ppermute | solution.py:29
  17.5 12.6 %collective-permute-start.3 = (f32[60992]{0:T(1024)S(1)}, f32[60992]{0:T(1024)S(1)}, u32[]{:S(2)}, u32[]{:S(2)}) collective-permute-start(f32[60992]{0:T(1024)S(1)} %pad_maximum_fusion.5), channel_id=1, source_target_pairs={{1,0},{2,1},{3,2},{4,3},{5,4},{6,5},{7,6},{8,7},{9,8},{10,9},{11,1... | collective-permute-start | bytes 731912 | tf_op jit(solution)/shard_map/ppermute | solution.py:30
  28.4 1.7 %copy-start.5 = (f32[60992]{0:T(1024)}, f32[60992]{0:T(1024)S(1)}, u32[]{:S(2)}) copy-start(f32[60992]{0:T(1024)S(1)} %collective-permute-done.2) | copy-start | bytes 731908
  30.1 0.7 copy-start.6
  31.2 6.3 %slice-start = ((f32[60992]{0:T(1024)}), f32[32768]{0:T(1024)S(1)}, s32[]{:S(2)}) async-start(f32[60992]{0:T(1024)} %copy-done.5), calls=%async_computation | async-start | bytes 262144 | tf_op jit(solution)/shard_map/slice | solution.py:38
  48.6 2.9 %copy-start = (f32[14,22,512]{2,1,0:T(8,128)S(1)}, f32[14,22,512]{2,1,0:T(8,128)}, u32[]{:S(2)}) copy-start(f32[14,22,512]{2,1,0:T(8,128)} %squeeze.19) | copy-start | bytes 1892356
  58.1 72.2 %copy-start.1 = (f32[8,8192]{1,0:T(8,128)S(1)}, f32[8,8192]{1,0:T(8,128)}, u32[]{:S(2)}) copy-start(f32[8,8192]{1,0:T(8,128)} %param.4) | copy-start | bytes 786436
  68.1 6.7 %collective-permute-start.4 = (f32[64,64]{1,0:T(8,128)S(1)}, f32[64,64]{1,0:T(8,128)S(1)}, u32[]{:S(2)}, u32[]{:S(2)}) collective-permute-start(f32[64,64]{1,0:T(8,128)S(1)} %reshape.239), channel_id=1, source_target_pairs={{0,32},{32,0},{64,96},{96,64},{128,160},{160,128},{192,224},{224,1... | collective-permute-start | bytes 49160 | tf_op jit(solution)/shard_map/ppermute | solution.py:73
  74.8 7.1 %collective-permute-start.5 = (f32[64,64]{1,0:T(8,128)S(1)}, f32[64,64]{1,0:T(8,128)S(1)}, u32[]{:S(2)}, u32[]{:S(2)}) collective-permute-start(f32[64,64]{1,0:T(8,128)S(1)} %add.230), channel_id=1, source_target_pairs={{0,64},{32,96},{64,0},{96,32},{128,192},{160,224},{192,128},{224,1... | collective-permute-start | bytes 49160 | tf_op jit(solution)/shard_map/ppermute | solution.py:73
  81.9 7.3 %collective-permute-start.6 = (f32[64,64]{1,0:T(8,128)S(1)}, f32[64,64]{1,0:T(8,128)S(1)}, u32[]{:S(2)}, u32[]{:S(2)}) collective-permute-start(f32[64,64]{1,0:T(8,128)S(1)} %add.231), channel_id=1, source_target_pairs={{0,128},{32,160},{64,192},{96,224},{128,0},{160,32},{192,64},{224,... | collective-permute-start | bytes 49160 | tf_op jit(solution)/shard_map/ppermute | solution.py:73
  89.2 10.1 %collective-permute-start.7 = (f32[64,64]{1,0:T(8,128)S(1)}, f32[64,64]{1,0:T(8,128)S(1)}, u32[]{:S(2)}, u32[]{:S(2)}) collective-permute-start(f32[64,64]{1,0:T(8,128)S(1)} %add.232), channel_id=1, source_target_pairs={{0,256},{32,288},{64,320},{96,352},{128,384},{160,416},{192,448},{... | collective-permute-start | bytes 49160 | tf_op jit(solution)/shard_map/ppermute | solution.py:73
  99.3 5.8 %collective-permute-start.8 = (f32[64,64]{1,0:T(8,128)S(1)}, f32[64,64]{1,0:T(8,128)S(1)}, u32[]{:S(2)}, u32[]{:S(2)}) collective-permute-start(f32[64,64]{1,0:T(8,128)S(1)} %add.233), channel_id=1, source_target_pairs={{0,1},{1,0},{2,3},{3,2},{4,5},{5,4},{6,7},{7,6},{8,9},{9,8},{10,11... | collective-permute-start | bytes 49160 | tf_op jit(solution)/shard_map/ppermute | solution.py:73
  105.1 6.7 %collective-permute-start.9 = (f32[64,64]{1,0:T(8,128)S(1)}, f32[64,64]{1,0:T(8,128)S(1)}, u32[]{:S(2)}, u32[]{:S(2)}) collective-permute-start(f32[64,64]{1,0:T(8,128)S(1)} %add.234), channel_id=1, source_target_pairs={{0,2},{1,3},{2,0},{3,1},{4,6},{5,7},{6,4},{7,5},{8,10},{9,11},{10,... | collective-permute-start | bytes 49160 | tf_op jit(solution)/shard_map/ppermute | solution.py:73
  111.8 9.8 %collective-permute-start.10 = (f32[64,64]{1,0:T(8,128)S(1)}, f32[64,64]{1,0:T(8,128)S(1)}, u32[]{:S(2)}, u32[]{:S(2)}) collective-permute-start(f32[64,64]{1,0:T(8,128)S(1)} %add.235), channel_id=1, source_target_pairs={{0,4},{1,5},{2,6},{3,7},{4,0},{5,1},{6,2},{7,3},{8,12},{9,13},{10,... | collective-permute-start | bytes 49160 | tf_op jit(solution)/shard_map/ppermute | solution.py:73
  121.6 5.8 %collective-permute-start.11 = (f32[64,64]{1,0:T(8,128)S(1)}, f32[64,64]{1,0:T(8,128)S(1)}, u32[]{:S(2)}, u32[]{:S(2)}) collective-permute-start(f32[64,64]{1,0:T(8,128)S(1)} %add.236), channel_id=1, source_target_pairs={{0,8},{1,9},{2,10},{3,11},{4,12},{5,13},{6,14},{7,15},{8,0},{9,1},... | collective-permute-start | bytes 49160 | tf_op jit(solution)/shard_map/ppermute | solution.py:73
  127.4 7.3 %collective-permute-start.12 = (f32[64,64]{1,0:T(8,128)S(1)}, f32[64,64]{1,0:T(8,128)S(1)}, u32[]{:S(2)}, u32[]{:S(2)}) collective-permute-start(f32[64,64]{1,0:T(8,128)S(1)} %add.237), channel_id=1, source_target_pairs={{0,16},{1,17},{2,18},{3,19},{4,20},{5,21},{6,22},{7,23},{8,24},{9,... | collective-permute-start | bytes 49160 | tf_op jit(solution)/shard_map/ppermute | solution.py:73

commit v2 on v1

--- a/solution.py
+++ b/solution.py
@@ -85,12 +85,12 @@
     coef = coefficients.reshape(5, rows_x, rows_y, NZ)
 
     guess_e, rhs_e, coef_e = exchange(
-        [(guess, depth), (rhs_field, depth - 1), (coef, depth - 1)],
+        [(guess, depth), (rhs_field, depth - 1), (coef, depth)],
         "gx",
         lambda a: 0 if a.ndim == 3 else 1,
     )
     guess_e, rhs_e, coef_e = exchange(
-        [(guess_e, depth), (rhs_e, depth - 1), (coef_e, depth - 1)],
+        [(guess_e, depth), (rhs_e, depth - 1), (coef_e, depth)],
         "gy",
         lambda a: 1 if a.ndim == 3 else 2,
     )
@@ -99,10 +99,10 @@
     wide = jnp.dot(coef_e.reshape(5 * ex * ey, NZ), spread, precision=HIGH).reshape(5, ex, ey, width)
     coefs = [wide[i] for i in range(5)]
 
-    current = rhs_e - operate(guess_e, coefs)
+    current = rhs_e - operate(guess_e, crop(coefs, 1))
     krylov = [current]
     for step in range(STEPS):
-        inner = crop(coefs, step + 1)
+        inner = crop(coefs, step + 2)
         center = current[1:-1, 1:-1]
         current = (operate(current, inner) - SHIFT * center) / SCALE
         krylov.append(current)
@@ -114,12 +114,18 @@
         local.append(block)
 
     blocks = len(local)
-    groups = 128 // RHS
-    stacked = jnp.concatenate([v.reshape(-1, 128) for v in local], axis=1)
+    lanes = 128
+    stacked = jnp.concatenate([v.reshape(-1, lanes) for v in local], axis=1)
+    cols = blocks * lanes
+    col = jnp.arange(cols)
+    same_z = ((col[:, None] % lanes) // RHS) == ((col[None, :] % lanes) // RHS)
+    gather = (
+        (col[:, None] // lanes == jnp.arange(blocks * RHS)[None, :] // RHS)
+        & (col[:, None] % RHS == jnp.arange(blocks * RHS)[None, :] % RHS)
+    ).astype(jnp.float32)
     products = jnp.dot(stacked.T, stacked, precision=HIGH)
-    products = products.reshape(blocks, groups, RHS, blocks, groups, RHS)
-    diagonal = jnp.eye(groups, dtype=jnp.float32)[None, :, None, None, :, None]
-    local_gram = jnp.sum(products * diagonal, axis=(1, 4)).reshape(blocks * RHS, blocks * RHS)
+    products = jnp.where(same_z, products, 0.0)
+    local_gram = jnp.dot(gather.T, jnp.dot(products, gather, precision=HIGH), precision=HIGH)
     gram = allreduce(local_gram, ("gx", "gy"))
     shift_map = SHIFT * jnp.eye(blocks * RHS, STEPS * RHS, dtype=jnp.float32) + SCALE * jnp.eye(
         blocks * RHS, STEPS * RHS, k=-RHS, dtype=jnp.float32
@@ -134,20 +140,18 @@
     weights = jax.scipy.linalg.cho_solve((factor, True), target)
     padded = jnp.concatenate([weights, jnp.zeros((RHS, RHS), jnp.float32)], axis=0)
     applied = jnp.dot(shift_map, weights, precision=HIGH)
-    eye_g = jnp.eye(groups, dtype=jnp.float32)
-    mix = jnp.concatenate(
-        [
-            jnp.concatenate(
-                [jnp.kron(eye_g, padded[j * RHS : (j + 1) * RHS]), jnp.kron(eye_g, applied[j * RHS : (j + 1) * RHS])],
-                axis=1,
-            )
-            for j in range(blocks)
-        ],
-        axis=0,
-    )
+    both = jnp.concatenate([padded, applied], axis=1)
+    out_col = jnp.arange(2 * lanes)
+    spread_out = (
+        (out_col[:, None] // lanes == jnp.arange(2 * RHS)[None, :] // RHS)
+        & (out_col[:, None] % RHS == jnp.arange(2 * RHS)[None, :] % RHS)
+    ).astype(jnp.float32)
+    out_z = ((col[:, None] % lanes) // RHS) == ((out_col[None, :] % lanes) // RHS)
+    mix = jnp.dot(jnp.dot(gather, both, precision=HIGH), spread_out.T, precision=HIGH)
+    mix = jnp.where(out_z, mix, 0.0)
     updates = jnp.dot(stacked, mix, precision=HIGH)
-    solution = guess.reshape(-1, 128) + updates[:, :128]
-    residual = local[0].reshape(-1, 128) - updates[:, 128:]
+    solution = guess.reshape(-1, lanes) + updates[:, :lanes]
+    residual = local[0].reshape(-1, lanes) - updates[:, lanes:]
     return (
         solution.reshape(rows_x, rows_y * NZ * RHS),
         residual.reshape(rows_x, rows_y * NZ * RHS),

time: 157 us -> 140 us (0.89)
  local copies, waits for them, and re-layouts: 35.8 us -> 20.3 us
  other arithmetic: 22.3 us -> 17.8 us
  matrix products: 6.94 us -> 10.1 us
    mul x7 -> x0, local copies, waits for them, and re-layouts: 5.48 us -> none  [the longest x4 2.83 us: per_device(): jnp.kron(eye_g, applied[j * RHS:(j + 1) * RHS])]
    reduce_sum x1 -> x0, other arithmetic: 4.78 us -> none  [per_device(): jnp.sum(products * diagonal, axis=(1, 4))]
    reshape x7 -> x4, local copies, waits for them, and re-layouts: 6.3 us -> 1.98 us  [per_device(): stacked = jnp.concatenate([v.reshape(-1, lanes) for v in local], axis=1)]
    dot_general x0 -> x4, matrix products: none -> 2.4 us  [the longest x1 0.74 us: per_device(): jnp.dot(products, gather, precision=HIGH)]
    squeeze x5 -> x0, local copies, waits for them, and re-layouts: 2.3 us -> none  [per_device(): coefs = [wide[i] for i in range(5)]]
    mul x1 -> x0, other arithmetic: 1.62 us -> none  [per_device(): jnp.kron(eye_g, padded[j * RHS:(j + 1) * RHS])]
    unnamed x29 -> x33, local copies, waits for them, and re-layouts: 3.33 us -> 1.71 us
  transfers between devices with their start and end apart: 13 -> 13, of which waited for: 12 -> 12; matrix products, arithmetic and copies ran while one was open for 0% -> 1% of each run, Pallas kernels for 0% -> 0%
where the time goes in v2:
time: 140 us; the launch traced here: 139 us
  starting transfers between devices  57.4 us (41%)
  waiting for transfers between devices  31.8 us (23%)
  local copies, waits for them, and re-layouts  20.3 us (14%)
  other arithmetic  17.8 us (13%)
  matrix products  10.1 us (7%)
  between operations  1.47 us (1%)
    ppermute x9, starting transfers between devices, allreduce(): x = x + lax.ppermute(x, axis, [(i, i ^ bit) for i in range(count)])  41 us
    ppermute x9, waiting for transfers between devices, allreduce(): x = x + lax.ppermute(x, axis, [(i, i ^ bit) for i in range(count)])  25.6 us
    ppermute x2, starting transfers between devices, exchange(): high = lax.ppermute(jnp.concatenate(downs), axis, backward)  10.3 us
    ppermute x2, starting transfers between devices, exchange(): low = lax.ppermute(jnp.concatenate(ups), axis, forward)  6.02 us
    another operation x3, other arithmetic, per_device(): factor = jnp.linalg.cholesky(normal)  5.05 us
    ppermute x2, waiting for transfers between devices, exchange(): high = lax.ppermute(jnp.concatenate(downs), axis, backward)  4.67 us
    another operation x2, other arithmetic, per_device(): weights = jax.scipy.linalg.cho_solve((factor, True), target)  4.32 us
    dot_general x1, matrix products, per_device(): jnp.dot(coef_e.reshape(5 * ex * ey, NZ), spread, precision=HIGH)  3.35 us
  transfers between devices with their start and end apart: 13, of which 12 were waited for; matrix products, arithmetic and copies ran while one was open for 1% of the time, Pallas kernels for 0%

profile of v2, /device:TPU:6, one launch (start us, length us, event | category | flops | bytes accessed | tf_op | source)
XLA Modules:
  0.0 138.9 jit_solution(17753863897144125958)
XLA Ops:
  0.6 1.0 reshape.512
  1.8 1.1 slice_bitcast_fusion.2
  2.9 1.1 fusion.119
  4.1 1.8 %collective-permute-start = (f32[67584]{0:T(1024)S(1)}, f32[67584]{0:T(1024)S(1)}, u32[]{:S(2)}, u32[]{:S(2)}) collective-permute-start(f32[67584]{0:T(1024)S(1)} %pad_maximum_fusion.2), channel_id=1, source_target_pairs={{0,32},{32,64},{64,96},{96,128},{128,160},{160,192},{192,224},{224... | collective-permute-start | bytes 811016 | tf_op jit(solution)/shard_map/ppermute | solution.py:29
  6.1 1.3 collective-permute-start.1
  7.6 3.3 %collective-permute-done.1 = f32[67584]{0:T(1024)S(1)} collective-permute-done((f32[67584]{0:T(1024)S(1)}, f32[67584]{0:T(1024)S(1)}, u32[]{:S(2)}, u32[]{:S(2)}) %collective-permute-start.1) | collective-permute-done | bytes 270368 | tf_op jit(solution)/shard_map/ppermute | solution.py:30
  12.8 4.3 %collective-permute-start.2 = (f32[64512]{0:T(1024)}, f32[64512]{0:T(1024)S(1)}, u32[]{:S(2)}, u32[]{:S(2)}) collective-permute-start(f32[64512]{0:T(1024)} %pad_maximum_fusion.4), channel_id=1, source_target_pairs={{0,1},{1,2},{2,3},{3,4},{4,5},{5,6},{6,7},{7,8},{8,9},{9,10},{10,1... | collective-permute-start | bytes 774152 | tf_op jit(solution)/shard_map/ppermute | solution.py:29
  17.3 9.0 %collective-permute-start.3 = (f32[64512]{0:T(1024)S(1)}, f32[64512]{0:T(1024)S(1)}, u32[]{:S(2)}, u32[]{:S(2)}) collective-permute-start(f32[64512]{0:T(1024)S(1)} %pad_maximum_fusion.5), channel_id=1, source_target_pairs={{1,0},{2,1},{3,2},{4,3},{5,4},{6,5},{7,6},{8,7},{9,8},{10,9},{11,1... | collective-permute-start | bytes 774152 | tf_op jit(solution)/shard_map/ppermute | solution.py:30
  26.9 1.5 %collective-permute-done.2 = f32[64512]{0:T(1024)S(1)} collective-permute-done((f32[64512]{0:T(1024)}, f32[64512]{0:T(1024)S(1)}, u32[]{:S(2)}, u32[]{:S(2)}) %collective-permute-start.2) | collective-permute-done | bytes 258080 | tf_op jit(solution)/shard_map/ppermute | solution.py:29
  28.6 1.4 collective-permute-done.3
  30.4 3.4 %fusion.120 = f32[1920,512]{1,0:T(8,128)S(1)} fusion(f32[1920,32]{1,0:T(8,128)S(1)} %bitcast.70, f32[32,512]{0,1:T(8,128)S(1)} %bitcast.72), kind=kOutput, calls=%fused_computation.210 | convolution fusion | flops 377487360 | bytes 4243456 | tf_op jit(solution)/shard_map/dot_general | solution.py:99
  33.7 1.7 %fusion.111 = (f32[384,512]{1,0:T(8,128)S(1)}, f32[384,512]{1,0:T(8,128)S(1)}, f32[384,512]{1,0:T(8,128)S(1)}, f32[384,512]{1,0:T(8,128)}, f32[384,512]{1,0:T(8,128)}) fusion(f32[1920,512]{1,0:T(8,128)S(1)} %fusion.120), kind=kLoop, calls=%fused_computation.201 | loop fusion | bytes 7864320 | tf_op jit(solution)/shard_map/slice | solution.py:100
  36.2 1.2 pad_maximum_fusion.1
  37.4 1.4 fusion.112
  38.8 1.5 %slice.394 = f32[21504]{0:T(1024)} slice(f32[64512]{0:T(1024)} %copy-done.6), slice={[32768:54272]} | slice | bytes 172032 | tf_op jit(solution)/shard_map/slice | solution.py:38
  40.3 0.9 reshape.528
  41.2 1.5 %slice.398 = f32[21504]{0:T(1024)} slice(f32[64512]{0:T(1024)} %copy-done.7), slice={[32768:54272]} | slice | bytes 172032 | tf_op jit(solution)/shard_map/slice | solution.py:39
  42.7 1.6 %reshape.532 = f32[14,3,512]{2,1,0:T(4,128)} reshape(f32[21504]{0:T(1024)} %slice.398) | data formatting | bytes 172032 | tf_op jit(solution)/shard_map/reshape | solution.py:39
  44.3 3.2 %fusion.3 = f32[14,22,512]{2,1,0:T(8,128)S(1)} fusion(f32[16,24,512]{2,1,0:T(8,128)S(1)} %bitcast.54, f32[16,24,512]{2,1,0:T(8,128)S(1)} %bitcast.58, f32[16,24,512]{2,1,0:T(8,128)} %bitcast.62, f32[16,24,512]{2,1,0:T(8,128)S(1)} %pad_maximum_fusion.1, f32[16,24,512]{2,1,0:T(8,128)} %bitcast.66, f32[14,3,512]{2,1,0:T(4,128)} %reshape.532, ...), kind=kLoop, calls=%fused_computation.8 | loop fusion | flops 3627008 | bytes 8791552 | tf_op jit(solution)/shard_map/sub | solution.py:102
  47.8 1.0 fusion.10
  50.6 0.8 fusion.18
  52.0 1.0 reshape.540
  53.0 1.0 reshape.539
  54.1 1.9 %convolution_select_fusion = f32[512,512]{1,0:T(8,128)S(1)} fusion(f32[512,512]{1,0:T(8,128)S(1)} %constant_dynamic-update-slice_fusion.7, s32[512]{0:T(512)S(1)} %add_select_fusion.2), kind=kOutput, calls=%fused_computation | convolution fusion | flops 1611137024 | bytes 2099200 | tf_op jit(solution)/shard_map/dot_general | solution.py:126
  56.0 0.7 fusion.32
  57.5 5.9 %collective-permute-start.4 = (f32[64,64]{0,1:T(8,128)S(1)}, f32[64,64]{0,1:T(8,128)S(1)}, u32[]{:S(2)}, u32[]{:S(2)}) collective-permute-start(f32[64,64]{0,1:T(8,128)S(1)} %fusion.31), channel_id=1, source_target_pairs={{0,32},{32,0},{64,96},{96,64},{128,160},{160,128},{192,224},{224,1... | collective-permute-start | bytes 49160 | tf_op jit(solution)/shard_map/ppermute | solution.py:73
  63.4 0.8 collective-permute-done.4
  64.2 5.3 %collective-permute-start.5 = (f32[64,64]{0,1:T(8,128)S(1)}, f32[64,64]{0,1:T(8,128)S(1)}, u32[]{:S(2)}, u32[]{:S(2)}) collective-permute-start(f32[64,64]{0,1:T(8,128)S(1)} %add.363), channel_id=1, source_target_pairs={{0,64},{32,96},{64,0},{96,32},{128,192},{160,224},{192,128},{224,1... | collective-permute-start | bytes 49160 | tf_op jit(solution)/shard_map/ppermute | solution.py:73
  69.6 1.9 %collective-permute-done.5 = f32[64,64]{0,1:T(8,128)S(1)} collective-permute-done((f32[64,64]{0,1:T(8,128)S(1)}, f32[64,64]{0,1:T(8,128)S(1)}, u32[]{:S(2)}, u32[]{:S(2)}) %collective-permute-start.5) | collective-permute-done | bytes 16416 | tf_op jit(solution)/shard_map/ppermute | solution.py:73
  71.5 5.0 %collective-permute-start.6 = (f32[64,64]{0,1:T(8,128)S(1)}, f32[64,64]{0,1:T(8,128)S(1)}, u32[]{:S(2)}, u32[]{:S(2)}) collective-permute-start(f32[64,64]{0,1:T(8,128)S(1)} %add.364), channel_id=1, source_target_pairs={{0,128},{32,160},{64,192},{96,224},{128,0},{160,32},{192,64},{224,... | collective-permute-start | bytes 49160 | tf_op jit(solution)/shard_map/ppermute | solution.py:73
  76.5 2.2 %collective-permute-done.6 = f32[64,64]{0,1:T(8,128)S(1)} collective-permute-done((f32[64,64]{0,1:T(8,128)S(1)}, f32[64,64]{0,1:T(8,128)S(1)}, u32[]{:S(2)}, u32[]{:S(2)}) %collective-permute-start.6) | collective-permute-done | bytes 16416 | tf_op jit(solution)/shard_map/ppermute | solution.py:73
  78.7 8.2 %collective-permute-start.7 = (f32[64,64]{0,1:T(8,128)S(1)}, f32[64,64]{0,1:T(8,128)S(1)}, u32[]{:S(2)}, u32[]{:S(2)}) collective-permute-start(f32[64,64]{0,1:T(8,128)S(1)} %add.365), channel_id=1, source_target_pairs={{0,256},{32,288},{64,320},{96,352},{128,384},{160,416},{192,448},{... | collective-permute-start | bytes 49160 | tf_op jit(solution)/shard_map/ppermute | solution.py:73
  86.9 2.0 %collective-permute-done.7 = f32[64,64]{0,1:T(8,128)S(1)} collective-permute-done((f32[64,64]{0,1:T(8,128)S(1)}, f32[64,64]{0,1:T(8,128)S(1)}, u32[]{:S(2)}, u32[]{:S(2)}) %collective-permute-start.7) | collective-permute-done | bytes 16416 | tf_op jit(solution)/shard_map/ppermute | solution.py:73
  88.9 1.9 %collective-permute-start.8 = (f32[64,64]{0,1:T(8,128)S(1)}, f32[64,64]{0,1:T(8,128)S(1)}, u32[]{:S(2)}, u32[]{:S(2)}) collective-permute-start(f32[64,64]{0,1:T(8,128)S(1)} %add.366), channel_id=1, source_target_pairs={{0,1},{1,0},{2,3},{3,2},{4,5},{5,4},{6,7},{7,6},{8,9},{9,8},{10,11... | collective-permute-start | bytes 49160 | tf_op jit(solution)/shard_map/ppermute | solution.py:73
  90.8 3.9 %collective-permute-done.8 = f32[64,64]{0,1:T(8,128)S(1)} collective-permute-done((f32[64,64]{0,1:T(8,128)S(1)}, f32[64,64]{0,1:T(8,128)S(1)}, u32[]{:S(2)}, u32[]{:S(2)}) %collective-permute-start.8) | collective-permute-done | bytes 16416 | tf_op jit(solution)/shard_map/ppermute | solution.py:73
  94.7 4.1 %collective-permute-start.9 = (f32[64,64]{0,1:T(8,128)S(1)}, f32[64,64]{0,1:T(8,128)S(1)}, u32[]{:S(2)}, u32[]{:S(2)}) collective-permute-start(f32[64,64]{0,1:T(8,128)S(1)} %add.367), channel_id=1, source_target_pairs={{0,2},{1,3},{2,0},{3,1},{4,6},{5,7},{6,4},{7,5},{8,10},{9,11},{10,... | collective-permute-start | bytes 49160 | tf_op jit(solution)/shard_map/ppermute | solution.py:73
  98.8 2.6 %collective-permute-done.9 = f32[64,64]{0,1:T(8,128)S(1)} collective-permute-done((f32[64,64]{0,1:T(8,128)S(1)}, f32[64,64]{0,1:T(8,128)S(1)}, u32[]{:S(2)}, u32[]{:S(2)}) %collective-permute-start.9) | collective-permute-done | bytes 16416 | tf_op jit(solution)/shard_map/ppermute | solution.py:73
  101.4 5.3 %collective-permute-start.10 = (f32[64,64]{0,1:T(8,128)S(1)}, f32[64,64]{0,1:T(8,128)S(1)}, u32[]{:S(2)}, u32[]{:S(2)}) collective-permute-start(f32[64,64]{0,1:T(8,128)S(1)} %add.368), channel_id=1, source_target_pairs={{0,4},{1,5},{2,6},{3,7},{4,0},{5,1},{6,2},{7,3},{8,12},{9,13},{10,... | collective-permute-start | bytes 49160 | tf_op jit(solution)/shard_map/ppermute | solution.py:73
  106.7 4.5 %collective-permute-done.10 = f32[64,64]{0,1:T(8,128)S(1)} collective-permute-done((f32[64,64]{0,1:T(8,128)S(1)}, f32[64,64]{0,1:T(8,128)S(1)}, u32[]{:S(2)}, u32[]{:S(2)}) %collective-permute-start.10) | collective-permute-done | bytes 16416 | tf_op jit(solution)/shard_map/ppermute | solution.py:73
  111.2 2.3 %collective-permute-start.11 = (f32[64,64]{0,1:T(8,128)S(1)}, f32[64,64]{0,1:T(8,128)S(1)}, u32[]{:S(2)}, u32[]{:S(2)}) collective-permute-start(f32[64,64]{0,1:T(8,128)S(1)} %add.369), channel_id=1, source_target_pairs={{0,8},{1,9},{2,10},{3,11},{4,12},{5,13},{6,14},{7,15},{8,0},{9,1},... | collective-permute-start | bytes 49160 | tf_op jit(solution)/shard_map/ppermute | solution.py:73
  113.6 3.4 %collective-permute-done.11 = f32[64,64]{0,1:T(8,128)S(1)} collective-permute-done((f32[64,64]{0,1:T(8,128)S(1)}, f32[64,64]{0,1:T(8,128)S(1)}, u32[]{:S(2)}, u32[]{:S(2)}) %collective-permute-start.11) | collective-permute-done | bytes 16416 | tf_op jit(solution)/shard_map/ppermute | solution.py:73
  117.0 2.9 %collective-permute-start.12 = (f32[64,64]{0,1:T(8,128)S(1)}, f32[64,64]{0,1:T(8,128)S(1)}, u32[]{:S(2)}, u32[]{:S(2)}) collective-permute-start(f32[64,64]{0,1:T(8,128)S(1)} %add.370), channel_id=1, source_target_pairs={{0,16},{1,17},{2,18},{3,19},{4,20},{5,21},{6,22},{7,23},{8,24},{9,... | collective-permute-start | bytes 49160 | tf_op jit(solution)/shard_map/ppermute | solution.py:73
  120.0 4.3 %collective-permute-done.12 = f32[64,64]{0,1:T(8,128)S(1)} collective-permute-done((f32[64,64]{0,1:T(8,128)S(1)}, f32[64,64]{0,1:T(8,128)S(1)}, u32[]{:S(2)}, u32[]{:S(2)}) %collective-permute-start.12) | collective-permute-done | bytes 16416 | tf_op jit(solution)/shard_map/ppermute | solution.py:73
  125.3 4.4 %cholesky.16 = f32[48,48]{1,0:T(8,128)S(1)} custom-call(f32[48,48]{1,0:T(8,128)S(1)} %fusion.61), custom_call_target="Cholesky" | custom-call | tf_op jit(solution)/shard_map/jit(cholesky)/cholesky | solution.py:139
  131.0 3.7 %custom-call.10 = f32[1,48,48]{1,2,0:T(8,128)S(1)} custom-call(f32[1,48,48]{2,1,0:T(8,128)S(1)} %fusion.56), custom_call_target="InvertDiagBlocksLowerTriangular" | custom-call | tf_op jit(solution)/shard_map/jit(_cho_solve)/triangular_solve | solution.py:140
  136.3 1.0 fusion.121
  137.4 0.8 reshape.543
  138.1 0.8 reshape.544
  (115 shorter events, 11.7 us)
Async XLA Ops:
  1.7 9.6 %copy-start.2 = (f32[8,8192]{1,0:T(8,128)S(1)}, f32[8,8192]{1,0:T(8,128)}, u32[]{:S(2)}) copy-start(f32[8,8192]{1,0:T(8,128)} %param.4) | copy-start | bytes 786436
  4.1 3.3 %collective-permute-start = (f32[67584]{0:T(1024)S(1)}, f32[67584]{0:T(1024)S(1)}, u32[]{:S(2)}, u32[]{:S(2)}) collective-permute-start(f32[67584]{0:T(1024)S(1)} %pad_maximum_fusion.2), channel_id=1, source_target_pairs={{0,32},{32,64},{64,96},{96,128},{128,160},{160,192},{192,224},{224... | collective-permute-start | bytes 811016 | tf_op jit(solution)/shard_map/ppermute | solution.py:29
  5.8 5.9 %copy-start.5 = (f32[8,8192]{1,0:T(8,128)S(1)}, f32[8,8192]{1,0:T(8,128)}, u32[]{:S(2)}) copy-start(f32[8,8192]{1,0:T(8,128)} %param.3) | copy-start | bytes 786436
  6.1 4.8 %collective-permute-start.1 = (f32[67584]{0:T(1024)S(1)}, f32[67584]{0:T(1024)S(1)}, u32[]{:S(2)}, u32[]{:S(2)}) collective-permute-start(f32[67584]{0:T(1024)S(1)} %pad_maximum_fusion.3), channel_id=1, source_target_pairs={{32,0},{64,32},{96,64},{128,96},{160,128},{192,160},{224,192},{256... | collective-permute-start | bytes 811016 | tf_op jit(solution)/shard_map/ppermute | solution.py:30
  11.5 18.8 %copy-start.3 = (f32[16,16,512]{2,1,0:T(8,128)}, f32[16,16,512]{2,1,0:T(8,128)S(1)}, u32[]{:S(2)}) copy-start(f32[16,16,512]{2,1,0:T(8,128)S(1)} %constant_dynamic-update-slice_fusion) | copy-start | bytes 1572868
  11.9 18.4 %copy-start.4 = (f32[14,16,512]{2,1,0:T(8,128)}, f32[14,16,512]{2,1,0:T(8,128)S(1)}, u32[]{:S(2)}) copy-start(f32[14,16,512]{2,1,0:T(8,128)S(1)} %constant_dynamic-update-slice_fusion.2) | copy-start | bytes 1376260
  12.8 15.7 %collective-permute-start.2 = (f32[64512]{0:T(1024)}, f32[64512]{0:T(1024)S(1)}, u32[]{:S(2)}, u32[]{:S(2)}) collective-permute-start(f32[64512]{0:T(1024)} %pad_maximum_fusion.4), channel_id=1, source_target_pairs={{0,1},{1,2},{2,3},{3,4},{4,5},{5,6},{6,7},{7,8},{8,9},{9,10},{10,1... | collective-permute-start | bytes 774152 | tf_op jit(solution)/shard_map/ppermute | solution.py:29
  17.3 12.7 %collective-permute-start.3 = (f32[64512]{0:T(1024)S(1)}, f32[64512]{0:T(1024)S(1)}, u32[]{:S(2)}, u32[]{:S(2)}) collective-permute-start(f32[64512]{0:T(1024)S(1)} %pad_maximum_fusion.5), channel_id=1, source_target_pairs={{1,0},{2,1},{3,2},{4,3},{5,4},{6,5},{7,6},{8,7},{9,8},{10,9},{11,1... | collective-permute-start | bytes 774152 | tf_op jit(solution)/shard_map/ppermute | solution.py:30
  28.5 6.9 %copy-start.6 = (f32[64512]{0:T(1024)}, f32[64512]{0:T(1024)S(1)}, u32[]{:S(2)}) copy-start(f32[64512]{0:T(1024)S(1)} %collective-permute-done.2) | copy-start | bytes 774148
  30.0 5.5 %copy-start.7 = (f32[64512]{0:T(1024)}, f32[64512]{0:T(1024)S(1)}, u32[]{:S(2)}) copy-start(f32[64512]{0:T(1024)S(1)} %collective-permute-done.3) | copy-start | bytes 774148
  44.3 3.5 %copy-start = (f32[384,512]{1,0:T(8,128)S(1)}, f32[384,512]{1,0:T(8,128)}, u32[]{:S(2)}) copy-start(f32[384,512]{1,0:T(8,128)} %get-tuple-element.5) | copy-start | bytes 2359300
  44.3 3.5 %copy-start.1 = (f32[384,512]{1,0:T(8,128)S(1)}, f32[384,512]{1,0:T(8,128)}, u32[]{:S(2)}) copy-start(f32[384,512]{1,0:T(8,128)} %get-tuple-element.6) | copy-start | bytes 2359300
  52.0 4.0 %copy-start.8 = (s32[64]{0:T(128)S(1)}, s32[64]{0:T(128)}, u32[]{:S(2)}) copy-start(s32[64]{0:T(128)} %get-tuple-element.34) | copy-start | bytes 772
  57.5 6.7 %collective-permute-start.4 = (f32[64,64]{0,1:T(8,128)S(1)}, f32[64,64]{0,1:T(8,128)S(1)}, u32[]{:S(2)}, u32[]{:S(2)}) collective-permute-start(f32[64,64]{0,1:T(8,128)S(1)} %fusion.31), channel_id=1, source_target_pairs={{0,32},{32,0},{64,96},{96,64},{128,160},{160,128},{192,224},{224,1... | collective-permute-start | bytes 49160 | tf_op jit(solution)/shard_map/ppermute | solution.py:73
  64.2 7.2 %collective-permute-start.5 = (f32[64,64]{0,1:T(8,128)S(1)}, f32[64,64]{0,1:T(8,128)S(1)}, u32[]{:S(2)}, u32[]{:S(2)}) collective-permute-start(f32[64,64]{0,1:T(8,128)S(1)} %add.363), channel_id=1, source_target_pairs={{0,64},{32,96},{64,0},{96,32},{128,192},{160,224},{192,128},{224,1... | collective-permute-start | bytes 49160 | tf_op jit(solution)/shard_map/ppermute | solution.py:73
  71.5 7.2 %collective-permute-start.6 = (f32[64,64]{0,1:T(8,128)S(1)}, f32[64,64]{0,1:T(8,128)S(1)}, u32[]{:S(2)}, u32[]{:S(2)}) collective-permute-start(f32[64,64]{0,1:T(8,128)S(1)} %add.364), channel_id=1, source_target_pairs={{0,128},{32,160},{64,192},{96,224},{128,0},{160,32},{192,64},{224,... | collective-permute-start | bytes 49160 | tf_op jit(solution)/shard_map/ppermute | solution.py:73
  78.7 10.2 %collective-permute-start.7 = (f32[64,64]{0,1:T(8,128)S(1)}, f32[64,64]{0,1:T(8,128)S(1)}, u32[]{:S(2)}, u32[]{:S(2)}) collective-permute-start(f32[64,64]{0,1:T(8,128)S(1)} %add.365), channel_id=1, source_target_pairs={{0,256},{32,288},{64,320},{96,352},{128,384},{160,416},{192,448},{... | collective-permute-start | bytes 49160 | tf_op jit(solution)/shard_map/ppermute | solution.py:73
  88.9 5.8 %collective-permute-start.8 = (f32[64,64]{0,1:T(8,128)S(1)}, f32[64,64]{0,1:T(8,128)S(1)}, u32[]{:S(2)}, u32[]{:S(2)}) collective-permute-start(f32[64,64]{0,1:T(8,128)S(1)} %add.366), channel_id=1, source_target_pairs={{0,1},{1,0},{2,3},{3,2},{4,5},{5,4},{6,7},{7,6},{8,9},{9,8},{10,11... | collective-permute-start | bytes 49160 | tf_op jit(solution)/shard_map/ppermute | solution.py:73
  94.7 6.7 %collective-permute-start.9 = (f32[64,64]{0,1:T(8,128)S(1)}, f32[64,64]{0,1:T(8,128)S(1)}, u32[]{:S(2)}, u32[]{:S(2)}) collective-permute-start(f32[64,64]{0,1:T(8,128)S(1)} %add.367), channel_id=1, source_target_pairs={{0,2},{1,3},{2,0},{3,1},{4,6},{5,7},{6,4},{7,5},{8,10},{9,11},{10,... | collective-permute-start | bytes 49160 | tf_op jit(solution)/shard_map/ppermute | solution.py:73
  101.4 9.8 %collective-permute-start.10 = (f32[64,64]{0,1:T(8,128)S(1)}, f32[64,64]{0,1:T(8,128)S(1)}, u32[]{:S(2)}, u32[]{:S(2)}) collective-permute-start(f32[64,64]{0,1:T(8,128)S(1)} %add.368), channel_id=1, source_target_pairs={{0,4},{1,5},{2,6},{3,7},{4,0},{5,1},{6,2},{7,3},{8,12},{9,13},{10,... | collective-permute-start | bytes 49160 | tf_op jit(solution)/shard_map/ppermute | solution.py:73
  111.2 5.8 %collective-permute-start.11 = (f32[64,64]{0,1:T(8,128)S(1)}, f32[64,64]{0,1:T(8,128)S(1)}, u32[]{:S(2)}, u32[]{:S(2)}) collective-permute-start(f32[64,64]{0,1:T(8,128)S(1)} %add.369), channel_id=1, source_target_pairs={{0,8},{1,9},{2,10},{3,11},{4,12},{5,13},{6,14},{7,15},{8,0},{9,1},... | collective-permute-start | bytes 49160 | tf_op jit(solution)/shard_map/ppermute | solution.py:73
  117.0 7.3 %collective-permute-start.12 = (f32[64,64]{0,1:T(8,128)S(1)}, f32[64,64]{0,1:T(8,128)S(1)}, u32[]{:S(2)}, u32[]{:S(2)}) collective-permute-start(f32[64,64]{0,1:T(8,128)S(1)} %add.370), channel_id=1, source_target_pairs={{0,16},{1,17},{2,18},{3,19},{4,20},{5,21},{6,22},{7,23},{8,24},{9,... | collective-permute-start | bytes 49160 | tf_op jit(solution)/shard_map/ppermute | solution.py:73

commit v3 on v2

--- a/solution.py
+++ b/solution.py
@@ -14,32 +14,15 @@
 HIGH = lax.Precision.HIGHEST
 
 
-def exchange(arrays, axis, dim_of):
+def exchange(block, axis, dim, width):
     count = lax.axis_size(axis)
     forward = [(i, i + 1) for i in range(count - 1)]
     backward = [(i + 1, i) for i in range(count - 1)]
-    ups, downs, shapes = [], [], []
-    for block, width in arrays:
-        dim = dim_of(block)
-        top = lax.slice_in_dim(block, block.shape[dim] - width, None, axis=dim)
-        bottom = lax.slice_in_dim(block, 0, width, axis=dim)
-        ups.append(top.reshape(-1))
-        downs.append(bottom.reshape(-1))
-        shapes.append(top.shape)
-    low = lax.ppermute(jnp.concatenate(ups), axis, forward)
-    high = lax.ppermute(jnp.concatenate(downs), axis, backward)
-    out = []
-    offset = 0
-    for (block, width), shape in zip(arrays, shapes):
-        size = 1
-        for s in shape:
-            size *= s
-        dim = dim_of(block)
-        lo = low[offset : offset + size].reshape(shape)
-        hi = high[offset : offset + size].reshape(shape)
-        offset += size
-        out.append(jnp.concatenate([lo, block, hi], axis=dim))
-    return out
+    top = lax.slice_in_dim(block, block.shape[dim] - width, None, axis=dim)
+    bottom = lax.slice_in_dim(block, 0, width, axis=dim)
+    low = lax.ppermute(top, axis, forward)
+    high = lax.ppermute(bottom, axis, backward)
+    return jnp.concatenate([low, block, high], axis=dim)
 
 
 def operate(padded, coefs):
@@ -82,22 +65,19 @@
     depth = STEPS + 1
     rhs_field = right_side.reshape(rows_x, rows_y, width)
     guess = initial_guess.reshape(rows_x, rows_y, width)
-    coef = coefficients.reshape(5, rows_x, rows_y, NZ)
-
-    guess_e, rhs_e, coef_e = exchange(
-        [(guess, depth), (rhs_field, depth - 1), (coef, depth)],
-        "gx",
-        lambda a: 0 if a.ndim == 3 else 1,
+    coef = jnp.transpose(coefficients.reshape(5, rows_x, rows_y, NZ), (1, 2, 0, 3)).reshape(
+        rows_x, rows_y, 5 * NZ
     )
-    guess_e, rhs_e, coef_e = exchange(
-        [(guess_e, depth), (rhs_e, depth - 1), (coef_e, depth)],
-        "gy",
-        lambda a: 1 if a.ndim == 3 else 2,
-    )
-    ex, ey = coef_e.shape[1], coef_e.shape[2]
-    spread = jnp.repeat(jnp.eye(NZ, dtype=jnp.float32), RHS, axis=1)
-    wide = jnp.dot(coef_e.reshape(5 * ex * ey, NZ), spread, precision=HIGH).reshape(5, ex, ey, width)
-    coefs = [wide[i] for i in range(5)]
+    packed = jnp.concatenate([guess, rhs_field, coef], axis=2)
+    packed = exchange(packed, "gx", 0, depth)
+    packed = exchange(packed, "gy", 1, depth)
+    ex, ey = packed.shape[0], packed.shape[1]
+    guess_e = packed[:, :, :width]
+    rhs_e = packed[1:-1, 1:-1, width : 2 * width]
+    coef_e = packed[:, :, 2 * width :].reshape(ex * ey, 5 * NZ)
+    spread = jnp.kron(jnp.eye(5, dtype=jnp.float32), jnp.repeat(jnp.eye(NZ, dtype=jnp.float32), RHS, axis=1))
+    wide = jnp.dot(coef_e, spread, precision=HIGH).reshape(ex, ey, 5 * width)
+    coefs = [wide[:, :, i * width : (i + 1) * width] for i in range(5)]
 
     current = rhs_e - operate(guess_e, crop(coefs, 1))
     krylov = [current]

time: 140 us -> 127 us (0.907)
  local copies, waits for them, and re-layouts: 20.3 us -> 9.44 us
  starting transfers between devices: 57.4 us -> 59.6 us
  other arithmetic: 17.8 us -> 16 us
    slice x15 -> x0, local copies, waits for them, and re-layouts: 5.88 us -> none  [the longest x1 1.65 us: per_device(): coefs = [wide[i] for i in range(5)]]
    reshape x21 -> x3, local copies, waits for them, and re-layouts: 5.43 us -> 1.35 us  [the longest x2 1.22 us: per_device(): coefficients.reshape(5, rows_x, rows_y, NZ)]
    sub x1, other arithmetic: 3.23 us -> 1.14 us  [per_device(): current = rhs_e - operate(guess_e, crop(coefs, 1))]
    mul x0 -> x2, local copies, waits for them, and re-layouts: none -> 1.93 us  [per_device(): jnp.kron(jnp.eye(5, dtype=jnp.float32), jnp.repeat(jnp.eye(NZ, dtype=jnp....]
    reshape x4, local copies, waits for them, and re-layouts: 1.98 us -> 0.08 us  [per_device(): stacked = jnp.concatenate([v.reshape(-1, lanes) for v in local], axis=1)]
    ppermute x9, starting transfers between devices: 41 us -> 42.7 us  [allreduce(): x = x + lax.ppermute(x, axis, [(i, i ^ bit) for i in range(count)])]
    slice x2, local copies, waits for them, and re-layouts: 1.47 us -> 0.06 us  [per_device(): block = block[margin:-margin, margin:-margin]]
  transfers between devices with their start and end apart: 13 -> 13, of which waited for: 12 -> 12; matrix products, arithmetic and copies ran while one was open for 1% -> 2% of each run, Pallas kernels for 0% -> 0%
where the time goes in v3:
time: 127 us
  starting transfers between devices  59.6 us (47%)
  waiting for transfers between devices  30.5 us (24%)
  other arithmetic  16 us (13%)
  matrix products  10 us (8%)
  local copies, waits for them, and re-layouts  9.44 us (7%)
    ppermute x9, starting transfers between devices, allreduce(): x = x + lax.ppermute(x, axis, [(i, i ^ bit) for i in range(count)])  42.7 us
    ppermute x9, waiting for transfers between devices, allreduce(): x = x + lax.ppermute(x, axis, [(i, i ^ bit) for i in range(count)])  25.1 us
    ppermute x2, starting transfers between devices, exchange(): high = lax.ppermute(bottom, axis, backward)  10.1 us
    ppermute x2, starting transfers between devices, exchange(): low = lax.ppermute(top, axis, forward)  6.75 us
    another operation x3, other arithmetic, per_device(): factor = jnp.linalg.cholesky(normal)  5.05 us
    another operation x2, other arithmetic, per_device(): weights = jax.scipy.linalg.cho_solve((factor, True), target)  4.32 us
    dot_general x1, matrix products, per_device(): wide = jnp.dot(coef_e, spread, precision=HIGH).reshape(ex, ey, 5 * width)  3.46 us
    ppermute x2, waiting for transfers between devices, exchange(): low = lax.ppermute(top, axis, forward)  3.08 us
  transfers between devices with their start and end apart: 13, of which 12 were waited for; matrix products, arithmetic and copies ran while one was open for 2% of the time, Pallas kernels for 0%

profile of v3, /device:TPU:6, one launch (start us, length us, event | category | flops | bytes accessed | tf_op | source)
XLA Modules:
  0.0 126.7 jit_solution(5223566958953007862)
XLA Ops:
  0.6 1.2 bitcast_dynamic-update-slice_fusion.1
  1.8 1.0 reshape.425
  3.3 0.9 fusion.116
  4.2 2.5 %collective-permute-start = (f32[4,16,1184]{2,1,0:T(8,128)}, f32[4,16,1184]{2,1,0:T(8,128)}, u32[]{:S(2)}, u32[]{:S(2)}) collective-permute-start(f32[4,16,1184]{2,1,0:T(8,128)} %get-tuple-element.8), channel_id=1, source_target_pairs={{0,32},{32,64},{64,96},{96,128},{128,160},{160,192},{192,224},{224... | collective-permute-start | bytes 909320 | tf_op jit(solution)/shard_map/ppermute | solution.py:23
  6.7 1.3 %collective-permute-start.1 = (f32[4,16,1184]{2,1,0:T(8,128)}, f32[4,16,1184]{2,1,0:T(8,128)}, u32[]{:S(2)}, u32[]{:S(2)}) collective-permute-start(f32[4,16,1184]{2,1,0:T(8,128)} %get-tuple-element.9), channel_id=1, source_target_pairs={{32,0},{64,32},{96,64},{128,96},{160,128},{192,160},{224,192},{256... | collective-permute-start | bytes 909320 | tf_op jit(solution)/shard_map/ppermute | solution.py:24
  8.5 1.8 %reshape.433 = f32[160,2560,1]{1,0,2:T(8,128)} reshape(f32[5,32,5,512]{3,2,1,0:T(8,128)S(1)} %broadcast_multiply_fusion) | data formatting | bytes 3276800 | tf_op jit(solution)/shard_map/jit(kron)/mul | solution.py:78
  10.4 0.8 collective-permute-done.1
  11.2 1.3 %pad_maximum_fusion.3 = (f32[16,4,1184]{2,1,0:T(4,128)S(1)}, f32[16,4,1184]{2,1,0:T(4,128)S(1)}) fusion(f32[4,16,1184]{2,1,0:T(8,128)} %collective-permute-done.1, f32[8,16,1184]{2,1,0:T(8,128)S(1)} %constant_dynamic-update-slice_fusion, f32[4,16,1184]{2,1,0:T(8,128)} %collective-permute-done), kind=kLoop, calls=%fused_computation.44 | loop fusion | flops 303104 | bytes 1818624 | tf_op jit(solution)/shard_map/slice | solution.py:21
  12.5 4.3 %collective-permute-start.2 = (f32[16,4,1184]{2,1,0:T(4,128)S(1)}, f32[16,4,1184]{2,1,0:T(4,128)S(1)}, u32[]{:S(2)}, u32[]{:S(2)}) collective-permute-start(f32[16,4,1184]{2,1,0:T(4,128)S(1)} %get-tuple-element.4), channel_id=1, source_target_pairs={{0,1},{1,2},{2,3},{3,4},{4,5},{5,6},{6,7},{7,8},{8,9},{9,10},{10,1... | collective-permute-start | bytes 909320 | tf_op jit(solution)/shard_map/ppermute | solution.py:23
  16.7 8.9 %collective-permute-start.3 = (f32[16,4,1184]{2,1,0:T(4,128)S(1)}, f32[16,4,1184]{2,1,0:T(4,128)S(1)}, u32[]{:S(2)}, u32[]{:S(2)}) collective-permute-start(f32[16,4,1184]{2,1,0:T(4,128)S(1)} %get-tuple-element.5), channel_id=1, source_target_pairs={{1,0},{2,1},{3,2},{4,3},{5,4},{6,5},{7,6},{8,7},{9,8},{10,9},{11,1... | collective-permute-start | bytes 909320 | tf_op jit(solution)/shard_map/ppermute | solution.py:24
  25.6 3.1 %collective-permute-done.2 = f32[16,4,1184]{2,1,0:T(4,128)S(1)} collective-permute-done((f32[16,4,1184]{2,1,0:T(4,128)S(1)}, f32[16,4,1184]{2,1,0:T(4,128)S(1)}, u32[]{:S(2)}, u32[]{:S(2)}) %collective-permute-start.2) | collective-permute-done | bytes 303136 | tf_op jit(solution)/shard_map/ppermute | solution.py:23
  28.7 1.5 %collective-permute-done.3 = f32[16,4,1184]{2,1,0:T(4,128)S(1)} collective-permute-done((f32[16,4,1184]{2,1,0:T(4,128)S(1)}, f32[16,4,1184]{2,1,0:T(4,128)S(1)}, u32[]{:S(2)}, u32[]{:S(2)}) %collective-permute-start.3) | collective-permute-done | bytes 303136 | tf_op jit(solution)/shard_map/ppermute | solution.py:24
  30.2 1.4 %pad_maximum_fusion = f32[16,24,1184]{2,1,0:T(8,128)S(1)} fusion(f32[16,4,1184]{2,1,0:T(4,128)S(1)} %collective-permute-done.3, f32[4,16,1184]{2,1,0:T(8,128)} %collective-permute-done.1, f32[8,16,1184]{2,1,0:T(8,128)S(1)} %constant_dynamic-update-slice_fusion, f32[4,16,1184]{2,1,0:T(8,128)} %collective-permute-done, f32[16,4,1184]{2,1,0:T(4,128)S(1)} %collective-permute-done.2), kind=kLoop, calls=%fused_computation | loop fusion | flops 1818624 | bytes 3637248 | tf_op jit(solution)/shard_map/concatenate | solution.py:25
  31.9 1.1 copy-done
  33.0 3.5 %fusion.22 = f32[16,24,2560]{2,1,0:T(8,128)S(1)} fusion(f32[160,2560,1]{1,0,2:T(8,128)S(1)} %copy-done, f32[16,24,1184]{2,1,0:T(8,128)S(1)} %pad_maximum_fusion), kind=kOutput, calls=%fused_computation.40 | convolution fusion | flops 1887436800 | bytes 5963776 | tf_op jit(solution)/shard_map/dot_general | solution.py:79
  36.5 1.1 fusion.3
  37.9 1.0 fusion.10
  39.2 0.8 fusion.18
  40.2 0.4 fusion.28
  40.9 1.9 %convolution_select_fusion = f32[512,512]{1,0:T(8,128)S(1)} fusion(f32[512,512]{1,0:T(8,128)S(1)} %constant_dynamic-update-slice_fusion.1, s32[512]{0:T(512)S(1)} %add_select_fusion.2), kind=kOutput, calls=%fused_computation.1 | convolution fusion | flops 1611137024 | bytes 2099200 | tf_op jit(solution)/shard_map/dot_general | solution.py:106
  42.8 0.7 fusion.34
  43.5 0.5 fusion.33
  44.1 6.4 %collective-permute-start.4 = (f32[64,64]{0,1:T(8,128)S(1)}, f32[64,64]{0,1:T(8,128)S(1)}, u32[]{:S(2)}, u32[]{:S(2)}) collective-permute-start(f32[64,64]{0,1:T(8,128)S(1)} %fusion.33), channel_id=1, source_target_pairs={{0,32},{32,0},{64,96},{96,64},{128,160},{160,128},{192,224},{224,1... | collective-permute-start | bytes 49160 | tf_op jit(solution)/shard_map/ppermute | solution.py:56
  50.5 0.8 collective-permute-done.4
  51.3 6.1 %collective-permute-start.5 = (f32[64,64]{0,1:T(8,128)S(1)}, f32[64,64]{0,1:T(8,128)S(1)}, u32[]{:S(2)}, u32[]{:S(2)}) collective-permute-start(f32[64,64]{0,1:T(8,128)S(1)} %add.363), channel_id=1, source_target_pairs={{0,64},{32,96},{64,0},{96,32},{128,192},{160,224},{192,128},{224,1... | collective-permute-start | bytes 49160 | tf_op jit(solution)/shard_map/ppermute | solution.py:56
  57.4 1.9 %collective-permute-done.5 = f32[64,64]{0,1:T(8,128)S(1)} collective-permute-done((f32[64,64]{0,1:T(8,128)S(1)}, f32[64,64]{0,1:T(8,128)S(1)}, u32[]{:S(2)}, u32[]{:S(2)}) %collective-permute-start.5) | collective-permute-done | bytes 16416 | tf_op jit(solution)/shard_map/ppermute | solution.py:56
  59.3 4.9 %collective-permute-start.6 = (f32[64,64]{0,1:T(8,128)S(1)}, f32[64,64]{0,1:T(8,128)S(1)}, u32[]{:S(2)}, u32[]{:S(2)}) collective-permute-start(f32[64,64]{0,1:T(8,128)S(1)} %add.364), channel_id=1, source_target_pairs={{0,128},{32,160},{64,192},{96,224},{128,0},{160,32},{192,64},{224,... | collective-permute-start | bytes 49160 | tf_op jit(solution)/shard_map/ppermute | solution.py:56
  64.2 1.9 %collective-permute-done.6 = f32[64,64]{0,1:T(8,128)S(1)} collective-permute-done((f32[64,64]{0,1:T(8,128)S(1)}, f32[64,64]{0,1:T(8,128)S(1)}, u32[]{:S(2)}, u32[]{:S(2)}) %collective-permute-start.6) | collective-permute-done | bytes 16416 | tf_op jit(solution)/shard_map/ppermute | solution.py:56
  66.1 8.6 %collective-permute-start.7 = (f32[64,64]{0,1:T(8,128)S(1)}, f32[64,64]{0,1:T(8,128)S(1)}, u32[]{:S(2)}, u32[]{:S(2)}) collective-permute-start(f32[64,64]{0,1:T(8,128)S(1)} %add.365), channel_id=1, source_target_pairs={{0,256},{32,288},{64,320},{96,352},{128,384},{160,416},{192,448},{... | collective-permute-start | bytes 49160 | tf_op jit(solution)/shard_map/ppermute | solution.py:56
  74.7 2.0 %collective-permute-done.7 = f32[64,64]{0,1:T(8,128)S(1)} collective-permute-done((f32[64,64]{0,1:T(8,128)S(1)}, f32[64,64]{0,1:T(8,128)S(1)}, u32[]{:S(2)}, u32[]{:S(2)}) %collective-permute-start.7) | collective-permute-done | bytes 16416 | tf_op jit(solution)/shard_map/ppermute | solution.py:56
  76.7 1.9 %collective-permute-start.8 = (f32[64,64]{0,1:T(8,128)S(1)}, f32[64,64]{0,1:T(8,128)S(1)}, u32[]{:S(2)}, u32[]{:S(2)}) collective-permute-start(f32[64,64]{0,1:T(8,128)S(1)} %add.366), channel_id=1, source_target_pairs={{0,1},{1,0},{2,3},{3,2},{4,5},{5,4},{6,7},{7,6},{8,9},{9,8},{10,11... | collective-permute-start | bytes 49160 | tf_op jit(solution)/shard_map/ppermute | solution.py:56
  78.6 3.9 %collective-permute-done.8 = f32[64,64]{0,1:T(8,128)S(1)} collective-permute-done((f32[64,64]{0,1:T(8,128)S(1)}, f32[64,64]{0,1:T(8,128)S(1)}, u32[]{:S(2)}, u32[]{:S(2)}) %collective-permute-start.8) | collective-permute-done | bytes 16416 | tf_op jit(solution)/shard_map/ppermute | solution.py:56
  82.5 4.1 %collective-permute-start.9 = (f32[64,64]{0,1:T(8,128)S(1)}, f32[64,64]{0,1:T(8,128)S(1)}, u32[]{:S(2)}, u32[]{:S(2)}) collective-permute-start(f32[64,64]{0,1:T(8,128)S(1)} %add.367), channel_id=1, source_target_pairs={{0,2},{1,3},{2,0},{3,1},{4,6},{5,7},{6,4},{7,5},{8,10},{9,11},{10,... | collective-permute-start | bytes 49160 | tf_op jit(solution)/shard_map/ppermute | solution.py:56
  86.7 2.6 %collective-permute-done.9 = f32[64,64]{0,1:T(8,128)S(1)} collective-permute-done((f32[64,64]{0,1:T(8,128)S(1)}, f32[64,64]{0,1:T(8,128)S(1)}, u32[]{:S(2)}, u32[]{:S(2)}) %collective-permute-start.9) | collective-permute-done | bytes 16416 | tf_op jit(solution)/shard_map/ppermute | solution.py:56
  89.2 5.3 %collective-permute-start.10 = (f32[64,64]{0,1:T(8,128)S(1)}, f32[64,64]{0,1:T(8,128)S(1)}, u32[]{:S(2)}, u32[]{:S(2)}) collective-permute-start(f32[64,64]{0,1:T(8,128)S(1)} %add.368), channel_id=1, source_target_pairs={{0,4},{1,5},{2,6},{3,7},{4,0},{5,1},{6,2},{7,3},{8,12},{9,13},{10,... | collective-permute-start | bytes 49160 | tf_op jit(solution)/shard_map/ppermute | solution.py:56
  94.5 4.5 %collective-permute-done.10 = f32[64,64]{0,1:T(8,128)S(1)} collective-permute-done((f32[64,64]{0,1:T(8,128)S(1)}, f32[64,64]{0,1:T(8,128)S(1)}, u32[]{:S(2)}, u32[]{:S(2)}) %collective-permute-start.10) | collective-permute-done | bytes 16416 | tf_op jit(solution)/shard_map/ppermute | solution.py:56
  99.0 2.3 %collective-permute-start.11 = (f32[64,64]{0,1:T(8,128)S(1)}, f32[64,64]{0,1:T(8,128)S(1)}, u32[]{:S(2)}, u32[]{:S(2)}) collective-permute-start(f32[64,64]{0,1:T(8,128)S(1)} %add.369), channel_id=1, source_target_pairs={{0,8},{1,9},{2,10},{3,11},{4,12},{5,13},{6,14},{7,15},{8,0},{9,1},... | collective-permute-start | bytes 49160 | tf_op jit(solution)/shard_map/ppermute | solution.py:56
  101.4 3.4 %collective-permute-done.11 = f32[64,64]{0,1:T(8,128)S(1)} collective-permute-done((f32[64,64]{0,1:T(8,128)S(1)}, f32[64,64]{0,1:T(8,128)S(1)}, u32[]{:S(2)}, u32[]{:S(2)}) %collective-permute-start.11) | collective-permute-done | bytes 16416 | tf_op jit(solution)/shard_map/ppermute | solution.py:56
  104.8 3.1 %collective-permute-start.12 = (f32[64,64]{0,1:T(8,128)S(1)}, f32[64,64]{0,1:T(8,128)S(1)}, u32[]{:S(2)}, u32[]{:S(2)}) collective-permute-start(f32[64,64]{0,1:T(8,128)S(1)} %add.370), channel_id=1, source_target_pairs={{0,16},{1,17},{2,18},{3,19},{4,20},{5,21},{6,22},{7,23},{8,24},{9,... | collective-permute-start | bytes 49160 | tf_op jit(solution)/shard_map/ppermute | solution.py:56
  108.0 4.1 %collective-permute-done.12 = f32[64,64]{0,1:T(8,128)S(1)} collective-permute-done((f32[64,64]{0,1:T(8,128)S(1)}, f32[64,64]{0,1:T(8,128)S(1)}, u32[]{:S(2)}, u32[]{:S(2)}) %collective-permute-start.12) | collective-permute-done | bytes 16416 | tf_op jit(solution)/shard_map/ppermute | solution.py:56
  113.1 4.4 %cholesky.16 = f32[48,48]{1,0:T(8,128)S(1)} custom-call(f32[48,48]{1,0:T(8,128)S(1)} %fusion.63), custom_call_target="Cholesky" | custom-call | tf_op jit(solution)/shard_map/jit(cholesky)/cholesky | solution.py:119
  117.5 0.6 compare_reduce_fusion
  118.2 0.7 fusion.58
  118.8 3.7 %custom-call.10 = f32[1,48,48]{1,2,0:T(8,128)S(1)} custom-call(f32[1,48,48]{2,1,0:T(8,128)S(1)} %fusion.58), custom_call_target="InvertDiagBlocksLowerTriangular" | custom-call | tf_op jit(solution)/shard_map/jit(_cho_solve)/triangular_solve | solution.py:120
  123.6 0.5 convolution_select_fusion.1
  124.1 1.0 fusion.119
  125.2 0.8 reshape.431
  125.9 0.8 reshape.432
  (57 shorter events, 4.5 us)
Async XLA Ops:
  0.6 2.5 %copy-start.2 = (f32[8,8192]{1,0:T(8,128)S(1)}, f32[8,8192]{1,0:T(8,128)}, u32[]{:S(2)}) copy-start(f32[8,8192]{1,0:T(8,128)} %param.3) | copy-start | bytes 786436
  4.2 6.2 %collective-permute-start = (f32[4,16,1184]{2,1,0:T(8,128)}, f32[4,16,1184]{2,1,0:T(8,128)}, u32[]{:S(2)}, u32[]{:S(2)}) collective-permute-start(f32[4,16,1184]{2,1,0:T(8,128)} %get-tuple-element.8), channel_id=1, source_target_pairs={{0,32},{32,64},{64,96},{96,128},{128,160},{160,192},{192,224},{224... | collective-permute-start | bytes 909320 | tf_op jit(solution)/shard_map/ppermute | solution.py:23
  6.7 4.5 %collective-permute-start.1 = (f32[4,16,1184]{2,1,0:T(8,128)}, f32[4,16,1184]{2,1,0:T(8,128)}, u32[]{:S(2)}, u32[]{:S(2)}) collective-permute-start(f32[4,16,1184]{2,1,0:T(8,128)} %get-tuple-element.9), channel_id=1, source_target_pairs={{32,0},{64,32},{96,64},{128,96},{160,128},{192,160},{224,192},{256... | collective-permute-start | bytes 909320 | tf_op jit(solution)/shard_map/ppermute | solution.py:24
  12.5 16.3 %collective-permute-start.2 = (f32[16,4,1184]{2,1,0:T(4,128)S(1)}, f32[16,4,1184]{2,1,0:T(4,128)S(1)}, u32[]{:S(2)}, u32[]{:S(2)}) collective-permute-start(f32[16,4,1184]{2,1,0:T(4,128)S(1)} %get-tuple-element.4), channel_id=1, source_target_pairs={{0,1},{1,2},{2,3},{3,4},{4,5},{5,6},{6,7},{7,8},{8,9},{9,10},{10,1... | collective-permute-start | bytes 909320 | tf_op jit(solution)/shard_map/ppermute | solution.py:23
  16.7 13.4 %collective-permute-start.3 = (f32[16,4,1184]{2,1,0:T(4,128)S(1)}, f32[16,4,1184]{2,1,0:T(4,128)S(1)}, u32[]{:S(2)}, u32[]{:S(2)}) collective-permute-start(f32[16,4,1184]{2,1,0:T(4,128)S(1)} %get-tuple-element.5), channel_id=1, source_target_pairs={{1,0},{2,1},{3,2},{4,3},{5,4},{6,5},{7,6},{8,7},{9,8},{10,9},{11,1... | collective-permute-start | bytes 909320 | tf_op jit(solution)/shard_map/ppermute | solution.py:24
  31.6 1.4 %copy-start = (f32[160,2560,1]{1,0,2:T(8,128)S(1)}, f32[160,2560,1]{1,0,2:T(8,128)}, u32[]{:S(2)}) copy-start(f32[160,2560,1]{1,0,2:T(8,128)} %reshape.433) | copy-start | bytes 4915204
  42.8 65.2 %copy-start.1 = (f32[8,8192]{1,0:T(8,128)S(1)}, f32[8,8192]{1,0:T(8,128)}, u32[]{:S(2)}) copy-start(f32[8,8192]{1,0:T(8,128)} %param.4) | copy-start | bytes 786436
  44.1 7.2 %collective-permute-start.4 = (f32[64,64]{0,1:T(8,128)S(1)}, f32[64,64]{0,1:T(8,128)S(1)}, u32[]{:S(2)}, u32[]{:S(2)}) collective-permute-start(f32[64,64]{0,1:T(8,128)S(1)} %fusion.33), channel_id=1, source_target_pairs={{0,32},{32,0},{64,96},{96,64},{128,160},{160,128},{192,224},{224,1... | collective-permute-start | bytes 49160 | tf_op jit(solution)/shard_map/ppermute | solution.py:56
  51.3 8.0 %collective-permute-start.5 = (f32[64,64]{0,1:T(8,128)S(1)}, f32[64,64]{0,1:T(8,128)S(1)}, u32[]{:S(2)}, u32[]{:S(2)}) collective-permute-start(f32[64,64]{0,1:T(8,128)S(1)} %add.363), channel_id=1, source_target_pairs={{0,64},{32,96},{64,0},{96,32},{128,192},{160,224},{192,128},{224,1... | collective-permute-start | bytes 49160 | tf_op jit(solution)/shard_map/ppermute | solution.py:56
  59.3 6.8 %collective-permute-start.6 = (f32[64,64]{0,1:T(8,128)S(1)}, f32[64,64]{0,1:T(8,128)S(1)}, u32[]{:S(2)}, u32[]{:S(2)}) collective-permute-start(f32[64,64]{0,1:T(8,128)S(1)} %add.364), channel_id=1, source_target_pairs={{0,128},{32,160},{64,192},{96,224},{128,0},{160,32},{192,64},{224,... | collective-permute-start | bytes 49160 | tf_op jit(solution)/shard_map/ppermute | solution.py:56
  66.1 10.6 %collective-permute-start.7 = (f32[64,64]{0,1:T(8,128)S(1)}, f32[64,64]{0,1:T(8,128)S(1)}, u32[]{:S(2)}, u32[]{:S(2)}) collective-permute-start(f32[64,64]{0,1:T(8,128)S(1)} %add.365), channel_id=1, source_target_pairs={{0,256},{32,288},{64,320},{96,352},{128,384},{160,416},{192,448},{... | collective-permute-start | bytes 49160 | tf_op jit(solution)/shard_map/ppermute | solution.py:56
  76.7 5.8 %collective-permute-start.8 = (f32[64,64]{0,1:T(8,128)S(1)}, f32[64,64]{0,1:T(8,128)S(1)}, u32[]{:S(2)}, u32[]{:S(2)}) collective-permute-start(f32[64,64]{0,1:T(8,128)S(1)} %add.366), channel_id=1, source_target_pairs={{0,1},{1,0},{2,3},{3,2},{4,5},{5,4},{6,7},{7,6},{8,9},{9,8},{10,11... | collective-permute-start | bytes 49160 | tf_op jit(solution)/shard_map/ppermute | solution.py:56
  82.5 6.7 %collective-permute-start.9 = (f32[64,64]{0,1:T(8,128)S(1)}, f32[64,64]{0,1:T(8,128)S(1)}, u32[]{:S(2)}, u32[]{:S(2)}) collective-permute-start(f32[64,64]{0,1:T(8,128)S(1)} %add.367), channel_id=1, source_target_pairs={{0,2},{1,3},{2,0},{3,1},{4,6},{5,7},{6,4},{7,5},{8,10},{9,11},{10,... | collective-permute-start | bytes 49160 | tf_op jit(solution)/shard_map/ppermute | solution.py:56
  89.2 9.8 %collective-permute-start.10 = (f32[64,64]{0,1:T(8,128)S(1)}, f32[64,64]{0,1:T(8,128)S(1)}, u32[]{:S(2)}, u32[]{:S(2)}) collective-permute-start(f32[64,64]{0,1:T(8,128)S(1)} %add.368), channel_id=1, source_target_pairs={{0,4},{1,5},{2,6},{3,7},{4,0},{5,1},{6,2},{7,3},{8,12},{9,13},{10,... | collective-permute-start | bytes 49160 | tf_op jit(solution)/shard_map/ppermute | solution.py:56
  99.0 5.8 %collective-permute-start.11 = (f32[64,64]{0,1:T(8,128)S(1)}, f32[64,64]{0,1:T(8,128)S(1)}, u32[]{:S(2)}, u32[]{:S(2)}) collective-permute-start(f32[64,64]{0,1:T(8,128)S(1)} %add.369), channel_id=1, source_target_pairs={{0,8},{1,9},{2,10},{3,11},{4,12},{5,13},{6,14},{7,15},{8,0},{9,1},... | collective-permute-start | bytes 49160 | tf_op jit(solution)/shard_map/ppermute | solution.py:56
  104.8 7.3 %collective-permute-start.12 = (f32[64,64]{0,1:T(8,128)S(1)}, f32[64,64]{0,1:T(8,128)S(1)}, u32[]{:S(2)}, u32[]{:S(2)}) collective-permute-start(f32[64,64]{0,1:T(8,128)S(1)} %add.370), channel_id=1, source_target_pairs={{0,16},{1,17},{2,18},{3,19},{4,20},{5,21},{6,22},{7,23},{8,24},{9,... | collective-permute-start | bytes 49160 | tf_op jit(solution)/shard_map/ppermute | solution.py:56

commit v4 on v3

--- a/solution.py
+++ b/solution.py
@@ -14,15 +14,36 @@
 HIGH = lax.Precision.HIGHEST
 
 
-def exchange(block, axis, dim, width):
-    count = lax.axis_size(axis)
-    forward = [(i, i + 1) for i in range(count - 1)]
-    backward = [(i + 1, i) for i in range(count - 1)]
-    top = lax.slice_in_dim(block, block.shape[dim] - width, None, axis=dim)
-    bottom = lax.slice_in_dim(block, 0, width, axis=dim)
-    low = lax.ppermute(top, axis, forward)
-    high = lax.ppermute(bottom, axis, backward)
-    return jnp.concatenate([low, block, high], axis=dim)
+def exchange(block, width):
+    nx = lax.axis_size("gx")
+    ny = lax.axis_size("gy")
+
+    def shifted(part, dx, dy):
+        if dy == 0:
+            pairs = [(i, i + dx) for i in range(nx) if 0 <= i + dx < nx]
+            return lax.ppermute(part, "gx", pairs)
+        if dx == 0:
+            pairs = [(j, j + dy) for j in range(ny) if 0 <= j + dy < ny]
+            return lax.ppermute(part, "gy", pairs)
+        pairs = [
+            (i * ny + j, (i + dx) * ny + (j + dy))
+            for i in range(nx)
+            for j in range(ny)
+            if 0 <= i + dx < nx and 0 <= j + dy < ny
+        ]
+        return lax.ppermute(part, ("gx", "gy"), pairs)
+
+    w = width
+    x_top, x_bot = block[-w:], block[:w]
+    y_top, y_bot = block[:, -w:], block[:, :w]
+    rows_lo = jnp.concatenate(
+        [shifted(x_top[:, -w:], 1, 1), shifted(x_top, 1, 0), shifted(x_top[:, :w], 1, -1)], axis=1
+    )
+    rows_mid = jnp.concatenate([shifted(y_top, 0, 1), block, shifted(y_bot, 0, -1)], axis=1)
+    rows_hi = jnp.concatenate(
+        [shifted(x_bot[:, -w:], -1, 1), shifted(x_bot, -1, 0), shifted(x_bot[:, :w], -1, -1)], axis=1
+    )
+    return jnp.concatenate([rows_lo, rows_mid, rows_hi], axis=0)
 
 
 def operate(padded, coefs):
@@ -69,8 +90,7 @@
         rows_x, rows_y, 5 * NZ
     )
     packed = jnp.concatenate([guess, rhs_field, coef], axis=2)
-    packed = exchange(packed, "gx", 0, depth)
-    packed = exchange(packed, "gy", 1, depth)
+    packed = exchange(packed, depth)
     ex, ey = packed.shape[0], packed.shape[1]
     guess_e = packed[:, :, :width]
     rhs_e = packed[1:-1, 1:-1, width : 2 * width]

time: 127 us -> 137 us (1.079)
  starting transfers between devices: 59.6 us -> 64.6 us
  waiting for transfers between devices: 30.5 us -> 34.2 us
  local copies, waits for them, and re-layouts: 9.44 us -> 10.9 us
    ppermute x4 -> x8, starting transfers between devices: 16.9 us -> 29.5 us  [the longest x4 15.9 us: shifted(): return lax.ppermute(part, ('gx', 'gy'), pairs)]
    ppermute x9, starting transfers between devices: 42.7 us -> 35.1 us  [allreduce(): x = x + lax.ppermute(x, axis, [(i, i ^ bit) for i in range(count)])]
    ppermute x9, waiting for transfers between devices: 25.1 us -> 29.9 us  [allreduce(): x = x + lax.ppermute(x, axis, [(i, i ^ bit) for i in range(count)])]
    slice x1 -> x3, local copies, waits for them, and re-layouts: 0.88 us -> 2.37 us  [the longest x1 0.9 us: exchange(): x_top, x_bot = (block[-w:], block[:w])]
    ppermute x4 -> x8, waiting for transfers between devices: 5.35 us -> 4.29 us  [the longest x4 4.28 us: shifted(): return lax.ppermute(part, ('gx', 'gy'), pairs)]
  transfers between devices with their start and end apart: 13 -> 17, of which waited for: 12 -> 10; matrix products, arithmetic and copies ran while one was open for 2% -> 3% of each run, Pallas kernels for 0% -> 0%
where the time goes in v4:
time: 137 us; the launch traced here: 136 us
  starting transfers between devices  64.6 us (47%)
  waiting for transfers between devices  34.2 us (25%)
  other arithmetic  14.9 us (11%)
  local copies, waits for them, and re-layouts  10.9 us (8%)
  matrix products  10 us (7%)
    ppermute x9, starting transfers between devices, allreduce(): x = x + lax.ppermute(x, axis, [(i, i ^ bit) for i in range(count)])  35.1 us
    ppermute x9, waiting for transfers between devices, allreduce(): x = x + lax.ppermute(x, axis, [(i, i ^ bit) for i in range(count)])  29.9 us
    ppermute x4, starting transfers between devices, shifted(): return lax.ppermute(part, ('gx', 'gy'), pairs)  15.9 us
    ppermute x2, starting transfers between devices, shifted(): return lax.ppermute(part, 'gy', pairs)  7.95 us
    ppermute x2, starting transfers between devices, shifted(): return lax.ppermute(part, 'gx', pairs)  5.62 us
    another operation x3, other arithmetic, per_device(): factor = jnp.linalg.cholesky(normal)  5.05 us
    another operation x2, other arithmetic, per_device(): weights = jax.scipy.linalg.cho_solve((factor, True), target)  4.32 us
    ppermute x4, waiting for transfers between devices, shifted(): return lax.ppermute(part, ('gx', 'gy'), pairs)  4.28 us
  transfers between devices with their start and end apart: 17, of which 10 were waited for; matrix products, arithmetic and copies ran while one was open for 3% of the time, Pallas kernels for 0%

profile of v4, /device:TPU:6, one launch (start us, length us, event | category | flops | bytes accessed | tf_op | source)
XLA Modules:
  0.0 135.8 jit_solution(11484976892767816625)
XLA Ops:
  0.6 1.2 bitcast_dynamic-update-slice_fusion.1
  1.8 1.0 reshape.425
  3.3 0.8 fusion.116
  4.1 4.3 %collective-permute-start = (f32[4,4,1184]{2,1,0:T(4,128)}, f32[4,4,1184]{2,1,0:T(4,128)}, u32[]{:S(2)}, u32[]{:S(2)}) collective-permute-start(f32[4,4,1184]{2,1,0:T(4,128)} %get-tuple-element.6), channel_id=1, source_target_pairs={{0,33},{1,34},{2,35},{3,36},{4,37},{5,38},{6,39},{7,40},{8,41},{9,... | collective-permute-start | bytes 227336 | tf_op jit(solution)/shard_map/ppermute | solution.py:34
  8.4 8.9 %collective-permute-start.2 = (f32[4,4,1184]{2,1,0:T(4,128)}, f32[4,4,1184]{2,1,0:T(4,128)}, u32[]{:S(2)}, u32[]{:S(2)}) collective-permute-start(f32[4,4,1184]{2,1,0:T(4,128)} %get-tuple-element.9), channel_id=1, source_target_pairs={{1,32},{2,33},{3,34},{4,35},{5,36},{6,37},{7,38},{8,39},{9,40},{10... | collective-permute-start | bytes 227336 | tf_op jit(solution)/shard_map/ppermute | solution.py:34
  17.3 1.3 collective-permute-start.5
  18.6 0.9 fusion.117
  19.5 4.3 %collective-permute-start.1 = (f32[4,16,1184]{2,1,0:T(8,128)}, f32[4,16,1184]{2,1,0:T(8,128)}, u32[]{:S(2)}, u32[]{:S(2)}) collective-permute-start(f32[4,16,1184]{2,1,0:T(8,128)} %get-tuple-element.10), channel_id=1, source_target_pairs={{0,32},{32,64},{64,96},{96,128},{128,160},{160,192},{192,224},{224... | collective-permute-start | bytes 909320 | tf_op jit(solution)/shard_map/ppermute | solution.py:24
  23.8 1.3 collective-permute-start.6
  25.1 0.7 fusion.118
  26.4 1.9 %collective-permute-start.3 = (f32[8,4,1184]{2,1,0:T(4,128)}, f32[8,4,1184]{2,1,0:T(4,128)}, u32[]{:S(2)}, u32[]{:S(2)}) collective-permute-start(f32[8,4,1184]{2,1,0:T(4,128)} %get-tuple-element.12), channel_id=1, source_target_pairs={{0,1},{1,2},{2,3},{3,4},{4,5},{5,6},{6,7},{7,8},{8,9},{9,10},{10,1... | collective-permute-start | bytes 454664 | tf_op jit(solution)/shard_map/ppermute | solution.py:27
  28.3 6.0 %collective-permute-start.4 = (f32[8,4,1184]{2,1,0:T(4,128)S(1)}, f32[8,4,1184]{2,1,0:T(4,128)}, u32[]{:S(2)}, u32[]{:S(2)}) collective-permute-start(f32[8,4,1184]{2,1,0:T(4,128)S(1)} %get-tuple-element.13), channel_id=1, source_target_pairs={{1,0},{2,1},{3,2},{4,3},{5,4},{6,5},{7,6},{8,7},{9,8},{10,9},{11,1... | collective-permute-start | bytes 454664 | tf_op jit(solution)/shard_map/ppermute | solution.py:27
  34.4 1.8 %reshape.433 = f32[160,2560,1]{1,0,2:T(8,128)} reshape(f32[5,32,5,512]{3,2,1,0:T(8,128)S(1)} %broadcast_multiply_fusion) | data formatting | bytes 3276800 | tf_op jit(solution)/shard_map/jit(kron)/mul | solution.py:98
  36.2 1.5 %collective-permute-start.7 = (f32[4,4,1184]{2,1,0:T(4,128)S(1)}, f32[4,4,1184]{2,1,0:T(4,128)S(1)}, u32[]{:S(2)}, u32[]{:S(2)}) collective-permute-start(f32[4,4,1184]{2,1,0:T(4,128)S(1)} %copy-done.3), channel_id=1, source_target_pairs={{33,0},{34,1},{35,2},{36,3},{37,4},{38,5},{39,6},{40,7},{41,8},{42... | collective-permute-start | bytes 227336 | tf_op jit(solution)/shard_map/ppermute | solution.py:34
  37.7 4.3 %collective-permute-done.7 = f32[4,4,1184]{2,1,0:T(4,128)S(1)} collective-permute-done((f32[4,4,1184]{2,1,0:T(4,128)S(1)}, f32[4,4,1184]{2,1,0:T(4,128)S(1)}, u32[]{:S(2)}, u32[]{:S(2)}) %collective-permute-start.7) | collective-permute-done | bytes 75808 | tf_op jit(solution)/shard_map/ppermute | solution.py:34
  42.0 1.6 %maximum_maximum_fusion = f32[16,24,1184]{2,1,0:T(8,128)S(1)} fusion(f32[4,4,1184]{2,1,0:T(4,128)S(1)} %collective-permute-done.7, f32[4,16,1184]{2,1,0:T(8,128)} %collective-permute-done.6, f32[4,4,1184]{2,1,0:T(4,128)} %collective-permute-done.5, f32[8,4,1184]{2,1,0:T(4,128)} %collective-permute-done.4, ...), kind=kLoop, calls=%fused_computation | loop fusion | flops 3637248 | bytes 3637248 | tf_op jit(solution)/shard_map/concatenate | solution.py:46
  43.9 1.1 copy-done
  45.0 3.5 %fusion.22 = f32[16,24,2560]{2,1,0:T(8,128)S(1)} fusion(f32[160,2560,1]{1,0,2:T(8,128)S(1)} %copy-done, f32[16,24,1184]{2,1,0:T(8,128)S(1)} %maximum_maximum_fusion), kind=kOutput, calls=%fused_computation.40 | convolution fusion | flops 1887436800 | bytes 5963776 | tf_op jit(solution)/shard_map/dot_general | solution.py:99
  48.5 1.1 fusion.3
  49.9 1.0 fusion.10
  51.2 0.8 fusion.18
  52.9 1.9 %convolution_select_fusion = f32[512,512]{1,0:T(8,128)S(1)} fusion(f32[512,512]{1,0:T(8,128)S(1)} %constant_dynamic-update-slice_fusion.1, s32[512]{0:T(512)S(1)} %add_select_fusion.2), kind=kOutput, calls=%fused_computation.1 | convolution fusion | flops 1611137024 | bytes 2099200 | tf_op jit(solution)/shard_map/dot_general | solution.py:126
  54.8 0.7 fusion.34
  56.1 3.6 %collective-permute-start.8 = (f32[64,64]{0,1:T(8,128)S(1)}, f32[64,64]{0,1:T(8,128)S(1)}, u32[]{:S(2)}, u32[]{:S(2)}) collective-permute-start(f32[64,64]{0,1:T(8,128)S(1)} %fusion.33), channel_id=1, source_target_pairs={{0,32},{32,0},{64,96},{96,64},{128,160},{160,128},{192,224},{224,1... | collective-permute-start | bytes 49160 | tf_op jit(solution)/shard_map/ppermute | solution.py:77
  59.7 0.8 collective-permute-done.8
  60.6 4.1 %collective-permute-start.9 = (f32[64,64]{0,1:T(8,128)S(1)}, f32[64,64]{0,1:T(8,128)S(1)}, u32[]{:S(2)}, u32[]{:S(2)}) collective-permute-start(f32[64,64]{0,1:T(8,128)S(1)} %add.363), channel_id=1, source_target_pairs={{0,64},{32,96},{64,0},{96,32},{128,192},{160,224},{192,128},{224,1... | collective-permute-start | bytes 49160 | tf_op jit(solution)/shard_map/ppermute | solution.py:77
  64.7 1.9 %collective-permute-done.9 = f32[64,64]{0,1:T(8,128)S(1)} collective-permute-done((f32[64,64]{0,1:T(8,128)S(1)}, f32[64,64]{0,1:T(8,128)S(1)}, u32[]{:S(2)}, u32[]{:S(2)}) %collective-permute-start.9) | collective-permute-done | bytes 16416 | tf_op jit(solution)/shard_map/ppermute | solution.py:77
  66.6 7.5 %collective-permute-start.10 = (f32[64,64]{0,1:T(8,128)S(1)}, f32[64,64]{0,1:T(8,128)S(1)}, u32[]{:S(2)}, u32[]{:S(2)}) collective-permute-start(f32[64,64]{0,1:T(8,128)S(1)} %add.364), channel_id=1, source_target_pairs={{0,128},{32,160},{64,192},{96,224},{128,0},{160,32},{192,64},{224,... | collective-permute-start | bytes 49160 | tf_op jit(solution)/shard_map/ppermute | solution.py:77
  74.1 2.2 %collective-permute-done.10 = f32[64,64]{0,1:T(8,128)S(1)} collective-permute-done((f32[64,64]{0,1:T(8,128)S(1)}, f32[64,64]{0,1:T(8,128)S(1)}, u32[]{:S(2)}, u32[]{:S(2)}) %collective-permute-start.10) | collective-permute-done | bytes 16416 | tf_op jit(solution)/shard_map/ppermute | solution.py:77
  76.2 6.7 %collective-permute-start.11 = (f32[64,64]{0,1:T(8,128)S(1)}, f32[64,64]{0,1:T(8,128)S(1)}, u32[]{:S(2)}, u32[]{:S(2)}) collective-permute-start(f32[64,64]{0,1:T(8,128)S(1)} %add.365), channel_id=1, source_target_pairs={{0,256},{32,288},{64,320},{96,352},{128,384},{160,416},{192,448},{... | collective-permute-start | bytes 49160 | tf_op jit(solution)/shard_map/ppermute | solution.py:77
  83.0 3.0 %collective-permute-done.11 = f32[64,64]{0,1:T(8,128)S(1)} collective-permute-done((f32[64,64]{0,1:T(8,128)S(1)}, f32[64,64]{0,1:T(8,128)S(1)}, u32[]{:S(2)}, u32[]{:S(2)}) %collective-permute-start.11) | collective-permute-done | bytes 16416 | tf_op jit(solution)/shard_map/ppermute | solution.py:77
  86.0 1.9 %collective-permute-start.12 = (f32[64,64]{0,1:T(8,128)S(1)}, f32[64,64]{0,1:T(8,128)S(1)}, u32[]{:S(2)}, u32[]{:S(2)}) collective-permute-start(f32[64,64]{0,1:T(8,128)S(1)} %add.366), channel_id=1, source_target_pairs={{0,1},{1,0},{2,3},{3,2},{4,5},{5,4},{6,7},{7,6},{8,9},{9,8},{10,11... | collective-permute-start | bytes 49160 | tf_op jit(solution)/shard_map/ppermute | solution.py:77
  87.9 3.9 %collective-permute-done.12 = f32[64,64]{0,1:T(8,128)S(1)} collective-permute-done((f32[64,64]{0,1:T(8,128)S(1)}, f32[64,64]{0,1:T(8,128)S(1)}, u32[]{:S(2)}, u32[]{:S(2)}) %collective-permute-start.12) | collective-permute-done | bytes 16416 | tf_op jit(solution)/shard_map/ppermute | solution.py:77
  91.8 2.2 %collective-permute-start.13 = (f32[64,64]{0,1:T(8,128)S(1)}, f32[64,64]{0,1:T(8,128)S(1)}, u32[]{:S(2)}, u32[]{:S(2)}) collective-permute-start(f32[64,64]{0,1:T(8,128)S(1)} %add.367), channel_id=1, source_target_pairs={{0,2},{1,3},{2,0},{3,1},{4,6},{5,7},{6,4},{7,5},{8,10},{9,11},{10,... | collective-permute-start | bytes 49160 | tf_op jit(solution)/shard_map/ppermute | solution.py:77
  94.0 4.5 %collective-permute-done.13 = f32[64,64]{0,1:T(8,128)S(1)} collective-permute-done((f32[64,64]{0,1:T(8,128)S(1)}, f32[64,64]{0,1:T(8,128)S(1)}, u32[]{:S(2)}, u32[]{:S(2)}) %collective-permute-start.13) | collective-permute-done | bytes 16416 | tf_op jit(solution)/shard_map/ppermute | solution.py:77
  98.5 3.4 %collective-permute-start.14 = (f32[64,64]{0,1:T(8,128)S(1)}, f32[64,64]{0,1:T(8,128)S(1)}, u32[]{:S(2)}, u32[]{:S(2)}) collective-permute-start(f32[64,64]{0,1:T(8,128)S(1)} %add.368), channel_id=1, source_target_pairs={{0,4},{1,5},{2,6},{3,7},{4,0},{5,1},{6,2},{7,3},{8,12},{9,13},{10,... | collective-permute-start | bytes 49160 | tf_op jit(solution)/shard_map/ppermute | solution.py:77
  101.8 6.3 %collective-permute-done.14 = f32[64,64]{0,1:T(8,128)S(1)} collective-permute-done((f32[64,64]{0,1:T(8,128)S(1)}, f32[64,64]{0,1:T(8,128)S(1)}, u32[]{:S(2)}, u32[]{:S(2)}) %collective-permute-start.14) | collective-permute-done | bytes 16416 | tf_op jit(solution)/shard_map/ppermute | solution.py:77
  108.2 2.4 %collective-permute-start.15 = (f32[64,64]{0,1:T(8,128)S(1)}, f32[64,64]{0,1:T(8,128)S(1)}, u32[]{:S(2)}, u32[]{:S(2)}) collective-permute-start(f32[64,64]{0,1:T(8,128)S(1)} %add.369), channel_id=1, source_target_pairs={{0,8},{1,9},{2,10},{3,11},{4,12},{5,13},{6,14},{7,15},{8,0},{9,1},... | collective-permute-start | bytes 49160 | tf_op jit(solution)/shard_map/ppermute | solution.py:77
  110.6 3.4 %collective-permute-done.15 = f32[64,64]{0,1:T(8,128)S(1)} collective-permute-done((f32[64,64]{0,1:T(8,128)S(1)}, f32[64,64]{0,1:T(8,128)S(1)}, u32[]{:S(2)}, u32[]{:S(2)}) %collective-permute-start.15) | collective-permute-done | bytes 16416 | tf_op jit(solution)/shard_map/ppermute | solution.py:77
  114.0 3.3 %collective-permute-start.16 = (f32[64,64]{0,1:T(8,128)S(1)}, f32[64,64]{0,1:T(8,128)S(1)}, u32[]{:S(2)}, u32[]{:S(2)}) collective-permute-start(f32[64,64]{0,1:T(8,128)S(1)} %add.370), channel_id=1, source_target_pairs={{0,16},{1,17},{2,18},{3,19},{4,20},{5,21},{6,22},{7,23},{8,24},{9,... | collective-permute-start | bytes 49160 | tf_op jit(solution)/shard_map/ppermute | solution.py:77
  117.3 4.0 %collective-permute-done.16 = f32[64,64]{0,1:T(8,128)S(1)} collective-permute-done((f32[64,64]{0,1:T(8,128)S(1)}, f32[64,64]{0,1:T(8,128)S(1)}, u32[]{:S(2)}, u32[]{:S(2)}) %collective-permute-start.16) | collective-permute-done | bytes 16416 | tf_op jit(solution)/shard_map/ppermute | solution.py:77
  122.3 4.4 %cholesky.16 = f32[48,48]{1,0:T(8,128)S(1)} custom-call(f32[48,48]{1,0:T(8,128)S(1)} %fusion.63), custom_call_target="Cholesky" | custom-call | tf_op jit(solution)/shard_map/jit(cholesky)/cholesky | solution.py:139
  126.7 0.6 compare_reduce_fusion
  127.3 0.7 fusion.58
  128.0 3.7 %custom-call.10 = f32[1,48,48]{1,2,0:T(8,128)S(1)} custom-call(f32[1,48,48]{2,1,0:T(8,128)S(1)} %fusion.58), custom_call_target="InvertDiagBlocksLowerTriangular" | custom-call | tf_op jit(solution)/shard_map/jit(_cho_solve)/triangular_solve | solution.py:140
  133.3 1.0 fusion.121
  134.3 0.8 reshape.431
  135.1 0.8 reshape.432
  (68 shorter events, 6.0 us)
Async XLA Ops:
  0.6 2.5 %copy-start.2 = (f32[8,8192]{1,0:T(8,128)S(1)}, f32[8,8192]{1,0:T(8,128)}, u32[]{:S(2)}) copy-start(f32[8,8192]{1,0:T(8,128)} %param.3) | copy-start | bytes 786436
  4.1 22.3 %collective-permute-start = (f32[4,4,1184]{2,1,0:T(4,128)}, f32[4,4,1184]{2,1,0:T(4,128)}, u32[]{:S(2)}, u32[]{:S(2)}) collective-permute-start(f32[4,4,1184]{2,1,0:T(4,128)} %get-tuple-element.6), channel_id=1, source_target_pairs={{0,33},{1,34},{2,35},{3,36},{4,37},{5,38},{6,39},{7,40},{8,41},{9,... | collective-permute-start | bytes 227336 | tf_op jit(solution)/shard_map/ppermute | solution.py:34
  8.4 19.9 %collective-permute-start.2 = (f32[4,4,1184]{2,1,0:T(4,128)}, f32[4,4,1184]{2,1,0:T(4,128)}, u32[]{:S(2)}, u32[]{:S(2)}) collective-permute-start(f32[4,4,1184]{2,1,0:T(4,128)} %get-tuple-element.9), channel_id=1, source_target_pairs={{1,32},{2,33},{3,34},{4,35},{5,36},{6,37},{7,38},{8,39},{9,40},{10... | collective-permute-start | bytes 227336 | tf_op jit(solution)/shard_map/ppermute | solution.py:34
  17.3 18.9 %collective-permute-start.5 = (f32[4,4,1184]{2,1,0:T(4,128)}, f32[4,4,1184]{2,1,0:T(4,128)}, u32[]{:S(2)}, u32[]{:S(2)}) collective-permute-start(f32[4,4,1184]{2,1,0:T(4,128)} %get-tuple-element.8), channel_id=1, source_target_pairs={{32,1},{33,2},{34,3},{35,4},{36,5},{37,6},{38,7},{39,8},{40,9},{41... | collective-permute-start | bytes 227336 | tf_op jit(solution)/shard_map/ppermute | solution.py:34
  19.5 22.5 %collective-permute-start.1 = (f32[4,16,1184]{2,1,0:T(8,128)}, f32[4,16,1184]{2,1,0:T(8,128)}, u32[]{:S(2)}, u32[]{:S(2)}) collective-permute-start(f32[4,16,1184]{2,1,0:T(8,128)} %get-tuple-element.10), channel_id=1, source_target_pairs={{0,32},{32,64},{64,96},{96,128},{128,160},{160,192},{192,224},{224... | collective-permute-start | bytes 909320 | tf_op jit(solution)/shard_map/ppermute | solution.py:24
  23.8 18.2 %collective-permute-start.6 = (f32[4,16,1184]{2,1,0:T(8,128)}, f32[4,16,1184]{2,1,0:T(8,128)}, u32[]{:S(2)}, u32[]{:S(2)}) collective-permute-start(f32[4,16,1184]{2,1,0:T(8,128)} %get-tuple-element.11), channel_id=1, source_target_pairs={{32,0},{64,32},{96,64},{128,96},{160,128},{192,160},{224,192},{256... | collective-permute-start | bytes 909320 | tf_op jit(solution)/shard_map/ppermute | solution.py:24
  26.4 15.6 %collective-permute-start.3 = (f32[8,4,1184]{2,1,0:T(4,128)}, f32[8,4,1184]{2,1,0:T(4,128)}, u32[]{:S(2)}, u32[]{:S(2)}) collective-permute-start(f32[8,4,1184]{2,1,0:T(4,128)} %get-tuple-element.12), channel_id=1, source_target_pairs={{0,1},{1,2},{2,3},{3,4},{4,5},{5,6},{6,7},{7,8},{8,9},{9,10},{10,1... | collective-permute-start | bytes 454664 | tf_op jit(solution)/shard_map/ppermute | solution.py:27
  28.3 13.6 %collective-permute-start.4 = (f32[8,4,1184]{2,1,0:T(4,128)S(1)}, f32[8,4,1184]{2,1,0:T(4,128)}, u32[]{:S(2)}, u32[]{:S(2)}) collective-permute-start(f32[8,4,1184]{2,1,0:T(4,128)S(1)} %get-tuple-element.13), channel_id=1, source_target_pairs={{1,0},{2,1},{3,2},{4,3},{5,4},{6,5},{7,6},{8,7},{9,8},{10,9},{11,1... | collective-permute-start | bytes 454664 | tf_op jit(solution)/shard_map/ppermute | solution.py:27
  34.4 1.8 %copy-start.3 = (f32[4,4,1184]{2,1,0:T(4,128)S(1)}, f32[4,4,1184]{2,1,0:T(4,128)}, u32[]{:S(2)}) copy-start(f32[4,4,1184]{2,1,0:T(4,128)} %get-tuple-element.7) | copy-start | bytes 227332
  36.2 5.7 %collective-permute-start.7 = (f32[4,4,1184]{2,1,0:T(4,128)S(1)}, f32[4,4,1184]{2,1,0:T(4,128)S(1)}, u32[]{:S(2)}, u32[]{:S(2)}) collective-permute-start(f32[4,4,1184]{2,1,0:T(4,128)S(1)} %copy-done.3), channel_id=1, source_target_pairs={{33,0},{34,1},{35,2},{36,3},{37,4},{38,5},{39,6},{40,7},{41,8},{42... | collective-permute-start | bytes 227336 | tf_op jit(solution)/shard_map/ppermute | solution.py:34
  43.6 1.4 %copy-start = (f32[160,2560,1]{1,0,2:T(8,128)S(1)}, f32[160,2560,1]{1,0,2:T(8,128)}, u32[]{:S(2)}) copy-start(f32[160,2560,1]{1,0,2:T(8,128)} %reshape.433) | copy-start | bytes 4915204
  54.8 62.5 %copy-start.1 = (f32[8,8192]{1,0:T(8,128)S(1)}, f32[8,8192]{1,0:T(8,128)}, u32[]{:S(2)}) copy-start(f32[8,8192]{1,0:T(8,128)} %param.4) | copy-start | bytes 786436
  56.1 4.5 %collective-permute-start.8 = (f32[64,64]{0,1:T(8,128)S(1)}, f32[64,64]{0,1:T(8,128)S(1)}, u32[]{:S(2)}, u32[]{:S(2)}) collective-permute-start(f32[64,64]{0,1:T(8,128)S(1)} %fusion.33), channel_id=1, source_target_pairs={{0,32},{32,0},{64,96},{96,64},{128,160},{160,128},{192,224},{224,1... | collective-permute-start | bytes 49160 | tf_op jit(solution)/shard_map/ppermute | solution.py:77
  60.6 6.0 %collective-permute-start.9 = (f32[64,64]{0,1:T(8,128)S(1)}, f32[64,64]{0,1:T(8,128)S(1)}, u32[]{:S(2)}, u32[]{:S(2)}) collective-permute-start(f32[64,64]{0,1:T(8,128)S(1)} %add.363), channel_id=1, source_target_pairs={{0,64},{32,96},{64,0},{96,32},{128,192},{160,224},{192,128},{224,1... | collective-permute-start | bytes 49160 | tf_op jit(solution)/shard_map/ppermute | solution.py:77
  66.6 9.7 %collective-permute-start.10 = (f32[64,64]{0,1:T(8,128)S(1)}, f32[64,64]{0,1:T(8,128)S(1)}, u32[]{:S(2)}, u32[]{:S(2)}) collective-permute-start(f32[64,64]{0,1:T(8,128)S(1)} %add.364), channel_id=1, source_target_pairs={{0,128},{32,160},{64,192},{96,224},{128,0},{160,32},{192,64},{224,... | collective-permute-start | bytes 49160 | tf_op jit(solution)/shard_map/ppermute | solution.py:77
  76.2 9.7 %collective-permute-start.11 = (f32[64,64]{0,1:T(8,128)S(1)}, f32[64,64]{0,1:T(8,128)S(1)}, u32[]{:S(2)}, u32[]{:S(2)}) collective-permute-start(f32[64,64]{0,1:T(8,128)S(1)} %add.365), channel_id=1, source_target_pairs={{0,256},{32,288},{64,320},{96,352},{128,384},{160,416},{192,448},{... | collective-permute-start | bytes 49160 | tf_op jit(solution)/shard_map/ppermute | solution.py:77
  86.0 5.8 %collective-permute-start.12 = (f32[64,64]{0,1:T(8,128)S(1)}, f32[64,64]{0,1:T(8,128)S(1)}, u32[]{:S(2)}, u32[]{:S(2)}) collective-permute-start(f32[64,64]{0,1:T(8,128)S(1)} %add.366), channel_id=1, source_target_pairs={{0,1},{1,0},{2,3},{3,2},{4,5},{5,4},{6,7},{7,6},{8,9},{9,8},{10,11... | collective-permute-start | bytes 49160 | tf_op jit(solution)/shard_map/ppermute | solution.py:77
  91.8 6.7 %collective-permute-start.13 = (f32[64,64]{0,1:T(8,128)S(1)}, f32[64,64]{0,1:T(8,128)S(1)}, u32[]{:S(2)}, u32[]{:S(2)}) collective-permute-start(f32[64,64]{0,1:T(8,128)S(1)} %add.367), channel_id=1, source_target_pairs={{0,2},{1,3},{2,0},{3,1},{4,6},{5,7},{6,4},{7,5},{8,10},{9,11},{10,... | collective-permute-start | bytes 49160 | tf_op jit(solution)/shard_map/ppermute | solution.py:77
  98.5 9.7 %collective-permute-start.14 = (f32[64,64]{0,1:T(8,128)S(1)}, f32[64,64]{0,1:T(8,128)S(1)}, u32[]{:S(2)}, u32[]{:S(2)}) collective-permute-start(f32[64,64]{0,1:T(8,128)S(1)} %add.368), channel_id=1, source_target_pairs={{0,4},{1,5},{2,6},{3,7},{4,0},{5,1},{6,2},{7,3},{8,12},{9,13},{10,... | collective-permute-start | bytes 49160 | tf_op jit(solution)/shard_map/ppermute | solution.py:77
  108.2 5.8 %collective-permute-start.15 = (f32[64,64]{0,1:T(8,128)S(1)}, f32[64,64]{0,1:T(8,128)S(1)}, u32[]{:S(2)}, u32[]{:S(2)}) collective-permute-start(f32[64,64]{0,1:T(8,128)S(1)} %add.369), channel_id=1, source_target_pairs={{0,8},{1,9},{2,10},{3,11},{4,12},{5,13},{6,14},{7,15},{8,0},{9,1},... | collective-permute-start | bytes 49160 | tf_op jit(solution)/shard_map/ppermute | solution.py:77
  114.0 7.3 %collective-permute-start.16 = (f32[64,64]{0,1:T(8,128)S(1)}, f32[64,64]{0,1:T(8,128)S(1)}, u32[]{:S(2)}, u32[]{:S(2)}) collective-permute-start(f32[64,64]{0,1:T(8,128)S(1)} %add.370), channel_id=1, source_target_pairs={{0,16},{1,17},{2,18},{3,19},{4,20},{5,21},{6,22},{7,23},{8,24},{9,... | collective-permute-start | bytes 49160 | tf_op jit(solution)/shard_map/ppermute | solution.py:77

commit v5 on v3

--- a/solution.py
+++ b/solution.py
@@ -48,14 +48,21 @@
     return [c[margin:-margin, margin:-margin] for c in coefs]
 
 
-def allreduce(x, axes):
-    for axis in axes:
-        count = lax.axis_size(axis)
-        bit = 1
-        while bit < count:
-            x = x + lax.ppermute(x, axis, [(i, i ^ bit) for i in range(count)])
-            bit *= 2
+def butterfly(x, axis):
+    count = lax.axis_size(axis)
+    bit = 1
+    while bit < count:
+        x = x + lax.ppermute(x, axis, [(i, i ^ bit) for i in range(count)])
+        bit *= 2
     return x
+
+
+def allreduce(x):
+    count = lax.axis_size("gy")
+    parts = lax.all_to_all(x.reshape(count, -1), "gy", 0, 0, tiled=True)
+    mine = butterfly(parts.reshape(count, -1).sum(0), "gx")
+    full = lax.all_to_all(jnp.broadcast_to(mine, (count,) + mine.shape), "gy", 0, 0, tiled=True)
+    return full.reshape(x.shape)
 
 
 def per_device(right_side, initial_guess, coefficients):
@@ -106,7 +113,7 @@
     products = jnp.dot(stacked.T, stacked, precision=HIGH)
     products = jnp.where(same_z, products, 0.0)
     local_gram = jnp.dot(gather.T, jnp.dot(products, gather, precision=HIGH), precision=HIGH)
-    gram = allreduce(local_gram, ("gx", "gy"))
+    gram = allreduce(local_gram)
     shift_map = SHIFT * jnp.eye(blocks * RHS, STEPS * RHS, dtype=jnp.float32) + SCALE * jnp.eye(
         blocks * RHS, STEPS * RHS, k=-RHS, dtype=jnp.float32
     )

time: 127 us -> 124 us (0.976); the launches traced: 127 us -> 122 us
  blocking collectives: 0 us -> 16.5 us
  waiting for transfers between devices: 30.5 us -> 18.5 us
  starting transfers between devices: 59.6 us -> 48.5 us
    ppermute x9 -> x4, waiting for transfers between devices: 25.1 us -> 5.36 us  [butterfly(): x = x + lax.ppermute(x, axis, [(i, i ^ bit) for i in range(count)])]
    ppermute x9 -> x4, starting transfers between devices: 42.7 us -> 25.7 us  [butterfly(): x = x + lax.ppermute(x, axis, [(i, i ^ bit) for i in range(count)])]
    all_to_all x0 -> x1, blocking collectives: none -> 16.5 us  [allreduce(): parts = lax.all_to_all(x.reshape(count, -1), 'gy', 0, 0, tiled=True)]
    all_to_all x0 -> x1, waiting for transfers between devices: none -> 7.74 us  [allreduce(): lax.all_to_all(jnp.broadcast_to(mine, (count,) + mine.shape), 'gy', 0, 0,...]
    all_to_all x0 -> x1, starting transfers between devices: none -> 5.89 us  [allreduce(): lax.all_to_all(jnp.broadcast_to(mine, (count,) + mine.shape), 'gy', 0, 0,...]
  transfers between devices with their start and end apart: 13 -> 9, of which waited for: 12 -> 8; matrix products, arithmetic and copies ran while one was open for 2% -> 2% of each run, Pallas kernels for 0% -> 0%
where the time goes in v5:
time: 124 us; the launch traced here: 122 us
  starting transfers between devices  48.5 us (39%)
  waiting for transfers between devices  18.5 us (15%)
  other arithmetic  16.7 us (13%)
  blocking collectives  16.5 us (13%)
  local copies, waits for them, and re-layouts  10.7 us (9%)
  matrix products  9.9 us (8%)
    ppermute x4, starting transfers between devices, butterfly(): x = x + lax.ppermute(x, axis, [(i, i ^ bit) for i in range(count)])  25.7 us
    all_to_all x1, blocking collectives, allreduce(): parts = lax.all_to_all(x.reshape(count, -1), 'gy', 0, 0, tiled=True)  16.5 us
    ppermute x2, starting transfers between devices, exchange(): high = lax.ppermute(bottom, axis, backward)  10.1 us
    all_to_all x1, waiting for transfers between devices, allreduce(): lax.all_to_all(jnp.broadcast_to(mine, (count,) + mine.shape), 'gy', 0, 0,...  7.74 us
    ppermute x2, starting transfers between devices, exchange(): low = lax.ppermute(top, axis, forward)  6.76 us
    all_to_all x1, starting transfers between devices, allreduce(): lax.all_to_all(jnp.broadcast_to(mine, (count,) + mine.shape), 'gy', 0, 0,...  5.89 us
    ppermute x4, waiting for transfers between devices, butterfly(): x = x + lax.ppermute(x, axis, [(i, i ^ bit) for i in range(count)])  5.36 us
    another operation x3, other arithmetic, per_device(): factor = jnp.linalg.cholesky(normal)  5.05 us
  transfers between devices with their start and end apart: 9, of which 8 were waited for; matrix products, arithmetic and copies ran while one was open for 2% of the time, Pallas kernels for 0%

profile of v5, /device:TPU:6, one launch (start us, length us, event | category | flops | bytes accessed | tf_op | source)
XLA Modules:
  0.0 121.8 jit_solution(8302898554271947352)
XLA Ops:
  0.6 1.2 bitcast_dynamic-update-slice_fusion.1
  1.8 1.0 reshape.437
  3.3 0.9 fusion.118
  4.2 2.5 %collective-permute-start = (f32[4,16,1184]{2,1,0:T(8,128)}, f32[4,16,1184]{2,1,0:T(8,128)}, u32[]{:S(2)}, u32[]{:S(2)}) collective-permute-start(f32[4,16,1184]{2,1,0:T(8,128)} %get-tuple-element.8), channel_id=1, source_target_pairs={{0,32},{32,64},{64,96},{96,128},{128,160},{160,192},{192,224},{224... | collective-permute-start | bytes 909320 | tf_op jit(solution)/shard_map/ppermute | solution.py:23
  6.7 1.3 %collective-permute-start.1 = (f32[4,16,1184]{2,1,0:T(8,128)}, f32[4,16,1184]{2,1,0:T(8,128)}, u32[]{:S(2)}, u32[]{:S(2)}) collective-permute-start(f32[4,16,1184]{2,1,0:T(8,128)} %get-tuple-element.9), channel_id=1, source_target_pairs={{32,0},{64,32},{96,64},{128,96},{160,128},{192,160},{224,192},{256... | collective-permute-start | bytes 909320 | tf_op jit(solution)/shard_map/ppermute | solution.py:24
  8.2 0.4 broadcast_multiply_fusion
  8.6 1.8 %reshape.446 = f32[160,2560,1]{1,0,2:T(8,128)} reshape(f32[5,32,5,512]{3,2,1,0:T(8,128)S(1)} %broadcast_multiply_fusion) | data formatting | bytes 3276800 | tf_op jit(solution)/shard_map/jit(kron)/mul | solution.py:85
  10.4 0.8 collective-permute-done.1
  11.2 1.3 %pad_maximum_fusion.3 = (f32[16,4,1184]{2,1,0:T(4,128)S(1)}, f32[16,4,1184]{2,1,0:T(4,128)S(1)}) fusion(f32[4,16,1184]{2,1,0:T(8,128)} %collective-permute-done.1, f32[8,16,1184]{2,1,0:T(8,128)S(1)} %constant_dynamic-update-slice_fusion, f32[4,16,1184]{2,1,0:T(8,128)} %collective-permute-done), kind=kLoop, calls=%fused_computation.44 | loop fusion | flops 303104 | bytes 1818624 | tf_op jit(solution)/shard_map/slice | solution.py:21
  12.5 4.3 %collective-permute-start.2 = (f32[16,4,1184]{2,1,0:T(4,128)S(1)}, f32[16,4,1184]{2,1,0:T(4,128)S(1)}, u32[]{:S(2)}, u32[]{:S(2)}) collective-permute-start(f32[16,4,1184]{2,1,0:T(4,128)S(1)} %get-tuple-element.4), channel_id=1, source_target_pairs={{0,1},{1,2},{2,3},{3,4},{4,5},{5,6},{6,7},{7,8},{8,9},{9,10},{10,1... | collective-permute-start | bytes 909320 | tf_op jit(solution)/shard_map/ppermute | solution.py:23
  16.8 8.9 %collective-permute-start.3 = (f32[16,4,1184]{2,1,0:T(4,128)S(1)}, f32[16,4,1184]{2,1,0:T(4,128)S(1)}, u32[]{:S(2)}, u32[]{:S(2)}) collective-permute-start(f32[16,4,1184]{2,1,0:T(4,128)S(1)} %get-tuple-element.5), channel_id=1, source_target_pairs={{1,0},{2,1},{3,2},{4,3},{5,4},{6,5},{7,6},{8,7},{9,8},{10,9},{11,1... | collective-permute-start | bytes 909320 | tf_op jit(solution)/shard_map/ppermute | solution.py:24
  25.7 3.1 %collective-permute-done.2 = f32[16,4,1184]{2,1,0:T(4,128)S(1)} collective-permute-done((f32[16,4,1184]{2,1,0:T(4,128)S(1)}, f32[16,4,1184]{2,1,0:T(4,128)S(1)}, u32[]{:S(2)}, u32[]{:S(2)}) %collective-permute-start.2) | collective-permute-done | bytes 303136 | tf_op jit(solution)/shard_map/ppermute | solution.py:23
  28.7 1.5 %collective-permute-done.3 = f32[16,4,1184]{2,1,0:T(4,128)S(1)} collective-permute-done((f32[16,4,1184]{2,1,0:T(4,128)S(1)}, f32[16,4,1184]{2,1,0:T(4,128)S(1)}, u32[]{:S(2)}, u32[]{:S(2)}) %collective-permute-start.3) | collective-permute-done | bytes 303136 | tf_op jit(solution)/shard_map/ppermute | solution.py:24
  30.2 1.4 %pad_maximum_fusion = f32[16,24,1184]{2,1,0:T(8,128)S(1)} fusion(f32[16,4,1184]{2,1,0:T(4,128)S(1)} %collective-permute-done.3, f32[4,16,1184]{2,1,0:T(8,128)} %collective-permute-done.1, f32[8,16,1184]{2,1,0:T(8,128)S(1)} %constant_dynamic-update-slice_fusion, f32[4,16,1184]{2,1,0:T(8,128)} %collective-permute-done, f32[16,4,1184]{2,1,0:T(4,128)S(1)} %collective-permute-done.2), kind=kLoop, calls=%fused_computation | loop fusion | flops 1818624 | bytes 3637248 | tf_op jit(solution)/shard_map/concatenate | solution.py:25
  31.6 0.3 fusion.116
  31.9 1.1 copy-done
  33.0 3.5 %fusion.22 = f32[16,24,2560]{2,1,0:T(8,128)S(1)} fusion(f32[160,2560,1]{1,0,2:T(8,128)S(1)} %copy-done, f32[16,24,1184]{2,1,0:T(8,128)S(1)} %pad_maximum_fusion), kind=kOutput, calls=%fused_computation.40 | convolution fusion | flops 1887436800 | bytes 5963776 | tf_op jit(solution)/shard_map/dot_general | solution.py:86
  36.5 1.1 fusion.3
  37.9 1.0 fusion.10
  39.2 0.8 fusion.18
  40.2 0.4 fusion.28
  40.9 1.9 %convolution_select_fusion = f32[512,512]{1,0:T(8,128)S(1)} fusion(f32[512,512]{1,0:T(8,128)S(1)} %constant_dynamic-update-slice_fusion.1, s32[512]{0:T(512)S(1)} %add_select_fusion.2), kind=kOutput, calls=%fused_computation.1 | convolution fusion | flops 1611137024 | bytes 2099200 | tf_op jit(solution)/shard_map/dot_general | solution.py:113
  42.8 0.8 fusion.34
  43.6 0.5 fusion.35
  44.1 16.5 %all_to_all.15 = f32[32,1,128]{2,1,0:T(1,128)S(1)} all-to-all(f32[32,1,128]{2,1,0:T(1,128)S(1)} %bitcast.39), channel_id=1, replica_groups=mesh['gx'=16,'gy'=32] {'gy'}, dimensions={0} | all-to-all | bytes 32768 | tf_op jit(solution)/shard_map/all_to_all | solution.py:62
  60.6 4.7 %collective-permute-start.4 = (f32[128]{0:T(128)S(1)}, f32[128]{0:T(128)S(1)}, u32[]{:S(2)}, u32[]{:S(2)}) collective-permute-start(f32[128]{0:T(128)S(1)} %reduce_sum.9), channel_id=1, source_target_pairs={{0,32},{32,0},{64,96},{96,64},{128,160},{160,128},{192,224},{224,1... | collective-permute-start | bytes 1544 | tf_op jit(solution)/shard_map/ppermute | solution.py:55
  65.3 0.8 collective-permute-done.4
  66.1 7.2 %collective-permute-start.5 = (f32[128]{0:T(128)S(1)}, f32[128]{0:T(128)S(1)}, u32[]{:S(2)}, u32[]{:S(2)}) collective-permute-start(f32[128]{0:T(128)S(1)} %add.348), channel_id=1, source_target_pairs={{0,64},{32,96},{64,0},{96,32},{128,192},{160,224},{192,128},{224,1... | collective-permute-start | bytes 1544 | tf_op jit(solution)/shard_map/ppermute | solution.py:55
  73.3 1.5 %collective-permute-done.5 = f32[128]{0:T(128)S(1)} collective-permute-done((f32[128]{0:T(128)S(1)}, f32[128]{0:T(128)S(1)}, u32[]{:S(2)}, u32[]{:S(2)}) %collective-permute-start.5) | collective-permute-done | bytes 544 | tf_op jit(solution)/shard_map/ppermute | solution.py:55
  74.8 4.9 %collective-permute-start.6 = (f32[128]{0:T(128)S(1)}, f32[128]{0:T(128)S(1)}, u32[]{:S(2)}, u32[]{:S(2)}) collective-permute-start(f32[128]{0:T(128)S(1)} %add.349), channel_id=1, source_target_pairs={{0,128},{32,160},{64,192},{96,224},{128,0},{160,32},{192,64},{224,... | collective-permute-start | bytes 1544 | tf_op jit(solution)/shard_map/ppermute | solution.py:55
  79.8 1.5 %collective-permute-done.6 = f32[128]{0:T(128)S(1)} collective-permute-done((f32[128]{0:T(128)S(1)}, f32[128]{0:T(128)S(1)}, u32[]{:S(2)}, u32[]{:S(2)}) %collective-permute-start.6) | collective-permute-done | bytes 544 | tf_op jit(solution)/shard_map/ppermute | solution.py:55
  81.3 8.9 %collective-permute-start.7 = (f32[128]{0:T(128)S(1)}, f32[128]{0:T(128)S(1)}, u32[]{:S(2)}, u32[]{:S(2)}) collective-permute-start(f32[128]{0:T(128)S(1)} %add.350), channel_id=1, source_target_pairs={{0,256},{32,288},{64,320},{96,352},{128,384},{160,416},{192,448},{... | collective-permute-start | bytes 1544 | tf_op jit(solution)/shard_map/ppermute | solution.py:55
  90.2 1.5 %collective-permute-done.7 = f32[128]{0:T(128)S(1)} collective-permute-done((f32[128]{0:T(128)S(1)}, f32[128]{0:T(128)S(1)}, u32[]{:S(2)}, u32[]{:S(2)}) %collective-permute-start.7) | collective-permute-done | bytes 544 | tf_op jit(solution)/shard_map/ppermute | solution.py:55
  91.7 0.6 broadcast_in_dim.18
  92.4 5.9 %all-to-all-start.1 = ((f32[32,1,128]{2,1,0:T(1,128)}), f32[32,1,128]{2,1,0:T(1,128)S(1)}, u32[]{:S(2)}, u32[]{:S(2)}) async-start(f32[32,1,128]{2,1,0:T(1,128)} %broadcast_in_dim.18), calls=%async_computation.1 | async-start | bytes 32768 | tf_op jit(solution)/shard_map/all_to_all | solution.py:64
  98.3 7.7 %all-to-all-done.1 = f32[32,1,128]{2,1,0:T(1,128)S(1)} async-done(((f32[32,1,128]{2,1,0:T(1,128)}), f32[32,1,128]{2,1,0:T(1,128)S(1)}, u32[]{:S(2)}, u32[]{:S(2)}) %all-to-all-start.1) | async-done | bytes 16416 | tf_op jit(solution)/shard_map/all_to_all | solution.py:64
  106.1 0.5 broadcast.565
  106.6 0.7 reduce.10
  107.9 0.3 fusion.59
  108.3 4.4 %cholesky.16 = f32[48,48]{1,0:T(8,128)S(1)} custom-call(f32[48,48]{1,0:T(8,128)S(1)} %fusion.66), custom_call_target="Cholesky" | custom-call | tf_op jit(solution)/shard_map/jit(cholesky)/cholesky | solution.py:126
  112.7 0.6 compare_reduce_fusion
  113.4 0.7 fusion.61
  114.0 3.7 %custom-call.10 = f32[1,48,48]{1,2,0:T(8,128)S(1)} custom-call(f32[1,48,48]{2,1,0:T(8,128)S(1)} %fusion.61), custom_call_target="InvertDiagBlocksLowerTriangular" | custom-call | tf_op jit(solution)/shard_map/jit(_cho_solve)/triangular_solve | solution.py:127
  118.2 0.4 fusion.32
  118.7 0.5 convolution_select_fusion.1
  119.2 1.0 fusion.121
  120.3 0.8 reshape.444
  121.0 0.8 reshape.445
  (51 shorter events, 3.1 us)
Async XLA Ops:
  0.6 2.5 %copy-start.2 = (f32[8,8192]{1,0:T(8,128)S(1)}, f32[8,8192]{1,0:T(8,128)}, u32[]{:S(2)}) copy-start(f32[8,8192]{1,0:T(8,128)} %param.3) | copy-start | bytes 786436
  4.2 6.1 %collective-permute-start = (f32[4,16,1184]{2,1,0:T(8,128)}, f32[4,16,1184]{2,1,0:T(8,128)}, u32[]{:S(2)}, u32[]{:S(2)}) collective-permute-start(f32[4,16,1184]{2,1,0:T(8,128)} %get-tuple-element.8), channel_id=1, source_target_pairs={{0,32},{32,64},{64,96},{96,128},{128,160},{160,192},{192,224},{224... | collective-permute-start | bytes 909320 | tf_op jit(solution)/shard_map/ppermute | solution.py:23
  6.7 4.5 %collective-permute-start.1 = (f32[4,16,1184]{2,1,0:T(8,128)}, f32[4,16,1184]{2,1,0:T(8,128)}, u32[]{:S(2)}, u32[]{:S(2)}) collective-permute-start(f32[4,16,1184]{2,1,0:T(8,128)} %get-tuple-element.9), channel_id=1, source_target_pairs={{32,0},{64,32},{96,64},{128,96},{160,128},{192,160},{224,192},{256... | collective-permute-start | bytes 909320 | tf_op jit(solution)/shard_map/ppermute | solution.py:24
  12.5 16.3 %collective-permute-start.2 = (f32[16,4,1184]{2,1,0:T(4,128)S(1)}, f32[16,4,1184]{2,1,0:T(4,128)S(1)}, u32[]{:S(2)}, u32[]{:S(2)}) collective-permute-start(f32[16,4,1184]{2,1,0:T(4,128)S(1)} %get-tuple-element.4), channel_id=1, source_target_pairs={{0,1},{1,2},{2,3},{3,4},{4,5},{5,6},{6,7},{7,8},{8,9},{9,10},{10,1... | collective-permute-start | bytes 909320 | tf_op jit(solution)/shard_map/ppermute | solution.py:23
  16.8 13.4 %collective-permute-start.3 = (f32[16,4,1184]{2,1,0:T(4,128)S(1)}, f32[16,4,1184]{2,1,0:T(4,128)S(1)}, u32[]{:S(2)}, u32[]{:S(2)}) collective-permute-start(f32[16,4,1184]{2,1,0:T(4,128)S(1)} %get-tuple-element.5), channel_id=1, source_target_pairs={{1,0},{2,1},{3,2},{4,3},{5,4},{6,5},{7,6},{8,7},{9,8},{10,9},{11,1... | collective-permute-start | bytes 909320 | tf_op jit(solution)/shard_map/ppermute | solution.py:24
  31.6 1.4 %copy-start = (f32[160,2560,1]{1,0,2:T(8,128)S(1)}, f32[160,2560,1]{1,0,2:T(8,128)}, u32[]{:S(2)}) copy-start(f32[160,2560,1]{1,0,2:T(8,128)} %reshape.446) | copy-start | bytes 4915204
  40.9 57.4 %copy-start.1 = (f32[8,8192]{1,0:T(8,128)S(1)}, f32[8,8192]{1,0:T(8,128)}, u32[]{:S(2)}) copy-start(f32[8,8192]{1,0:T(8,128)} %param.4) | copy-start | bytes 786436
  60.6 5.5 %collective-permute-start.4 = (f32[128]{0:T(128)S(1)}, f32[128]{0:T(128)S(1)}, u32[]{:S(2)}, u32[]{:S(2)}) collective-permute-start(f32[128]{0:T(128)S(1)} %reduce_sum.9), channel_id=1, source_target_pairs={{0,32},{32,0},{64,96},{96,64},{128,160},{160,128},{192,224},{224,1... | collective-permute-start | bytes 1544 | tf_op jit(solution)/shard_map/ppermute | solution.py:55
  66.1 8.7 %collective-permute-start.5 = (f32[128]{0:T(128)S(1)}, f32[128]{0:T(128)S(1)}, u32[]{:S(2)}, u32[]{:S(2)}) collective-permute-start(f32[128]{0:T(128)S(1)} %add.348), channel_id=1, source_target_pairs={{0,64},{32,96},{64,0},{96,32},{128,192},{160,224},{192,128},{224,1... | collective-permute-start | bytes 1544 | tf_op jit(solution)/shard_map/ppermute | solution.py:55
  74.8 6.5 %collective-permute-start.6 = (f32[128]{0:T(128)S(1)}, f32[128]{0:T(128)S(1)}, u32[]{:S(2)}, u32[]{:S(2)}) collective-permute-start(f32[128]{0:T(128)S(1)} %add.349), channel_id=1, source_target_pairs={{0,128},{32,160},{64,192},{96,224},{128,0},{160,32},{192,64},{224,... | collective-permute-start | bytes 1544 | tf_op jit(solution)/shard_map/ppermute | solution.py:55
  81.3 10.5 %collective-permute-start.7 = (f32[128]{0:T(128)S(1)}, f32[128]{0:T(128)S(1)}, u32[]{:S(2)}, u32[]{:S(2)}) collective-permute-start(f32[128]{0:T(128)S(1)} %add.350), channel_id=1, source_target_pairs={{0,256},{32,288},{64,320},{96,352},{128,384},{160,416},{192,448},{... | collective-permute-start | bytes 1544 | tf_op jit(solution)/shard_map/ppermute | solution.py:55
  92.4 13.7 %all-to-all-start.1 = ((f32[32,1,128]{2,1,0:T(1,128)}), f32[32,1,128]{2,1,0:T(1,128)S(1)}, u32[]{:S(2)}, u32[]{:S(2)}) async-start(f32[32,1,128]{2,1,0:T(1,128)} %broadcast_in_dim.18), calls=%async_computation.1 | async-start | bytes 32768 | tf_op jit(solution)/shard_map/all_to_all | solution.py:64

commit v6 on v5

--- a/solution.py
+++ b/solution.py
@@ -14,15 +14,26 @@
 HIGH = lax.Precision.HIGHEST
 
 
-def exchange(block, axis, dim, width):
+def shift(part, axis, forward):
     count = lax.axis_size(axis)
-    forward = [(i, i + 1) for i in range(count - 1)]
-    backward = [(i + 1, i) for i in range(count - 1)]
-    top = lax.slice_in_dim(block, block.shape[dim] - width, None, axis=dim)
-    bottom = lax.slice_in_dim(block, 0, width, axis=dim)
-    low = lax.ppermute(top, axis, forward)
-    high = lax.ppermute(bottom, axis, backward)
-    return jnp.concatenate([low, block, high], axis=dim)
+    if forward:
+        pairs = [(i, i + 1) for i in range(count - 1)]
+    else:
+        pairs = [(i + 1, i) for i in range(count - 1)]
+    return lax.ppermute(part, axis, pairs)
+
+
+def exchange(block, w):
+    x_lo = shift(block[-w:], "gx", True)
+    x_hi = shift(block[:w], "gx", False)
+    y_lo = shift(block[:, -w:], "gy", True)
+    y_hi = shift(block[:, :w], "gy", False)
+    corner_lo = shift(jnp.concatenate([x_lo[:, -w:], x_hi[:, -w:]], axis=0), "gy", True)
+    corner_hi = shift(jnp.concatenate([x_lo[:, :w], x_hi[:, :w]], axis=0), "gy", False)
+    rows_lo = jnp.concatenate([corner_lo[:w], x_lo, corner_hi[:w]], axis=1)
+    rows_mid = jnp.concatenate([y_lo, block, y_hi], axis=1)
+    rows_hi = jnp.concatenate([corner_lo[w:], x_hi, corner_hi[w:]], axis=1)
+    return jnp.concatenate([rows_lo, rows_mid, rows_hi], axis=0)
 
 
 def operate(padded, coefs):
@@ -76,8 +87,7 @@
         rows_x, rows_y, 5 * NZ
     )
     packed = jnp.concatenate([guess, rhs_field, coef], axis=2)
-    packed = exchange(packed, "gx", 0, depth)
-    packed = exchange(packed, "gy", 1, depth)
+    packed = exchange(packed, depth)
     ex, ey = packed.shape[0], packed.shape[1]
     guess_e = packed[:, :, :width]
     rhs_e = packed[1:-1, 1:-1, width : 2 * width]

time: 124 us -> 128 us (1.032)
  local copies, waits for them, and re-layouts: 10.7 us -> 13.5 us
  starting transfers between devices: 48.5 us -> 50.8 us
    ppermute x4 -> x6, starting transfers between devices: 16.9 us -> 25 us  [shift(): return lax.ppermute(part, axis, pairs)]
    ppermute x4, starting transfers between devices: 25.7 us -> 19.9 us  [butterfly(): x = x + lax.ppermute(x, axis, [(i, i ^ bit) for i in range(count)])]
    slice x1 -> x6, local copies, waits for them, and re-layouts: 0.89 us -> 3.7 us  [the longest x1 1.03 us: exchange(): x_lo[:, -w:]]
    ppermute x4 -> x6, waiting for transfers between devices: 5.37 us -> 4.14 us  [shift(): return lax.ppermute(part, axis, pairs)]
  transfers between devices with their start and end apart: 9 -> 11, of which waited for: 8 -> 7; matrix products, arithmetic and copies ran while one was open for 2% -> 4% of each run, Pallas kernels for 0% -> 0%
where the time goes in v6:
time: 128 us; the launch traced here: 125 us
  starting transfers between devices  50.8 us (40%)
  waiting for transfers between devices  17.6 us (14%)
  blocking collectives  16.5 us (13%)
  other arithmetic  15.7 us (12%)
  local copies, waits for them, and re-layouts  13.5 us (11%)
  matrix products  9.9 us (8%)
    ppermute x6, starting transfers between devices, shift(): return lax.ppermute(part, axis, pairs)  25 us
    ppermute x4, starting transfers between devices, butterfly(): x = x + lax.ppermute(x, axis, [(i, i ^ bit) for i in range(count)])  19.9 us
    all_to_all x1, blocking collectives, allreduce(): parts = lax.all_to_all(x.reshape(count, -1), 'gy', 0, 0, tiled=True)  16.5 us
    all_to_all x1, waiting for transfers between devices, allreduce(): lax.all_to_all(jnp.broadcast_to(mine, (count,) + mine.shape), 'gy', 0, 0,...  7.74 us
    all_to_all x1, starting transfers between devices, allreduce(): lax.all_to_all(jnp.broadcast_to(mine, (count,) + mine.shape), 'gy', 0, 0,...  5.93 us
    ppermute x4, waiting for transfers between devices, butterfly(): x = x + lax.ppermute(x, axis, [(i, i ^ bit) for i in range(count)])  5.69 us
    another operation x3, other arithmetic, per_device(): factor = jnp.linalg.cholesky(normal)  5.05 us
    another operation x2, other arithmetic, per_device(): weights = jax.scipy.linalg.cho_solve((factor, True), target)  4.32 us
  transfers between devices with their start and end apart: 11, of which 7 were waited for; matrix products, arithmetic and copies ran while one was open for 4% of the time, Pallas kernels for 0%

profile of v6, /device:TPU:6, one launch (start us, length us, event | category | flops | bytes accessed | tf_op | source)
XLA Modules:
  0.0 125.1 jit_solution(7091066379279500349)
XLA Ops:
  0.6 1.2 bitcast_dynamic-update-slice_fusion.1
  1.8 1.0 reshape.437
  3.3 0.9 fusion.119
  4.2 2.5 %collective-permute-start = (f32[4,16,1184]{2,1,0:T(8,128)}, f32[4,16,1184]{2,1,0:T(8,128)}, u32[]{:S(2)}, u32[]{:S(2)}) collective-permute-start(f32[4,16,1184]{2,1,0:T(8,128)} %get-tuple-element.8), channel_id=1, source_target_pairs={{0,32},{32,64},{64,96},{96,128},{128,160},{160,192},{192,224},{224... | collective-permute-start | bytes 909320 | tf_op jit(solution)/shard_map/ppermute | solution.py:23
  6.7 1.3 %collective-permute-start.1 = (f32[4,16,1184]{2,1,0:T(8,128)}, f32[4,16,1184]{2,1,0:T(8,128)}, u32[]{:S(2)}, u32[]{:S(2)}) collective-permute-start(f32[4,16,1184]{2,1,0:T(8,128)} %get-tuple-element.9), channel_id=1, source_target_pairs={{32,0},{64,32},{96,64},{128,96},{160,128},{192,160},{224,192},{256... | collective-permute-start | bytes 909320 | tf_op jit(solution)/shard_map/ppermute | solution.py:23
  8.0 0.7 fusion.118
  8.7 4.3 %collective-permute-start.4 = (f32[8,4,1184]{2,1,0:T(4,128)}, f32[8,4,1184]{2,1,0:T(4,128)}, u32[]{:S(2)}, u32[]{:S(2)}) collective-permute-start(f32[8,4,1184]{2,1,0:T(4,128)} %get-tuple-element.6), channel_id=1, source_target_pairs={{0,1},{1,2},{2,3},{3,4},{4,5},{5,6},{6,7},{7,8},{8,9},{9,10},{10,1... | collective-permute-start | bytes 454664 | tf_op jit(solution)/shard_map/ppermute | solution.py:23
  13.0 8.9 %collective-permute-start.5 = (f32[8,4,1184]{2,1,0:T(4,128)S(1)}, f32[8,4,1184]{2,1,0:T(4,128)}, u32[]{:S(2)}, u32[]{:S(2)}) collective-permute-start(f32[8,4,1184]{2,1,0:T(4,128)S(1)} %get-tuple-element.7), channel_id=1, source_target_pairs={{1,0},{2,1},{3,2},{4,3},{5,4},{6,5},{7,6},{8,7},{9,8},{10,9},{11,1... | collective-permute-start | bytes 454664 | tf_op jit(solution)/shard_map/ppermute | solution.py:23
  22.4 1.8 %reshape.446 = f32[160,2560,1]{1,0,2:T(8,128)} reshape(f32[5,32,5,512]{3,2,1,0:T(8,128)S(1)} %broadcast_multiply_fusion) | data formatting | bytes 3276800 | tf_op jit(solution)/shard_map/jit(kron)/mul | solution.py:95
  24.3 1.0 fusion.122
  25.3 1.0 fusion.123
  26.4 1.9 %collective-permute-start.2 = (f32[8,4,1184]{2,1,0:T(4,128)S(1)}, f32[8,4,1184]{2,1,0:T(4,128)S(1)}, u32[]{:S(2)}, u32[]{:S(2)}) collective-permute-start(f32[8,4,1184]{2,1,0:T(4,128)S(1)} %pad_maximum_fusion), channel_id=1, source_target_pairs={{0,1},{1,2},{2,3},{3,4},{4,5},{5,6},{6,7},{7,8},{8,9},{9,10},{10,1... | collective-permute-start | bytes 454664 | tf_op jit(solution)/shard_map/ppermute | solution.py:23
  28.4 6.2 %collective-permute-start.3 = (f32[8,4,1184]{2,1,0:T(4,128)S(1)}, f32[8,4,1184]{2,1,0:T(4,128)S(1)}, u32[]{:S(2)}, u32[]{:S(2)}) collective-permute-start(f32[8,4,1184]{2,1,0:T(4,128)S(1)} %pad_maximum_fusion.1), channel_id=1, source_target_pairs={{1,0},{2,1},{3,2},{4,3},{5,4},{6,5},{7,6},{8,7},{9,8},{10,9},{11,1... | collective-permute-start | bytes 454664 | tf_op jit(solution)/shard_map/ppermute | solution.py:23
  34.6 2.4 %collective-permute-done.2 = f32[8,4,1184]{2,1,0:T(4,128)S(1)} collective-permute-done((f32[8,4,1184]{2,1,0:T(4,128)S(1)}, f32[8,4,1184]{2,1,0:T(4,128)S(1)}, u32[]{:S(2)}, u32[]{:S(2)}) %collective-permute-start.2) | collective-permute-done | bytes 151584 | tf_op jit(solution)/shard_map/ppermute | solution.py:23
  37.0 1.8 %collective-permute-done.3 = f32[8,4,1184]{2,1,0:T(4,128)S(1)} collective-permute-done((f32[8,4,1184]{2,1,0:T(4,128)S(1)}, f32[8,4,1184]{2,1,0:T(4,128)S(1)}, u32[]{:S(2)}, u32[]{:S(2)}) %collective-permute-start.3) | collective-permute-done | bytes 151584 | tf_op jit(solution)/shard_map/ppermute | solution.py:23
  38.8 1.5 %maximum_maximum_fusion = f32[16,24,1184]{2,1,0:T(8,128)S(1)} fusion(f32[4,4,1184]{2,1,0:T(4,128)S(1)} %get-tuple-element.25, f32[4,16,1184]{2,1,0:T(8,128)} %collective-permute-done.1, f32[4,4,1184]{2,1,0:T(4,128)S(1)} %get-tuple-element.23, f32[8,4,1184]{2,1,0:T(4,128)} %collective-permute-done.5, f32[8,16,1184]{2,1,0:T(8,128)S(1)} %constant_dynamic-update-slice_fusion, ...), kind=kLoop, calls=%fused_computation | loop fusion | flops 3637248 | bytes 3637248 | tf_op jit(solution)/shard_map/concatenate | solution.py:36
  40.6 1.1 copy-done
  41.7 3.5 %fusion.22 = f32[16,24,2560]{2,1,0:T(8,128)S(1)} fusion(f32[160,2560,1]{1,0,2:T(8,128)S(1)} %copy-done, f32[16,24,1184]{2,1,0:T(8,128)S(1)} %maximum_maximum_fusion), kind=kOutput, calls=%fused_computation.40 | convolution fusion | flops 1887436800 | bytes 5963776 | tf_op jit(solution)/shard_map/dot_general | solution.py:96
  45.2 1.1 fusion.3
  46.6 1.0 fusion.10
  48.0 0.8 fusion.18
  48.9 0.4 fusion.28
  49.6 1.9 %convolution_select_fusion = f32[512,512]{1,0:T(8,128)S(1)} fusion(f32[512,512]{1,0:T(8,128)S(1)} %constant_dynamic-update-slice_fusion.1, s32[512]{0:T(512)S(1)} %add_select_fusion.2), kind=kOutput, calls=%fused_computation.1 | convolution fusion | flops 1611137024 | bytes 2099200 | tf_op jit(solution)/shard_map/dot_general | solution.py:123
  51.5 0.8 fusion.34
  52.3 0.4 fusion.35
  52.9 16.5 %all_to_all.15 = f32[32,1,128]{2,1,0:T(1,128)S(1)} all-to-all(f32[32,1,128]{2,1,0:T(1,128)S(1)} %bitcast.39), channel_id=1, replica_groups=mesh['gx'=16,'gy'=32] {'gy'}, dimensions={0} | all-to-all | bytes 32768 | tf_op jit(solution)/shard_map/all_to_all | solution.py:73
  69.4 1.9 %collective-permute-start.6 = (f32[128]{0:T(128)S(1)}, f32[128]{0:T(128)S(1)}, u32[]{:S(2)}, u32[]{:S(2)}) collective-permute-start(f32[128]{0:T(128)S(1)} %reduce_sum.9), channel_id=1, source_target_pairs={{0,32},{32,0},{64,96},{96,64},{128,160},{160,128},{192,224},{224,1... | collective-permute-start | bytes 1544 | tf_op jit(solution)/shard_map/ppermute | solution.py:66
  71.3 1.1 collective-permute-done.6
  72.4 4.0 %collective-permute-start.7 = (f32[128]{0:T(128)S(1)}, f32[128]{0:T(128)S(1)}, u32[]{:S(2)}, u32[]{:S(2)}) collective-permute-start(f32[128]{0:T(128)S(1)} %add.348), channel_id=1, source_target_pairs={{0,64},{32,96},{64,0},{96,32},{128,192},{160,224},{192,128},{224,1... | collective-permute-start | bytes 1544 | tf_op jit(solution)/shard_map/ppermute | solution.py:66
  76.4 1.5 %collective-permute-done.7 = f32[128]{0:T(128)S(1)} collective-permute-done((f32[128]{0:T(128)S(1)}, f32[128]{0:T(128)S(1)}, u32[]{:S(2)}, u32[]{:S(2)}) %collective-permute-start.7) | collective-permute-done | bytes 544 | tf_op jit(solution)/shard_map/ppermute | solution.py:66
  77.9 5.7 %collective-permute-start.8 = (f32[128]{0:T(128)S(1)}, f32[128]{0:T(128)S(1)}, u32[]{:S(2)}, u32[]{:S(2)}) collective-permute-start(f32[128]{0:T(128)S(1)} %add.349), channel_id=1, source_target_pairs={{0,128},{32,160},{64,192},{96,224},{128,0},{160,32},{192,64},{224,... | collective-permute-start | bytes 1544 | tf_op jit(solution)/shard_map/ppermute | solution.py:66
  83.6 1.5 %collective-permute-done.8 = f32[128]{0:T(128)S(1)} collective-permute-done((f32[128]{0:T(128)S(1)}, f32[128]{0:T(128)S(1)}, u32[]{:S(2)}, u32[]{:S(2)}) %collective-permute-start.8) | collective-permute-done | bytes 544 | tf_op jit(solution)/shard_map/ppermute | solution.py:66
  85.2 8.3 %collective-permute-start.9 = (f32[128]{0:T(128)S(1)}, f32[128]{0:T(128)S(1)}, u32[]{:S(2)}, u32[]{:S(2)}) collective-permute-start(f32[128]{0:T(128)S(1)} %add.350), channel_id=1, source_target_pairs={{0,256},{32,288},{64,320},{96,352},{128,384},{160,416},{192,448},{... | collective-permute-start | bytes 1544 | tf_op jit(solution)/shard_map/ppermute | solution.py:66
  93.5 1.5 %collective-permute-done.9 = f32[128]{0:T(128)S(1)} collective-permute-done((f32[128]{0:T(128)S(1)}, f32[128]{0:T(128)S(1)}, u32[]{:S(2)}, u32[]{:S(2)}) %collective-permute-start.9) | collective-permute-done | bytes 544 | tf_op jit(solution)/shard_map/ppermute | solution.py:66
  95.0 0.6 broadcast_in_dim.18
  95.6 5.9 %all-to-all-start.1 = ((f32[32,1,128]{2,1,0:T(1,128)}), f32[32,1,128]{2,1,0:T(1,128)S(1)}, u32[]{:S(2)}, u32[]{:S(2)}) async-start(f32[32,1,128]{2,1,0:T(1,128)} %broadcast_in_dim.18), calls=%async_computation.1 | async-start | bytes 32768 | tf_op jit(solution)/shard_map/all_to_all | solution.py:75
  101.6 7.7 %all-to-all-done.1 = f32[32,1,128]{2,1,0:T(1,128)S(1)} async-done(((f32[32,1,128]{2,1,0:T(1,128)}), f32[32,1,128]{2,1,0:T(1,128)S(1)}, u32[]{:S(2)}, u32[]{:S(2)}) %all-to-all-start.1) | async-done | bytes 16416 | tf_op jit(solution)/shard_map/all_to_all | solution.py:75
  109.4 0.5 broadcast.565
  109.9 0.7 reduce.10
  111.6 4.4 %cholesky.16 = f32[48,48]{1,0:T(8,128)S(1)} custom-call(f32[48,48]{1,0:T(8,128)S(1)} %fusion.66), custom_call_target="Cholesky" | custom-call | tf_op jit(solution)/shard_map/jit(cholesky)/cholesky | solution.py:136
  116.0 0.6 compare_reduce_fusion
  116.6 0.7 fusion.61
  117.3 3.7 %custom-call.10 = f32[1,48,48]{1,2,0:T(8,128)S(1)} custom-call(f32[1,48,48]{2,1,0:T(8,128)S(1)} %fusion.61), custom_call_target="InvertDiagBlocksLowerTriangular" | custom-call | tf_op jit(solution)/shard_map/jit(_cho_solve)/triangular_solve | solution.py:137
  121.5 0.4 fusion.32
  122.0 0.5 convolution_select_fusion.1
  122.5 1.0 fusion.126
  123.5 0.8 reshape.444
  124.3 0.8 reshape.445
  (61 shorter events, 4.2 us)
Async XLA Ops:
  0.6 2.5 %copy-start.2 = (f32[8,8192]{1,0:T(8,128)S(1)}, f32[8,8192]{1,0:T(8,128)}, u32[]{:S(2)}) copy-start(f32[8,8192]{1,0:T(8,128)} %param.3) | copy-start | bytes 786436
  4.2 20.0 %collective-permute-start = (f32[4,16,1184]{2,1,0:T(8,128)}, f32[4,16,1184]{2,1,0:T(8,128)}, u32[]{:S(2)}, u32[]{:S(2)}) collective-permute-start(f32[4,16,1184]{2,1,0:T(8,128)} %get-tuple-element.8), channel_id=1, source_target_pairs={{0,32},{32,64},{64,96},{96,128},{128,160},{160,192},{192,224},{224... | collective-permute-start | bytes 909320 | tf_op jit(solution)/shard_map/ppermute | solution.py:23
  6.7 18.6 %collective-permute-start.1 = (f32[4,16,1184]{2,1,0:T(8,128)}, f32[4,16,1184]{2,1,0:T(8,128)}, u32[]{:S(2)}, u32[]{:S(2)}) collective-permute-start(f32[4,16,1184]{2,1,0:T(8,128)} %get-tuple-element.9), channel_id=1, source_target_pairs={{32,0},{64,32},{96,64},{128,96},{160,128},{192,160},{224,192},{256... | collective-permute-start | bytes 909320 | tf_op jit(solution)/shard_map/ppermute | solution.py:23
  8.7 30.0 %collective-permute-start.4 = (f32[8,4,1184]{2,1,0:T(4,128)}, f32[8,4,1184]{2,1,0:T(4,128)}, u32[]{:S(2)}, u32[]{:S(2)}) collective-permute-start(f32[8,4,1184]{2,1,0:T(4,128)} %get-tuple-element.6), channel_id=1, source_target_pairs={{0,1},{1,2},{2,3},{3,4},{4,5},{5,6},{6,7},{7,8},{8,9},{9,10},{10,1... | collective-permute-start | bytes 454664 | tf_op jit(solution)/shard_map/ppermute | solution.py:23
  13.0 25.8 %collective-permute-start.5 = (f32[8,4,1184]{2,1,0:T(4,128)S(1)}, f32[8,4,1184]{2,1,0:T(4,128)}, u32[]{:S(2)}, u32[]{:S(2)}) collective-permute-start(f32[8,4,1184]{2,1,0:T(4,128)S(1)} %get-tuple-element.7), channel_id=1, source_target_pairs={{1,0},{2,1},{3,2},{4,3},{5,4},{6,5},{7,6},{8,7},{9,8},{10,9},{11,1... | collective-permute-start | bytes 454664 | tf_op jit(solution)/shard_map/ppermute | solution.py:23
  26.4 10.6 %collective-permute-start.2 = (f32[8,4,1184]{2,1,0:T(4,128)S(1)}, f32[8,4,1184]{2,1,0:T(4,128)S(1)}, u32[]{:S(2)}, u32[]{:S(2)}) collective-permute-start(f32[8,4,1184]{2,1,0:T(4,128)S(1)} %pad_maximum_fusion), channel_id=1, source_target_pairs={{0,1},{1,2},{2,3},{3,4},{4,5},{5,6},{6,7},{7,8},{8,9},{9,10},{10,1... | collective-permute-start | bytes 454664 | tf_op jit(solution)/shard_map/ppermute | solution.py:23
  28.4 10.4 %collective-permute-start.3 = (f32[8,4,1184]{2,1,0:T(4,128)S(1)}, f32[8,4,1184]{2,1,0:T(4,128)S(1)}, u32[]{:S(2)}, u32[]{:S(2)}) collective-permute-start(f32[8,4,1184]{2,1,0:T(4,128)S(1)} %pad_maximum_fusion.1), channel_id=1, source_target_pairs={{1,0},{2,1},{3,2},{4,3},{5,4},{6,5},{7,6},{8,7},{9,8},{10,9},{11,1... | collective-permute-start | bytes 454664 | tf_op jit(solution)/shard_map/ppermute | solution.py:23
  40.3 1.4 %copy-start = (f32[160,2560,1]{1,0,2:T(8,128)S(1)}, f32[160,2560,1]{1,0,2:T(8,128)}, u32[]{:S(2)}) copy-start(f32[160,2560,1]{1,0,2:T(8,128)} %reshape.446) | copy-start | bytes 4915204
  49.6 51.9 %copy-start.1 = (f32[8,8192]{1,0:T(8,128)S(1)}, f32[8,8192]{1,0:T(8,128)}, u32[]{:S(2)}) copy-start(f32[8,8192]{1,0:T(8,128)} %param.4) | copy-start | bytes 786436
  69.4 3.0 %collective-permute-start.6 = (f32[128]{0:T(128)S(1)}, f32[128]{0:T(128)S(1)}, u32[]{:S(2)}, u32[]{:S(2)}) collective-permute-start(f32[128]{0:T(128)S(1)} %reduce_sum.9), channel_id=1, source_target_pairs={{0,32},{32,0},{64,96},{96,64},{128,160},{160,128},{192,224},{224,1... | collective-permute-start | bytes 1544 | tf_op jit(solution)/shard_map/ppermute | solution.py:66
  72.4 5.5 %collective-permute-start.7 = (f32[128]{0:T(128)S(1)}, f32[128]{0:T(128)S(1)}, u32[]{:S(2)}, u32[]{:S(2)}) collective-permute-start(f32[128]{0:T(128)S(1)} %add.348), channel_id=1, source_target_pairs={{0,64},{32,96},{64,0},{96,32},{128,192},{160,224},{192,128},{224,1... | collective-permute-start | bytes 1544 | tf_op jit(solution)/shard_map/ppermute | solution.py:66
  77.9 7.2 %collective-permute-start.8 = (f32[128]{0:T(128)S(1)}, f32[128]{0:T(128)S(1)}, u32[]{:S(2)}, u32[]{:S(2)}) collective-permute-start(f32[128]{0:T(128)S(1)} %add.349), channel_id=1, source_target_pairs={{0,128},{32,160},{64,192},{96,224},{128,0},{160,32},{192,64},{224,... | collective-permute-start | bytes 1544 | tf_op jit(solution)/shard_map/ppermute | solution.py:66
  85.2 9.8 %collective-permute-start.9 = (f32[128]{0:T(128)S(1)}, f32[128]{0:T(128)S(1)}, u32[]{:S(2)}, u32[]{:S(2)}) collective-permute-start(f32[128]{0:T(128)S(1)} %add.350), channel_id=1, source_target_pairs={{0,256},{32,288},{64,320},{96,352},{128,384},{160,416},{192,448},{... | collective-permute-start | bytes 1544 | tf_op jit(solution)/shard_map/ppermute | solution.py:66
  95.6 13.7 %all-to-all-start.1 = ((f32[32,1,128]{2,1,0:T(1,128)}), f32[32,1,128]{2,1,0:T(1,128)S(1)}, u32[]{:S(2)}, u32[]{:S(2)}) async-start(f32[32,1,128]{2,1,0:T(1,128)} %broadcast_in_dim.18), calls=%async_computation.1 | async-start | bytes 32768 | tf_op jit(solution)/shard_map/all_to_all | solution.py:75

commit v7 on v5

--- a/solution.py
+++ b/solution.py
@@ -76,8 +76,8 @@
         rows_x, rows_y, 5 * NZ
     )
     packed = jnp.concatenate([guess, rhs_field, coef], axis=2)
+    packed = exchange(packed, "gy", 1, depth)
     packed = exchange(packed, "gx", 0, depth)
-    packed = exchange(packed, "gy", 1, depth)
     ex, ey = packed.shape[0], packed.shape[1]
     guess_e = packed[:, :, :width]
     rhs_e = packed[1:-1, 1:-1, width : 2 * width]

time: 124 us -> 123 us (level)
  the two profiles are of different devices: /device:TPU:6 before, /device:TPU:24 now
where the time goes in v7:
time: 123 us; the launch traced here: 122 us
  waiting for transfers between devices  36.4 us (30%)
  starting transfers between devices  26 us (21%)
  blocking collectives  22.2 us (18%)
  other arithmetic  15.7 us (13%)
  local copies, waits for them, and re-layouts  10.9 us (9%)
  matrix products  9.9 us (8%)
    all_to_all x1, blocking collectives, allreduce(): parts = lax.all_to_all(x.reshape(count, -1), 'gy', 0, 0, tiled=True)  22.2 us
    ppermute x4, waiting for transfers between devices, butterfly(): x = x + lax.ppermute(x, axis, [(i, i ^ bit) for i in range(count)])  15.6 us
    ppermute x4, starting transfers between devices, butterfly(): x = x + lax.ppermute(x, axis, [(i, i ^ bit) for i in range(count)])  11.1 us
    all_to_all x1, waiting for transfers between devices, allreduce(): lax.all_to_all(jnp.broadcast_to(mine, (count,) + mine.shape), 'gy', 0, 0,...  9.67 us
    ppermute x2, waiting for transfers between devices, exchange(): high = lax.ppermute(bottom, axis, backward)  6.51 us
    ppermute x2, starting transfers between devices, exchange(): low = lax.ppermute(top, axis, forward)  6.2 us
    another operation x3, other arithmetic, per_device(): factor = jnp.linalg.cholesky(normal)  5.05 us
    ppermute x2, starting transfers between devices, exchange(): high = lax.ppermute(bottom, axis, backward)  4.94 us
  transfers between devices with their start and end apart: 9, of which 9 were waited for; matrix products, arithmetic and copies ran while one was open for 2% of the time, Pallas kernels for 0%

profile of v7, /device:TPU:24, one launch (start us, length us, event | category | flops | bytes accessed | tf_op | source)
XLA Modules:
  0.0 122.1 jit_solution(3054191816265457348)
XLA Ops:
  0.6 1.2 bitcast_dynamic-update-slice_fusion.1
  1.8 1.0 reshape.437
  3.4 4.3 %collective-permute-start = (f32[8,4,1184]{2,1,0:T(4,128)S(1)}, f32[8,4,1184]{2,1,0:T(4,128)S(1)}, u32[]{:S(2)}, u32[]{:S(2)}) collective-permute-start(f32[8,4,1184]{2,1,0:T(4,128)S(1)} %get-tuple-element.8), channel_id=1, source_target_pairs={{0,1},{1,2},{2,3},{3,4},{4,5},{5,6},{6,7},{7,8},{8,9},{9,10},{10,1... | collective-permute-start | bytes 454664 | tf_op jit(solution)/shard_map/ppermute | solution.py:23
  7.7 1.3 %collective-permute-start.1 = (f32[8,4,1184]{2,1,0:T(4,128)S(1)}, f32[8,4,1184]{2,1,0:T(4,128)S(1)}, u32[]{:S(2)}, u32[]{:S(2)}) collective-permute-start(f32[8,4,1184]{2,1,0:T(4,128)S(1)} %get-tuple-element.9), channel_id=1, source_target_pairs={{1,0},{2,1},{3,2},{4,3},{5,4},{6,5},{7,6},{8,7},{9,8},{10,9},{11,1... | collective-permute-start | bytes 454664 | tf_op jit(solution)/shard_map/ppermute | solution.py:24
  9.2 2.0 %collective-permute-done = f32[8,4,1184]{2,1,0:T(4,128)S(1)} collective-permute-done((f32[8,4,1184]{2,1,0:T(4,128)S(1)}, f32[8,4,1184]{2,1,0:T(4,128)S(1)}, u32[]{:S(2)}, u32[]{:S(2)}) %collective-permute-start) | collective-permute-done | bytes 151584 | tf_op jit(solution)/shard_map/ppermute | solution.py:23
  11.1 4.8 %collective-permute-done.1 = f32[8,4,1184]{2,1,0:T(4,128)S(1)} collective-permute-done((f32[8,4,1184]{2,1,0:T(4,128)S(1)}, f32[8,4,1184]{2,1,0:T(4,128)S(1)}, u32[]{:S(2)}, u32[]{:S(2)}) %collective-permute-start.1) | collective-permute-done | bytes 151584 | tf_op jit(solution)/shard_map/ppermute | solution.py:24
  16.0 1.0 fusion.117
  17.1 1.9 %collective-permute-start.2 = (f32[4,24,1184]{2,1,0:T(8,128)}, f32[4,24,1184]{2,1,0:T(8,128)}, u32[]{:S(2)}, u32[]{:S(2)}) collective-permute-start(f32[4,24,1184]{2,1,0:T(8,128)} %get-tuple-element.4), channel_id=1, source_target_pairs={{0,32},{32,64},{64,96},{96,128},{128,160},{160,192},{192,224},{224... | collective-permute-start | bytes 1363976 | tf_op jit(solution)/shard_map/ppermute | solution.py:23
  19.0 3.6 %collective-permute-start.3 = (f32[4,24,1184]{2,1,0:T(8,128)}, f32[4,24,1184]{2,1,0:T(8,128)}, u32[]{:S(2)}, u32[]{:S(2)}) collective-permute-start(f32[4,24,1184]{2,1,0:T(8,128)} %get-tuple-element.5), channel_id=1, source_target_pairs={{32,0},{64,32},{96,64},{128,96},{160,128},{192,160},{224,192},{256... | collective-permute-start | bytes 1363976 | tf_op jit(solution)/shard_map/ppermute | solution.py:24
  22.6 0.4 broadcast_multiply_fusion
  23.0 1.8 %reshape.446 = f32[160,2560,1]{1,0,2:T(8,128)} reshape(f32[5,32,5,512]{3,2,1,0:T(8,128)S(1)} %broadcast_multiply_fusion) | data formatting | bytes 3276800 | tf_op jit(solution)/shard_map/jit(kron)/mul | solution.py:85
  24.8 2.7 %collective-permute-done.2 = f32[4,24,1184]{2,1,0:T(8,128)} collective-permute-done((f32[4,24,1184]{2,1,0:T(8,128)}, f32[4,24,1184]{2,1,0:T(8,128)}, u32[]{:S(2)}, u32[]{:S(2)}) %collective-permute-start.2) | collective-permute-done | bytes 454688 | tf_op jit(solution)/shard_map/ppermute | solution.py:23
  27.5 1.8 %collective-permute-done.3 = f32[4,24,1184]{2,1,0:T(8,128)} collective-permute-done((f32[4,24,1184]{2,1,0:T(8,128)}, f32[4,24,1184]{2,1,0:T(8,128)}, u32[]{:S(2)}, u32[]{:S(2)}) %collective-permute-start.3) | collective-permute-done | bytes 454688 | tf_op jit(solution)/shard_map/ppermute | solution.py:24
  29.3 1.4 %pad_maximum_fusion = f32[16,24,1184]{2,1,0:T(8,128)S(1)} fusion(f32[4,24,1184]{2,1,0:T(8,128)} %collective-permute-done.3, f32[8,4,1184]{2,1,0:T(4,128)} %copy-done.2, f32[8,16,1184]{2,1,0:T(8,128)S(1)} %constant_dynamic-update-slice_fusion, f32[8,4,1184]{2,1,0:T(4,128)S(1)} %collective-permute-done, f32[4,24,1184]{2,1,0:T(8,128)} %collective-permute-done.2), kind=kLoop, calls=%fused_computation | loop fusion | flops 1818624 | bytes 3637248 | tf_op jit(solution)/shard_map/concatenate | solution.py:25
  30.7 0.3 fusion.116
  31.0 1.1 copy-done
  32.2 3.5 %fusion.22 = f32[16,24,2560]{2,1,0:T(8,128)S(1)} fusion(f32[160,2560,1]{1,0,2:T(8,128)S(1)} %copy-done, f32[16,24,1184]{2,1,0:T(8,128)S(1)} %pad_maximum_fusion), kind=kOutput, calls=%fused_computation.41 | convolution fusion | flops 1887436800 | bytes 5963776 | tf_op jit(solution)/shard_map/dot_general | solution.py:86
  35.6 1.1 fusion.3
  37.0 1.0 fusion.10
  38.4 0.8 fusion.18
  39.4 0.4 fusion.28
  40.1 1.9 %convolution_select_fusion = f32[512,512]{1,0:T(8,128)S(1)} fusion(f32[512,512]{1,0:T(8,128)S(1)} %constant_dynamic-update-slice_fusion.1, s32[512]{0:T(512)S(1)} %add_select_fusion.2), kind=kOutput, calls=%fused_computation.1 | convolution fusion | flops 1611137024 | bytes 2099200 | tf_op jit(solution)/shard_map/dot_general | solution.py:113
  41.9 0.8 fusion.34
  42.7 0.5 fusion.35
  43.3 22.2 %all_to_all.15 = f32[32,1,128]{2,1,0:T(1,128)S(1)} all-to-all(f32[32,1,128]{2,1,0:T(1,128)S(1)} %bitcast.39), channel_id=1, replica_groups=mesh['gx'=16,'gy'=32] {'gy'}, dimensions={0} | all-to-all | bytes 32768 | tf_op jit(solution)/shard_map/all_to_all | solution.py:62
  65.5 4.7 %collective-permute-start.4 = (f32[128]{0:T(128)S(1)}, f32[128]{0:T(128)S(1)}, u32[]{:S(2)}, u32[]{:S(2)}) collective-permute-start(f32[128]{0:T(128)S(1)} %reduce_sum.9), channel_id=1, source_target_pairs={{0,32},{32,0},{64,96},{96,64},{128,160},{160,128},{192,224},{224,1... | collective-permute-start | bytes 1544 | tf_op jit(solution)/shard_map/ppermute | solution.py:55
  70.2 0.8 collective-permute-done.4
  71.1 1.9 %collective-permute-start.5 = (f32[128]{0:T(128)S(1)}, f32[128]{0:T(128)S(1)}, u32[]{:S(2)}, u32[]{:S(2)}) collective-permute-start(f32[128]{0:T(128)S(1)} %add.348), channel_id=1, source_target_pairs={{0,64},{32,96},{64,0},{96,32},{128,192},{160,224},{192,128},{224,1... | collective-permute-start | bytes 1544 | tf_op jit(solution)/shard_map/ppermute | solution.py:55
  73.0 3.5 %collective-permute-done.5 = f32[128]{0:T(128)S(1)} collective-permute-done((f32[128]{0:T(128)S(1)}, f32[128]{0:T(128)S(1)}, u32[]{:S(2)}, u32[]{:S(2)}) %collective-permute-start.5) | collective-permute-done | bytes 544 | tf_op jit(solution)/shard_map/ppermute | solution.py:55
  76.5 1.9 %collective-permute-start.6 = (f32[128]{0:T(128)S(1)}, f32[128]{0:T(128)S(1)}, u32[]{:S(2)}, u32[]{:S(2)}) collective-permute-start(f32[128]{0:T(128)S(1)} %add.349), channel_id=1, source_target_pairs={{0,128},{32,160},{64,192},{96,224},{128,0},{160,32},{192,64},{224,... | collective-permute-start | bytes 1544 | tf_op jit(solution)/shard_map/ppermute | solution.py:55
  78.4 4.4 %collective-permute-done.6 = f32[128]{0:T(128)S(1)} collective-permute-done((f32[128]{0:T(128)S(1)}, f32[128]{0:T(128)S(1)}, u32[]{:S(2)}, u32[]{:S(2)}) %collective-permute-start.6) | collective-permute-done | bytes 544 | tf_op jit(solution)/shard_map/ppermute | solution.py:55
  82.9 2.5 %collective-permute-start.7 = (f32[128]{0:T(128)S(1)}, f32[128]{0:T(128)S(1)}, u32[]{:S(2)}, u32[]{:S(2)}) collective-permute-start(f32[128]{0:T(128)S(1)} %add.350), channel_id=1, source_target_pairs={{0,256},{32,288},{64,320},{96,352},{128,384},{160,416},{192,448},{... | collective-permute-start | bytes 1544 | tf_op jit(solution)/shard_map/ppermute | solution.py:55
  85.4 6.8 %collective-permute-done.7 = f32[128]{0:T(128)S(1)} collective-permute-done((f32[128]{0:T(128)S(1)}, f32[128]{0:T(128)S(1)}, u32[]{:S(2)}, u32[]{:S(2)}) %collective-permute-start.7) | collective-permute-done | bytes 544 | tf_op jit(solution)/shard_map/ppermute | solution.py:55
  92.2 0.6 broadcast_in_dim.18
  92.9 3.8 %all-to-all-start.1 = ((f32[32,1,128]{2,1,0:T(1,128)}), f32[32,1,128]{2,1,0:T(1,128)S(1)}, u32[]{:S(2)}, u32[]{:S(2)}) async-start(f32[32,1,128]{2,1,0:T(1,128)} %broadcast_in_dim.18), calls=%async_computation.1 | async-start | bytes 32768 | tf_op jit(solution)/shard_map/all_to_all | solution.py:64
  96.8 9.7 %all-to-all-done.1 = f32[32,1,128]{2,1,0:T(1,128)S(1)} async-done(((f32[32,1,128]{2,1,0:T(1,128)}), f32[32,1,128]{2,1,0:T(1,128)S(1)}, u32[]{:S(2)}, u32[]{:S(2)}) %all-to-all-start.1) | async-done | bytes 16416 | tf_op jit(solution)/shard_map/all_to_all | solution.py:64
  106.4 0.5 broadcast.565
  107.0 0.7 reduce.10
  108.3 0.3 fusion.59
  108.7 4.4 %cholesky.16 = f32[48,48]{1,0:T(8,128)S(1)} custom-call(f32[48,48]{1,0:T(8,128)S(1)} %fusion.66), custom_call_target="Cholesky" | custom-call | tf_op jit(solution)/shard_map/jit(cholesky)/cholesky | solution.py:126
  113.1 0.6 compare_reduce_fusion
  113.7 0.7 fusion.61
  114.4 3.7 %custom-call.10 = f32[1,48,48]{1,2,0:T(8,128)S(1)} custom-call(f32[1,48,48]{2,1,0:T(8,128)S(1)} %fusion.61), custom_call_target="InvertDiagBlocksLowerTriangular" | custom-call | tf_op jit(solution)/shard_map/jit(_cho_solve)/triangular_solve | solution.py:127
  118.6 0.4 fusion.32
  119.0 0.5 convolution_select_fusion.1
  119.6 1.0 fusion.122
  120.6 0.8 reshape.444
  121.4 0.8 reshape.445
  (54 shorter events, 3.3 us)
Async XLA Ops:
  0.6 2.5 %copy-start.3 = (f32[8,8192]{1,0:T(8,128)S(1)}, f32[8,8192]{1,0:T(8,128)}, u32[]{:S(2)}) copy-start(f32[8,8192]{1,0:T(8,128)} %param.3) | copy-start | bytes 786436
  3.4 7.7 %collective-permute-start = (f32[8,4,1184]{2,1,0:T(4,128)S(1)}, f32[8,4,1184]{2,1,0:T(4,128)S(1)}, u32[]{:S(2)}, u32[]{:S(2)}) collective-permute-start(f32[8,4,1184]{2,1,0:T(4,128)S(1)} %get-tuple-element.8), channel_id=1, source_target_pairs={{0,1},{1,2},{2,3},{3,4},{4,5},{5,6},{6,7},{7,8},{8,9},{9,10},{10,1... | collective-permute-start | bytes 454664 | tf_op jit(solution)/shard_map/ppermute | solution.py:23
  7.7 8.2 %collective-permute-start.1 = (f32[8,4,1184]{2,1,0:T(4,128)S(1)}, f32[8,4,1184]{2,1,0:T(4,128)S(1)}, u32[]{:S(2)}, u32[]{:S(2)}) collective-permute-start(f32[8,4,1184]{2,1,0:T(4,128)S(1)} %get-tuple-element.9), channel_id=1, source_target_pairs={{1,0},{2,1},{3,2},{4,3},{5,4},{6,5},{7,6},{8,7},{9,8},{10,9},{11,1... | collective-permute-start | bytes 454664 | tf_op jit(solution)/shard_map/ppermute | solution.py:24
  15.9 1.2 copy-start.2
  17.1 10.5 %collective-permute-start.2 = (f32[4,24,1184]{2,1,0:T(8,128)}, f32[4,24,1184]{2,1,0:T(8,128)}, u32[]{:S(2)}, u32[]{:S(2)}) collective-permute-start(f32[4,24,1184]{2,1,0:T(8,128)} %get-tuple-element.4), channel_id=1, source_target_pairs={{0,32},{32,64},{64,96},{96,128},{128,160},{160,192},{192,224},{224... | collective-permute-start | bytes 1363976 | tf_op jit(solution)/shard_map/ppermute | solution.py:23
  19.0 10.3 %collective-permute-start.3 = (f32[4,24,1184]{2,1,0:T(8,128)}, f32[4,24,1184]{2,1,0:T(8,128)}, u32[]{:S(2)}, u32[]{:S(2)}) collective-permute-start(f32[4,24,1184]{2,1,0:T(8,128)} %get-tuple-element.5), channel_id=1, source_target_pairs={{32,0},{64,32},{96,64},{128,96},{160,128},{192,160},{224,192},{256... | collective-permute-start | bytes 1363976 | tf_op jit(solution)/shard_map/ppermute | solution.py:24
  30.7 1.4 %copy-start = (f32[160,2560,1]{1,0,2:T(8,128)S(1)}, f32[160,2560,1]{1,0,2:T(8,128)}, u32[]{:S(2)}) copy-start(f32[160,2560,1]{1,0,2:T(8,128)} %reshape.446) | copy-start | bytes 4915204
  40.1 56.7 %copy-start.1 = (f32[8,8192]{1,0:T(8,128)S(1)}, f32[8,8192]{1,0:T(8,128)}, u32[]{:S(2)}) copy-start(f32[8,8192]{1,0:T(8,128)} %param.4) | copy-start | bytes 786436
  65.5 5.6 %collective-permute-start.4 = (f32[128]{0:T(128)S(1)}, f32[128]{0:T(128)S(1)}, u32[]{:S(2)}, u32[]{:S(2)}) collective-permute-start(f32[128]{0:T(128)S(1)} %reduce_sum.9), channel_id=1, source_target_pairs={{0,32},{32,0},{64,96},{96,64},{128,160},{160,128},{192,224},{224,1... | collective-permute-start | bytes 1544 | tf_op jit(solution)/shard_map/ppermute | solution.py:55
  71.1 5.5 %collective-permute-start.5 = (f32[128]{0:T(128)S(1)}, f32[128]{0:T(128)S(1)}, u32[]{:S(2)}, u32[]{:S(2)}) collective-permute-start(f32[128]{0:T(128)S(1)} %add.348), channel_id=1, source_target_pairs={{0,64},{32,96},{64,0},{96,32},{128,192},{160,224},{192,128},{224,1... | collective-permute-start | bytes 1544 | tf_op jit(solution)/shard_map/ppermute | solution.py:55
  76.5 6.3 %collective-permute-start.6 = (f32[128]{0:T(128)S(1)}, f32[128]{0:T(128)S(1)}, u32[]{:S(2)}, u32[]{:S(2)}) collective-permute-start(f32[128]{0:T(128)S(1)} %add.349), channel_id=1, source_target_pairs={{0,128},{32,160},{64,192},{96,224},{128,0},{160,32},{192,64},{224,... | collective-permute-start | bytes 1544 | tf_op jit(solution)/shard_map/ppermute | solution.py:55
  82.9 9.4 %collective-permute-start.7 = (f32[128]{0:T(128)S(1)}, f32[128]{0:T(128)S(1)}, u32[]{:S(2)}, u32[]{:S(2)}) collective-permute-start(f32[128]{0:T(128)S(1)} %add.350), channel_id=1, source_target_pairs={{0,256},{32,288},{64,320},{96,352},{128,384},{160,416},{192,448},{... | collective-permute-start | bytes 1544 | tf_op jit(solution)/shard_map/ppermute | solution.py:55
  92.9 13.6 %all-to-all-start.1 = ((f32[32,1,128]{2,1,0:T(1,128)}), f32[32,1,128]{2,1,0:T(1,128)S(1)}, u32[]{:S(2)}, u32[]{:S(2)}) async-start(f32[32,1,128]{2,1,0:T(1,128)} %broadcast_in_dim.18), calls=%async_computation.1 | async-start | bytes 32768 | tf_op jit(solution)/shard_map/all_to_all | solution.py:64
